TPU v7x, 128 devices: a whole 4x4x4 slice. The times are simulated.
128 devices in a mesh: nodes: 128 (over x, z, y, core).
Axes of the slice: x: 4, y: 4, z: 4, core: 2. Of those that a mesh axis runs over, the one named last changes fastest.
Arguments:
- features: bfloat16 [1048576, 256], P('nodes'), may hold values from -6 to 6
- cluster_ids: int32 [1048576], P('nodes'), may hold values from 0 to 65535, as said below
- tile_cols: int32 [512, 6], P('nodes'), may hold values from 0 to 511, as said below
- tile_counts: int32 [512], P('nodes'), may hold values from 1 to 6
- adjacency: bfloat16 [512, 6, 128, 128], P('nodes'), may hold values from -0.5 to 0.5
- w_first: bfloat16 [256, 256], replicated, may hold values from -0.375 to 0.375
- w_second: bfloat16 [256, 256], replicated, may hold values from -0.375 to 0.375
Outputs:
- unpooled: bfloat16 [1048576, 256], P('nodes')
Inputs may be any that keep to these rules, and one draw needn't show every extreme that they name: `cluster_ids`: cluster c is held by device c // 512. Exactly 1024 fine nodes of each device name clusters of other devices; at most 16 of them name clusters of any one other device, among at most 4 distinct clusters of it. `tile_cols`: tile s holds clusters s * 128 to s * 128 + 127; the column tiles named for a tile row of device p are tiles of devices p - 1, p and p + 1.
All inputs are finite; a program needn't handle non-finite values.
Results may differ from a plain program's by a relative error of at most 0.0051.
Values may be sent and summed in bfloat16 or wider, within the bound.
No kernel may reach another device: no remote copies, remote signals or barrier semaphores. Data moves between devices by JAX's collectives and lax.ppermute only.
A program may use at most 64 MiB of HBM per device.

v0:
```python
import jax
import jax.numpy as jnp
from jax import lax
from jax.sharding import PartitionSpec as P

CL_DEV = 512
CAP = 16


def with_halo(block, sides, width):
    for axis, dim in sides:
        count = lax.axis_size(axis)
        forward = [(i, i + 1) for i in range(count - 1)]
        backward = [(target, source) for source, target in forward]
        low = lax.ppermute(
            lax.slice_in_dim(block, block.shape[dim] - width, None, axis=dim), axis, forward
        )
        high = lax.ppermute(lax.slice_in_dim(block, 0, width, axis=dim), axis, backward)
        block = jnp.concatenate([low, block, high], axis=dim)
    return block


def convolve(values, tile_cols, tile_counts, adjacency, myself):
    window = with_halo(values, (("nodes", 0),), values.shape[0])
    tile_size = adjacency.shape[2]
    per_device = tile_cols.shape[0]
    window_tiles = window.reshape(-1, tile_size, window.shape[1])
    offsets = tile_cols - (myself - 1) * per_device
    picked = window_tiles[offsets]
    live = jnp.arange(tile_cols.shape[1], dtype=jnp.int32)[None, :] < tile_counts[:, None]
    weights = jnp.where(live[:, :, None, None], adjacency, jnp.zeros((), adjacency.dtype))
    result = jnp.einsum("tkij,tkjf->tif", weights, picked, preferred_element_type=jnp.float32)
    return result.reshape(values.shape[0], values.shape[1])


def ranks_within(hot_table, lower_tri):
    running = jnp.dot(lower_tri, hot_table.astype(jnp.bfloat16), preferred_element_type=jnp.float32)
    return (jnp.sum(running * hot_table.astype(jnp.float32), axis=1) - 1.0).astype(jnp.int32)


def local(features, cluster_ids, tile_cols, tile_counts, adjacency, w_first, w_second):
    device_count = lax.axis_size("nodes")
    myself = lax.axis_index("nodes")
    fine_rows, width = features.shape
    clusters_here = CL_DEV
    local_ids = cluster_ids - myself * clusters_here
    owners = cluster_ids // clusters_here
    remote = owners != myself
    columns = jnp.arange(clusters_here, dtype=jnp.int32)
    block_rows = min(fine_rows, 2048)
    block_count = fine_rows // block_rows
    feature_blocks = features.reshape(block_count, block_rows, width)
    id_blocks = local_ids.reshape(block_count, block_rows)
    contract_rows = (((0,), (0,)), ((), ()))

    def pool_block(running, pieces):
        sums_acc, counts_acc = running
        rows_x, ids_x = pieces
        one_hot = ids_x[:, None] == columns[None, :]
        sums_acc = sums_acc + lax.dot_general(
            one_hot.astype(jnp.bfloat16), rows_x, contract_rows, preferred_element_type=jnp.float32
        )
        counts_acc = counts_acc + jnp.sum(one_hot.astype(jnp.float32), axis=0)
        return ((sums_acc, counts_acc), None)

    start = (
        jnp.zeros((clusters_here, width), jnp.float32),
        jnp.zeros((clusters_here,), jnp.float32),
    )
    (sums_all, counts_all), _ = lax.scan(pool_block, start, (feature_blocks, id_blocks))
    bound_count = device_count * CAP // 2
    chosen = jnp.nonzero(remote, size=bound_count, fill_value=0)[0].astype(jnp.int32)
    bound_rows = features[chosen]
    bound_global = cluster_ids[chosen]
    bound_owner = owners[chosen]
    bound_local = bound_global - bound_owner * clusters_here
    peers = jnp.arange(device_count, dtype=jnp.int32)
    owner_hot = (bound_owner[:, None] == peers[None, :]).astype(jnp.int32)
    bound_index = jnp.arange(bound_count, dtype=jnp.int32)
    lower_tri = (bound_index[:, None] >= bound_index[None, :]).astype(jnp.bfloat16)
    rank_in = ranks_within(owner_hot, lower_tri)
    slots = bound_owner * CAP + rank_in
    slot_range = jnp.arange(device_count * CAP, dtype=jnp.int32)
    slot_hot = slots[:, None] == slot_range[None, :]
    send_rows = lax.dot_general(
        slot_hot.astype(jnp.bfloat16), bound_rows, contract_rows, preferred_element_type=jnp.float32
    ).astype(jnp.bfloat16)
    send_ids = jnp.max(jnp.where(slot_hot, bound_local[:, None], -1), axis=0)
    got_rows, got_ids = (
        lax.all_to_all(
            send_rows.reshape(device_count, CAP, width),
            "nodes",
            split_axis=0,
            concat_axis=0,
            tiled=True,
        ),
        lax.all_to_all(
            send_ids.reshape(device_count, CAP), "nodes", split_axis=0, concat_axis=0, tiled=True
        ),
    )
    flat_ids = got_ids.reshape(-1)
    one_hot = flat_ids[:, None] == columns[None, :]
    sums_all = sums_all + lax.dot_general(
        one_hot.astype(jnp.bfloat16),
        got_rows.reshape(-1, width),
        contract_rows,
        preferred_element_type=jnp.float32,
    )
    counts_all = counts_all + jnp.sum(one_hot.astype(jnp.float32), axis=0)
    pooled = (sums_all / jnp.sqrt(counts_all + 1.0)[:, None]).astype(jnp.bfloat16)
    first_proj = jnp.dot(pooled, w_first, preferred_element_type=jnp.float32).astype(jnp.bfloat16)
    hidden = jnp.maximum(
        convolve(first_proj, tile_cols, tile_counts, adjacency, myself), 0.0
    ).astype(jnp.bfloat16)
    second_proj = jnp.dot(hidden, w_second, preferred_element_type=jnp.float32).astype(jnp.bfloat16)
    coarse = convolve(second_proj, tile_cols, tile_counts, adjacency, myself).astype(jnp.bfloat16)
    answer_hot = (flat_ids[:, None] == columns[None, :]).astype(jnp.bfloat16)
    answers = jnp.dot(answer_hot, coarse, preferred_element_type=jnp.float32).astype(jnp.bfloat16)
    returned = lax.all_to_all(
        answers.reshape(device_count, CAP, width), "nodes", split_axis=0, concat_axis=0, tiled=True
    )
    remote_part = jnp.dot(
        slot_hot.astype(jnp.bfloat16),
        returned.reshape(-1, width),
        preferred_element_type=jnp.float32,
    ).astype(jnp.bfloat16)
    block_starts = jnp.arange(block_count, dtype=jnp.int32) * block_rows
    row_range = jnp.arange(block_rows, dtype=jnp.int32)

    def unpool_block(unused, pieces):
        rows_x, ids_x, first_row = pieces
        one_hot = (ids_x[:, None] == columns[None, :]).astype(jnp.bfloat16)
        hit = ((first_row + row_range)[:, None] == chosen[None, :]).astype(jnp.bfloat16)
        value = (
            rows_x.astype(jnp.float32)
            + jnp.dot(one_hot, coarse, preferred_element_type=jnp.float32)
            + jnp.dot(hit, remote_part, preferred_element_type=jnp.float32)
        )
        return (unused, value.astype(jnp.bfloat16))

    _, result = lax.scan(
        unpool_block, jnp.zeros((), jnp.int32), (feature_blocks, id_blocks, block_starts)
    )
    return result.reshape(fine_rows, width)


def solution(mesh):
    placed = (
        P("nodes", None),
        P("nodes"),
        P("nodes", None),
        P("nodes"),
        P("nodes", None, None, None),
        P(),
        P(),
    )
    return jax.shard_map(
        local, mesh=mesh, in_specs=placed, out_specs=P("nodes", None), check_vma=False
    )
```

profile of v0, /device:TPU:1, one launch (start us, length us, event | category | flops | bytes accessed | tf_op | source)
XLA Modules:
  0.0 213.7 jit_solution(1417069590788236649)
XLA Ops:
  2.2 57.0 %scatter_custom_fusion = s32[1024]{0:T(1024)S(1)} fusion(s32[8192]{0:T(1024)S(1)} %bitcast.88, s32[8192]{0:T(1024)S(1)} %ne.56, s32[]{:T(128)} %copy.29), kind=kCustom, calls=%fused_computation.107 | custom fusion | flops 8192 | bytes 4100 | tf_op jit(solution)/shard_map/scatter-add | solution.py:72
  61.2 6.2 %gather_fusion.1 = s32[1024]{0:T(1024)S(1)} fusion(s32[8192]{0:T(1024)S(1)} %copy-done.1, s32[1024]{0:T(1024)S(1)} %broadcast_clamp_fusion), kind=kCustom, calls=%fused_computation.1 | custom fusion | bytes 12288 | tf_op jit(solution)/shard_map/gather | solution.py:74
  67.3 6.2 %gather_fusion = s32[1024]{0:T(1024)S(1)} fusion(s32[8192]{0:T(1024)S(1)} %get-tuple-element.162, s32[1024]{0:T(1024)S(1)} %broadcast_clamp_fusion), kind=kCustom, calls=%fused_computation | custom fusion | bytes 12288 | tf_op jit(solution)/shard_map/gather | solution.py:75
  76.5 11.5 %all-to-all-start = ((s32[128,1,16]{2,1,0:T(1,128)}), s32[128,1,16]{2,1,0:T(1,128)S(1)}, u32[]{:S(2)}, u32[]{:S(2)}) async-start(s32[128,1,16]{2,1,0:T(1,128)} %bitcast.7), calls=%async_computation | async-start | bytes 131072 | tf_op jit(solution)/shard_map/all_to_all | solution.py:97
  88.0 6.2 %gather_fusion.2 = bf16[1024,256]{1,0:T(8,128)(2,1)S(1)} fusion(bf16[8192,256]{1,0:T(8,128)(2,1)} %param.11, s32[1024]{0:T(1024)S(1)} %broadcast_clamp_fusion), kind=kCustom, calls=%fused_computation.2 | custom fusion | bytes 1052672 | tf_op jit(solution)/shard_map/gather | solution.py:73
  94.2 3.5 %fusion.33 = bf16[2048,256]{1,0:T(8,128)(2,1)} fusion(bf16[1024,256]{1,0:T(8,128)(2,1)S(1)} %gather_fusion.2, s32[1024]{0:T(1024)S(1)} %get-tuple-element.165), kind=kOutput, calls=%fused_computation.47 | convolution fusion | flops 1076363264 | bytes 1576960 | tf_op jit(solution)/shard_map/dot_general | solution.py:85
  97.7 9.8 %all-to-all-start.1 = ((bf16[128,16,256]{2,1,0:T(8,128)(2,1)}), bf16[128,16,256]{2,1,0:T(8,128)(2,1)S(1)}, u32[]{:S(2)}, u32[]{:S(2)}) async-start(bf16[128,16,256]{2,1,0:T(8,128)(2,1)} %bitcast.8), calls=%async_computation.1 | async-start | bytes 2097152 | tf_op jit(solution)/shard_map/all_to_all | solution.py:90
  107.5 14.3 %while.25 = (s32[]{:T(128)}, f32[512,256]{1,0:T(8,128)S(1)}, f32[512]{0:T(512)S(1)}, s32[4,2048]{1,0:T(4,128)S(1)}, bf16[4,2048,256]{2,1,0:T(8,128)(2,1)}, /*index=5*/s32[]{:T(128)}, s32[]{:T(128)}) while((s32[]{:T(128)}, f32[512,256]{1,0:T(8,128)S(1)}, f32[512]{0:T(512)S(1)}, s32[4,2048]{1,0:T(4,128)S(1)}, ...), condition=%wide.region_8.9_spmd.clone, body=%wide.region_6.8_spmd.clone.sunk | while | flops 541327872 | bytes 2138716 | solution.py:70
  107.5 2.9 %fusion.83 = f32[512,256]{1,0:T(8,128)S(1)} fusion(s32[2048]{0:T(1024)S(1)} %bitcast.84, bf16[4,2048,256]{2,1,0:T(8,128)(2,1)} %get-tuple-element.264, s32[]{:T(128)} %get-tuple-element.253, f32[512,256]{1,0:T(8,128)S(1)} %get-tuple-element.254, pred[]{:T(512)S(6)} %compare.15), kind=kOutput, calls=%fused_computation.28.clone.1 | convolution fusion | flops 538181632 | bytes 2105857 | tf_op jit(solution)/shard_map/while/body/eval_jaxpr/dot_general | solution.py:60
  111.1 2.9 %fusion.83 = f32[512,256]{1,0:T(8,128)S(1)} fusion(s32[2048]{0:T(1024)S(1)} %bitcast.84, bf16[4,2048,256]{2,1,0:T(8,128)(2,1)} %get-tuple-element.264, s32[]{:T(128)} %get-tuple-element.253, f32[512,256]{1,0:T(8,128)S(1)} %get-tuple-element.254, pred[]{:T(512)S(6)} %compare.15), kind=kOutput, calls=%fused_computation.28.clone.1 | convolution fusion | flops 538181632 | bytes 2105857 | tf_op jit(solution)/shard_map/while/body/eval_jaxpr/dot_general | solution.py:60
  114.6 2.9 %fusion.83 = f32[512,256]{1,0:T(8,128)S(1)} fusion(s32[2048]{0:T(1024)S(1)} %bitcast.84, bf16[4,2048,256]{2,1,0:T(8,128)(2,1)} %get-tuple-element.264, s32[]{:T(128)} %get-tuple-element.253, f32[512,256]{1,0:T(8,128)S(1)} %get-tuple-element.254, pred[]{:T(512)S(6)} %compare.15), kind=kOutput, calls=%fused_computation.28.clone.1 | convolution fusion | flops 538181632 | bytes 2105857 | tf_op jit(solution)/shard_map/while/body/eval_jaxpr/dot_general | solution.py:60
  118.2 2.9 %fusion.83 = f32[512,256]{1,0:T(8,128)S(1)} fusion(s32[2048]{0:T(1024)S(1)} %bitcast.84, bf16[4,2048,256]{2,1,0:T(8,128)(2,1)} %get-tuple-element.264, s32[]{:T(128)} %get-tuple-element.253, f32[512,256]{1,0:T(8,128)S(1)} %get-tuple-element.254, pred[]{:T(512)S(6)} %compare.15), kind=kOutput, calls=%fused_computation.28.clone.1 | convolution fusion | flops 538181632 | bytes 2105857 | tf_op jit(solution)/shard_map/while/body/eval_jaxpr/dot_general | solution.py:60
  124.0 2.5 %all-to-all-done.1 = bf16[128,16,256]{2,1,0:T(8,128)(2,1)S(1)} async-done(((bf16[128,16,256]{2,1,0:T(8,128)(2,1)}), bf16[128,16,256]{2,1,0:T(8,128)(2,1)S(1)}, u32[]{:S(2)}, u32[]{:S(2)}) %all-to-all-start.1) | async-done | bytes 1048608 | tf_op jit(solution)/shard_map/all_to_all | solution.py:90
  128.2 3.1 %collective-permute-start = (bf16[512,256]{1,0:T(8,128)(2,1)S(1)}, bf16[512,256]{1,0:T(8,128)(2,1)S(1)}, u32[]{:S(2)}, u32[]{:S(2)}) collective-permute-start(bf16[512,256]{1,0:T(8,128)(2,1)S(1)} %convolution_convert_fusion.1), channel_id=1, source_target_pairs={{0,1},{1,2},{2,3},{3,4},{4,5},{5,6},{6,7},{7,8},{8,9},{9,10},{10,1... | collective-permute-start | bytes 786440 | tf_op jit(solution)/shard_map/ppermute | solution.py:15
  134.6 4.4 %collective-permute-done.1 = bf16[512,256]{1,0:T(8,128)(2,1)S(1)} collective-permute-done((bf16[512,256]{1,0:T(8,128)(2,1)S(1)}, bf16[512,256]{1,0:T(8,128)(2,1)S(1)}, u32[]{:S(2)}, u32[]{:S(2)}) %collective-permute-start.1) | collective-permute-done | bytes 262176 | tf_op jit(solution)/shard_map/ppermute | solution.py:18
  142.8 2.4 %collective-permute-start.3 = (bf16[512,256]{1,0:T(8,128)(2,1)S(1)}, bf16[512,256]{1,0:T(8,128)(2,1)S(1)}, u32[]{:S(2)}, u32[]{:S(2)}) collective-permute-start(bf16[512,256]{1,0:T(8,128)(2,1)S(1)} %convolution_convert_fusion), channel_id=1, source_target_pairs={{1,0},{2,1},{3,2},{4,3},{5,4},{6,5},{7,6},{8,7},{9,8},{10,9},{11,1... | collective-permute-start | bytes 786440 | tf_op jit(solution)/shard_map/ppermute | solution.py:18
  146.1 4.4 %collective-permute-done.3 = bf16[512,256]{1,0:T(8,128)(2,1)S(1)} collective-permute-done((bf16[512,256]{1,0:T(8,128)(2,1)S(1)}, bf16[512,256]{1,0:T(8,128)(2,1)S(1)}, u32[]{:S(2)}, u32[]{:S(2)}) %collective-permute-start.3) | collective-permute-done | bytes 262176 | tf_op jit(solution)/shard_map/ppermute | solution.py:18
  153.5 15.9 %all-to-all-start.2 = ((bf16[128,16,256]{2,1,0:T(8,128)(2,1)}), bf16[128,16,256]{2,1,0:T(8,128)(2,1)S(1)}, u32[]{:S(2)}, u32[]{:S(2)}) async-start(bf16[128,16,256]{2,1,0:T(8,128)(2,1)} %bitcast.21), calls=%async_computation.2 | async-start | bytes 2097152 | tf_op jit(solution)/shard_map/all_to_all | solution.py:119
  169.4 19.0 %all-to-all-done.2 = bf16[128,16,256]{2,1,0:T(8,128)(2,1)S(1)} async-done(((bf16[128,16,256]{2,1,0:T(8,128)(2,1)}), bf16[128,16,256]{2,1,0:T(8,128)(2,1)S(1)}, u32[]{:S(2)}, u32[]{:S(2)}) %all-to-all-start.2) | async-done | bytes 1048608 | tf_op jit(solution)/shard_map/all_to_all | solution.py:119
  189.9 23.7 %while.24 = (s32[]{:T(128)}, bf16[4,2048,256]{2,1,0:T(8,128)(2,1)}, bf16[4,2048,256]{2,1,0:T(8,128)(2,1)}, s32[4,2048]{1,0:T(4,128)S(1)}, bf16[512,256]{1,0:T(8,...) while((s32[]{:T(128)}, bf16[4,2048,256]{2,1,0:T(8,128)(2,1)}, ...), condition=%wide.region_13.14_spmd.clone, body=%wide.region_12.13_spmd.clone.sunk | while | flops 1615857664 | bytes 7123569 | solution.py:141
  192.8 3.1 %fusion.81 = bf16[4,2048,256]{2,1,0:T(8,128)(2,1)} fusion(bf16[4,2048,256]{2,1,0:T(8,128)(2,1)} %get-tuple-element.277, s32[]{:T(128)} %get-tuple-element.276, f32[2048,256]{1,0:T(8,128)S(1)} %fusion.80, bf16[512,256]{1,0:T(8,128)(2,1)S(1)} %get-tuple-element.289, s32[2048]{0:T(1024)S(1)} %bitcast.86, bf16[4,2048,256]{2,1,0:T(8,128)(2,1)} %get-tuple-element.287), kind=kOutput, calls=%fused_computation.19.clone.1 | convolution fusion | flops 540016640 | bytes 4465152 | tf_op jit(solution)/shard_map/while/body/eval_jaxpr/dot_general | solution.py:136
  198.7 3.1 %fusion.81 = bf16[4,2048,256]{2,1,0:T(8,128)(2,1)} fusion(bf16[4,2048,256]{2,1,0:T(8,128)(2,1)} %get-tuple-element.277, s32[]{:T(128)} %get-tuple-element.276, f32[2048,256]{1,0:T(8,128)S(1)} %fusion.80, bf16[512,256]{1,0:T(8,128)(2,1)S(1)} %get-tuple-element.289, s32[2048]{0:T(1024)S(1)} %bitcast.86, bf16[4,2048,256]{2,1,0:T(8,128)(2,1)} %get-tuple-element.287), kind=kOutput, calls=%fused_computation.19.clone.1 | convolution fusion | flops 540016640 | bytes 4465152 | tf_op jit(solution)/shard_map/while/body/eval_jaxpr/dot_general | solution.py:136
  204.6 3.1 %fusion.81 = bf16[4,2048,256]{2,1,0:T(8,128)(2,1)} fusion(bf16[4,2048,256]{2,1,0:T(8,128)(2,1)} %get-tuple-element.277, s32[]{:T(128)} %get-tuple-element.276, f32[2048,256]{1,0:T(8,128)S(1)} %fusion.80, bf16[512,256]{1,0:T(8,128)(2,1)S(1)} %get-tuple-element.289, s32[2048]{0:T(1024)S(1)} %bitcast.86, bf16[4,2048,256]{2,1,0:T(8,128)(2,1)} %get-tuple-element.287), kind=kOutput, calls=%fused_computation.19.clone.1 | convolution fusion | flops 540016640 | bytes 4465152 | tf_op jit(solution)/shard_map/while/body/eval_jaxpr/dot_general | solution.py:136
  210.6 3.1 %fusion.81 = bf16[4,2048,256]{2,1,0:T(8,128)(2,1)} fusion(bf16[4,2048,256]{2,1,0:T(8,128)(2,1)} %get-tuple-element.277, s32[]{:T(128)} %get-tuple-element.276, f32[2048,256]{1,0:T(8,128)S(1)} %fusion.80, bf16[512,256]{1,0:T(8,128)(2,1)S(1)} %get-tuple-element.289, s32[2048]{0:T(1024)S(1)} %bitcast.86, bf16[4,2048,256]{2,1,0:T(8,128)(2,1)} %get-tuple-element.287), kind=kOutput, calls=%fused_computation.19.clone.1 | convolution fusion | flops 540016640 | bytes 4465152 | tf_op jit(solution)/shard_map/while/body/eval_jaxpr/dot_general | solution.py:136
  (93 shorter events, 37.0 us)
Async XLA Ops:
  0.0 126.5 %copy-start = (bf16[256,256]{1,0:T(8,128)(2,1)S(1)}, bf16[256,256]{1,0:T(8,128)(2,1)}, u32[]{:S(2)}) copy-start(bf16[256,256]{1,0:T(8,128)(2,1)} %param.16) | copy-start | bytes 393220
  0.0 61.1 %copy-start.1 = (s32[8192]{0:T(1024)S(1)}, s32[8192]{0:T(1024)}, u32[]{:S(2)}) copy-start(s32[8192]{0:T(1024)} %param.12) | copy-start | bytes 98308
  76.5 21.2 %all-to-all-start = ((s32[128,1,16]{2,1,0:T(1,128)}), s32[128,1,16]{2,1,0:T(1,128)S(1)}, u32[]{:S(2)}, u32[]{:S(2)}) async-start(s32[128,1,16]{2,1,0:T(1,128)} %bitcast.7), calls=%async_computation | async-start | bytes 131072 | tf_op jit(solution)/shard_map/all_to_all | solution.py:97
  97.7 28.8 %all-to-all-start.1 = ((bf16[128,16,256]{2,1,0:T(8,128)(2,1)}), bf16[128,16,256]{2,1,0:T(8,128)(2,1)S(1)}, u32[]{:S(2)}, u32[]{:S(2)}) async-start(bf16[128,16,256]{2,1,0:T(8,128)(2,1)} %bitcast.8), calls=%async_computation.1 | async-start | bytes 2097152 | tf_op jit(solution)/shard_map/all_to_all | solution.py:90
  107.4 14.3 %copy-start.3 = (s32[4,6]{1,0:T(4,128)S(1)}, s32[4,6]{1,0:T(4,128)}, u32[]{:S(2)}) copy-start(s32[4,6]{1,0:T(4,128)} %param.13) | copy-start | bytes 292
  126.5 6.8 %copy-start.5 = (s32[4]{0:T(128)S(1)}, s32[4]{0:T(128)}, u32[]{:S(2)}) copy-start(s32[4]{0:T(128)} %param.14) | copy-start | bytes 52
  128.2 6.4 %collective-permute-start = (bf16[512,256]{1,0:T(8,128)(2,1)S(1)}, bf16[512,256]{1,0:T(8,128)(2,1)S(1)}, u32[]{:S(2)}, u32[]{:S(2)}) collective-permute-start(bf16[512,256]{1,0:T(8,128)(2,1)S(1)} %convolution_convert_fusion.1), channel_id=1, source_target_pairs={{0,1},{1,2},{2,3},{3,4},{4,5},{5,6},{6,7},{7,8},{8,9},{9,10},{10,1... | collective-permute-start | bytes 786440 | tf_op jit(solution)/shard_map/ppermute | solution.py:15
  131.3 7.7 %collective-permute-start.1 = (bf16[512,256]{1,0:T(8,128)(2,1)S(1)}, bf16[512,256]{1,0:T(8,128)(2,1)S(1)}, u32[]{:S(2)}, u32[]{:S(2)}) collective-permute-start(bf16[512,256]{1,0:T(8,128)(2,1)S(1)} %convolution_convert_fusion.1), channel_id=1, source_target_pairs={{1,0},{2,1},{3,2},{4,3},{5,4},{6,5},{7,6},{8,7},{9,8},{10,9},{11,1... | collective-permute-start | bytes 786440 | tf_op jit(solution)/shard_map/ppermute | solution.py:18
  133.3 6.4 %copy-start.4 = (bf16[4,6,128,128]{3,2,1,0:T(8,128)(2,1)S(1)}, bf16[4,6,128,128]{3,2,1,0:T(8,128)(2,1)}, u32[]{:S(2)}) copy-start(bf16[4,6,128,128]{3,2,1,0:T(8,128)(2,1)} %param.15) | copy-start | bytes 2359300
  139.7 0.9 copy-start.2
  140.9 5.2 %collective-permute-start.2 = (bf16[512,256]{1,0:T(8,128)(2,1)S(1)}, bf16[512,256]{1,0:T(8,128)(2,1)S(1)}, u32[]{:S(2)}, u32[]{:S(2)}) collective-permute-start(bf16[512,256]{1,0:T(8,128)(2,1)S(1)} %convolution_convert_fusion), channel_id=1, source_target_pairs={{0,1},{1,2},{2,3},{3,4},{4,5},{5,6},{6,7},{7,8},{8,9},{9,10},{10,1... | collective-permute-start | bytes 786440 | tf_op jit(solution)/shard_map/ppermute | solution.py:15
  142.8 7.7 %collective-permute-start.3 = (bf16[512,256]{1,0:T(8,128)(2,1)S(1)}, bf16[512,256]{1,0:T(8,128)(2,1)S(1)}, u32[]{:S(2)}, u32[]{:S(2)}) collective-permute-start(bf16[512,256]{1,0:T(8,128)(2,1)S(1)} %convolution_convert_fusion), channel_id=1, source_target_pairs={{1,0},{2,1},{3,2},{4,3},{5,4},{6,5},{7,6},{8,7},{9,8},{10,9},{11,1... | collective-permute-start | bytes 786440 | tf_op jit(solution)/shard_map/ppermute | solution.py:18
  151.6 1.9 copy-start.6
  153.5 34.9 %all-to-all-start.2 = ((bf16[128,16,256]{2,1,0:T(8,128)(2,1)}), bf16[128,16,256]{2,1,0:T(8,128)(2,1)S(1)}, u32[]{:S(2)}, u32[]{:S(2)}) async-start(bf16[128,16,256]{2,1,0:T(8,128)(2,1)} %bitcast.21), calls=%async_computation.2 | async-start | bytes 2097152 | tf_op jit(solution)/shard_map/all_to_all | solution.py:119
  188.4 1.5 copy-start.7
where the time goes:
time: 214 us
  other arithmetic  69.1 us (32%)
  starting transfers between devices  46.5 us (22%)
  matrix products  40.2 us (19%)
  waiting for transfers between devices  32.4 us (15%)
  local copies, waits for them, and re-layouts  24.9 us (12%)
    scatter-add x1, other arithmetic, local(): jnp.nonzero(remote, size=bound_count, fill_value=0)[0].astype(jnp.int32)  57 us
    all_to_all x1, waiting for transfers between devices, local(): lax.all_to_all(answers.reshape(device_count, CAP, width), 'nodes', split_...  19 us
    all_to_all x1, starting transfers between devices, local(): lax.all_to_all(answers.reshape(device_count, CAP, width), 'nodes', split_...  15.9 us
    dot_general x4, matrix products, unpool_block(): jnp.dot(one_hot, coarse, preferred_element_type=jnp.float32)  12.4 us
    dot_general x4, matrix products, pool_block(): lax.dot_general(one_hot.astype(jnp.bfloat16), rows_x, contract_rows, pref...  11.7 us
    all_to_all x1, starting transfers between devices, local(): lax.all_to_all(send_ids.reshape(device_count, CAP), 'nodes', split_axis=0...  11.5 us
    all_to_all x1, starting transfers between devices, local(): lax.all_to_all(send_rows.reshape(device_count, CAP, width), 'nodes', spli...  9.77 us
    ppermute x2, waiting for transfers between devices, with_halo(): lax.ppermute(lax.slice_in_dim(block, 0, width, axis=dim), axis, backward)  8.79 us
  transfers between devices with their start and end apart: 7, of which 6 were waited for; matrix products, arithmetic and copies ran while one was open for 12% of the time, Pallas kernels for 0%

commit v1 on v0

v1 whole, which is shorter than its diff:
```python
import jax
import jax.numpy as jnp
from jax import lax
from jax.sharding import PartitionSpec as P

DCAP = 4


def with_halo(block, sides, width):
    for axis, dim in sides:
        count = lax.axis_size(axis)
        forward = [(i, i + 1) for i in range(count - 1)]
        backward = [(target, source) for source, target in forward]
        low = lax.ppermute(
            lax.slice_in_dim(block, block.shape[dim] - width, None, axis=dim), axis, forward
        )
        high = lax.ppermute(lax.slice_in_dim(block, 0, width, axis=dim), axis, backward)
        block = jnp.concatenate([low, block, high], axis=dim)
    return block


def convolve(values, tile_cols, tile_counts, adjacency, myself):
    window = with_halo(values, (("nodes", 0),), values.shape[0])
    tile_size = adjacency.shape[2]
    per_device = tile_cols.shape[0]
    window_tiles = window.reshape(-1, tile_size, window.shape[1])
    offsets = tile_cols - (myself - 1) * per_device
    picked = window_tiles[offsets]
    live = jnp.arange(tile_cols.shape[1], dtype=jnp.int32)[None, :] < tile_counts[:, None]
    weights = jnp.where(live[:, :, None, None], adjacency, jnp.zeros((), adjacency.dtype))
    result = jnp.einsum("tkij,tkjf->tif", weights, picked, preferred_element_type=jnp.float32)
    return result.reshape(values.shape[0], values.shape[1])


def distinct_slots(cluster_ids, owners, remote, device_count):
    peers = jnp.arange(device_count, dtype=jnp.int32)
    big = jnp.int32(2**30)
    owner_hot = (owners[:, None] == peers[None, :]) & remote[:, None]
    grid = jnp.where(owner_hot, cluster_ids[:, None], big)
    lows = []
    for _ in range(DCAP):
        low = jnp.min(grid, axis=0)
        lows.append(low)
        grid = jnp.where(grid > low[None, :], grid, big)
    rank = jnp.zeros(grid.shape, jnp.int32)
    for low in lows[1:]:
        rank = rank + (cluster_ids[:, None] >= low[None, :]).astype(jnp.int32)
    slot = jnp.sum(jnp.where(owner_hot, rank, 0), axis=1)
    return slot, jnp.stack(lows, axis=1)


def local(features, cluster_ids, tile_cols, tile_counts, adjacency, w_first, w_second):
    device_count = lax.axis_size("nodes")
    myself = lax.axis_index("nodes")
    fine_rows, width = features.shape
    clusters_here = adjacency.shape[0] * adjacency.shape[2]
    owners = cluster_ids // clusters_here
    remote = owners != myself
    slot, lows = distinct_slots(cluster_ids, owners, remote, device_count)
    remote_slots = device_count * DCAP
    column = jnp.where(
        remote, clusters_here + owners * DCAP + slot, cluster_ids - myself * clusters_here
    )
    columns = jnp.arange(clusters_here + remote_slots, dtype=jnp.int32)
    one_hot = (column[:, None] == columns[None, :]).astype(jnp.bfloat16)
    contract_rows = (((0,), (0,)), ((), ()))
    sums_ext = lax.dot_general(
        one_hot, features, contract_rows, preferred_element_type=jnp.float32
    )
    counts_ext = jnp.sum(one_hot.astype(jnp.float32), axis=0)

    dest_ids = jnp.where(lows < 2**30, lows - jnp.arange(device_count)[:, None] * clusters_here, -1)
    meta = jnp.zeros((remote_slots, 128), jnp.float32)
    meta = meta.at[:, 0].set(counts_ext[clusters_here:])
    meta = meta.at[:, 1].set(dest_ids.reshape(-1).astype(jnp.float32))
    payload = jnp.concatenate([sums_ext[clusters_here:], meta], axis=1)
    got = lax.all_to_all(
        payload.reshape(device_count, DCAP, -1), "nodes", split_axis=0, concat_axis=0, tiled=True
    ).reshape(remote_slots, -1)
    got_ids = got[:, width + 1].astype(jnp.int32)
    here = jnp.arange(clusters_here, dtype=jnp.int32)
    got_hot = (got_ids[:, None] == here[None, :]).astype(jnp.float32)
    sums_all = sums_ext[:clusters_here] + lax.dot_general(
        got_hot, got[:, :width], contract_rows,
        precision=lax.Precision.HIGHEST, preferred_element_type=jnp.float32,
    )
    counts_all = counts_ext[:clusters_here] + jnp.sum(got_hot * got[:, width:width + 1], axis=0)
    pooled = (sums_all / jnp.sqrt(counts_all + 1.0)[:, None]).astype(jnp.bfloat16)
    first_proj = jnp.dot(pooled, w_first, preferred_element_type=jnp.float32).astype(jnp.bfloat16)
    hidden = jnp.maximum(
        convolve(first_proj, tile_cols, tile_counts, adjacency, myself), 0.0
    ).astype(jnp.bfloat16)
    second_proj = jnp.dot(hidden, w_second, preferred_element_type=jnp.float32).astype(jnp.bfloat16)
    coarse = convolve(second_proj, tile_cols, tile_counts, adjacency, myself).astype(jnp.bfloat16)
    answers = jnp.dot(
        got_hot.astype(jnp.bfloat16), coarse, preferred_element_type=jnp.float32
    ).astype(jnp.bfloat16)
    returned = lax.all_to_all(
        answers.reshape(device_count, DCAP, width), "nodes", split_axis=0, concat_axis=0, tiled=True
    ).reshape(remote_slots, width)
    table = jnp.concatenate([coarse, returned], axis=0)
    value = features.astype(jnp.float32) + jnp.dot(
        one_hot, table, preferred_element_type=jnp.float32
    )
    return value.astype(jnp.bfloat16)


def solution(mesh):
    placed = (
        P("nodes", None),
        P("nodes"),
        P("nodes", None),
        P("nodes"),
        P("nodes", None, None, None),
        P(),
        P(),
    )
    return jax.shard_map(
        local, mesh=mesh, in_specs=placed, out_specs=P("nodes", None), check_vma=False
    )
```

time: 214 us -> 139 us (0.65)
  other arithmetic: 69.1 us -> 40.9 us
  blocking collectives: 0 us -> 24.4 us
  starting transfers between devices: 46.5 us -> 23.4 us
  local copies, waits for them, and re-layouts: 24.9 us -> 3.66 us
  matrix products: 40.2 us -> 22.7 us
  waiting for transfers between devices: 32.4 us -> 22.6 us
    scatter-add x1 -> x0, other arithmetic: 57 us -> none  [local(): jnp.nonzero(remote, size=bound_count, fill_value=0)[0].astype(jnp.int32)]
    all_to_all x3 -> x1, starting transfers between devices: 37.1 us -> 11.5 us  [local(): lax.all_to_all(payload.reshape(device_count, DCAP, -1), 'nodes', split_ax...]
    reduce_min x0 -> x4, other arithmetic: none -> 25.3 us  [distinct_slots(): low = jnp.min(grid, axis=0)]
    all_to_all x0 -> x1, blocking collectives: none -> 24.4 us  [local(): lax.all_to_all(answers.reshape(device_count, DCAP, width), 'nodes', split...]
    gather x3 -> x0, local copies, waits for them, and re-layouts: 18.5 us -> none  [the longest x1 6.19 us: local(): bound_rows = features[chosen]]
    dot_general x16 -> x4, matrix products: 37.3 us -> 20.2 us  [the longest x1 9.57 us: local(): jnp.dot(one_hot, table, preferred_element_type=jnp.float32)]
    reduce_sum x6 -> x3, other arithmetic: 4.36 us -> 10.1 us  [the longest x1 5.99 us: distinct_slots(): slot = jnp.sum(jnp.where(owner_hot, rank, 0), axis=1)]
    all_to_all x3 -> x1, waiting for transfers between devices: 21.5 us -> 16.1 us  [local(): lax.all_to_all(payload.reshape(device_count, DCAP, -1), 'nodes', split_ax...]
  transfers between devices with their start and end apart: 7 -> 5, of which waited for: 6 -> 5; matrix products, arithmetic and copies ran while one was open for 12% -> 0% of each run, Pallas kernels for 0% -> 0%
where the time goes in v1:
time: 139 us; the launch traced here: 138 us
  other arithmetic  40.9 us (29%)
  blocking collectives  24.4 us (18%)
  starting transfers between devices  23.4 us (17%)
  matrix products  22.7 us (16%)
  waiting for transfers between devices  22.6 us (16%)
  local copies, waits for them, and re-layouts  3.66 us (3%)
    reduce_min x4, other arithmetic, distinct_slots(): low = jnp.min(grid, axis=0)  25.3 us
    all_to_all x1, blocking collectives, local(): lax.all_to_all(answers.reshape(device_count, DCAP, width), 'nodes', split...  24.4 us
    all_to_all x1, waiting for transfers between devices, local(): lax.all_to_all(payload.reshape(device_count, DCAP, -1), 'nodes', split_ax...  16.1 us
    all_to_all x1, starting transfers between devices, local(): lax.all_to_all(payload.reshape(device_count, DCAP, -1), 'nodes', split_ax...  11.5 us
    dot_general x1, matrix products, local(): jnp.dot(one_hot, table, preferred_element_type=jnp.float32)  9.57 us
    dot_general x1, matrix products, local(): lax.dot_general(one_hot, features, contract_rows, preferred_element_type=...  9.44 us
    ppermute x2, starting transfers between devices, with_halo(): lax.ppermute(lax.slice_in_dim(block, block.shape[dim] - width, None, axis...  6.84 us
    reduce_sum x1, other arithmetic, distinct_slots(): slot = jnp.sum(jnp.where(owner_hot, rank, 0), axis=1)  5.99 us
  transfers between devices with their start and end apart: 5, of which 5 were waited for; matrix products, arithmetic and copies ran while one was open for 0% of the time, Pallas kernels for 0%

profile of v1, /device:TPU:1, one launch (start us, length us, event | category | flops | bytes accessed | tf_op | source)
XLA Modules:
  0.0 137.9 jit_solution(9210084166086341461)
XLA Ops:
  2.1 0.8 fusion.27
  2.9 9.6 %select_reduce_fusion = s32[128]{0:T(128)S(1)} fusion(s32[8192]{0:T(1024)S(1)} %add_select_fusion, pred[8192]{0:T(1024)(128)(4,1)S(1)} %fusion.27, s32[8192]{0:T(1024)} %param.12), kind=kLoop, calls=%fused_computation.14 | loop fusion | flops 4194176 | bytes 74240 | tf_op jit(solution)/shard_map/reduce_min | solution.py:42
  12.6 5.2 %fusion.7 = s32[128]{0:T(128)S(1)} fusion(s32[128]{0:T(128)S(1)} %select_reduce_fusion, s32[8192]{0:T(1024)S(1)} %add_select_fusion, pred[8192]{0:T(1024)(128)(4,1)S(1)} %fusion.27, s32[8192]{0:T(1024)} %param.12), kind=kLoop, calls=%fused_computation.15 | loop fusion | flops 6291328 | bytes 74752 | tf_op jit(solution)/shard_map/reduce_min | solution.py:42
  17.8 5.2 %fusion.8 = s32[128]{0:T(128)S(1)} fusion(s32[128]{0:T(128)S(1)} %fusion.7, s32[128]{0:T(128)S(1)} %select_reduce_fusion, s32[8192]{0:T(1024)S(1)} %add_select_fusion, pred[8192]{0:T(1024)(128)(4,1)S(1)} %fusion.27, s32[8192]{0:T(1024)} %param.12), kind=kLoop, calls=%fused_computation.16 | loop fusion | flops 8388480 | bytes 75264 | tf_op jit(solution)/shard_map/reduce_min | solution.py:42
  23.0 5.2 %fusion.9 = s32[128]{0:T(128)S(1)} fusion(s32[128]{0:T(128)S(1)} %fusion.8, s32[128]{0:T(128)S(1)} %fusion.7, s32[128]{0:T(128)S(1)} %select_reduce_fusion, s32[8192]{0:T(1024)S(1)} %add_select_fusion, pred[8192]{0:T(1024)(128)(4,1)S(1)} %fusion.27, s32[8192]{0:T(1024)} %param.12), kind=kLoop, calls=%fused_computation.17 | loop fusion | flops 10485632 | bytes 75776 | tf_op jit(solution)/shard_map/reduce_min | solution.py:42
  28.2 6.0 %select_reduce_fusion.1 = s32[8192]{0:T(1024)S(1)} fusion(s32[128]{0:T(128)S(1)} %fusion.9, s32[128]{0:T(128)S(1)} %fusion.8, s32[128]{0:T(128)S(1)} %fusion.7, s32[8192]{0:T(1024)S(1)} %add_select_fusion, pred[8192]{0:T(1024)(128)(4,1)S(1)} %fusion.27, s32[8192]{0:T(1024)} %param.12), kind=kLoop, calls=%fused_computation.18 | loop fusion | flops 12574720 | bytes 108032 | tf_op jit(solution)/shard_map/reduce_sum | solution.py:48
  34.2 0.8 fusion.30
  35.0 3.9 %convert_reduce_fusion = f32[1024]{0:T(1024)S(1)} fusion(s32[8192]{0:T(1024)S(1)} %fusion.30), kind=kLoop, calls=%fused_computation.2 | loop fusion | flops 33553408 | bytes 36864 | tf_op jit(solution)/shard_map/reduce_sum | solution.py:70
  39.8 9.4 %fusion.2 = f32[1024,256]{0,1:T(8,128)S(1)} fusion(bf16[8192,256]{1,0:T(8,128)(2,1)} %param.11, s32[8192]{0:T(1024)S(1)} %fusion.30), kind=kOutput, calls=%fused_computation.6 | convolution fusion | flops 4303355904 | bytes 5275648 | tf_op jit(solution)/shard_map/dot_general | solution.py:67
  50.4 1.1 reshape.149
  51.5 11.5 %all-to-all-start = ((f32[128,4,384]{2,1,0:T(4,128)}), f32[128,4,384]{2,1,0:T(4,128)S(1)}, u32[]{:S(2)}, u32[]{:S(2)}) async-start(f32[128,4,384]{2,1,0:T(4,128)} %reshape.149), calls=%async_computation | async-start | bytes 1572864 | tf_op jit(solution)/shard_map/all_to_all | solution.py:77
  63.1 16.1 %all-to-all-done = f32[128,4,384]{2,1,0:T(4,128)S(1)} async-done(((f32[128,4,384]{2,1,0:T(4,128)}), f32[128,4,384]{2,1,0:T(4,128)S(1)}, u32[]{:S(2)}, u32[]{:S(2)}) %all-to-all-start) | async-done | bytes 786464 | tf_op jit(solution)/shard_map/all_to_all | solution.py:77
  80.1 0.8 fusion.13
  81.2 3.1 %collective-permute-start.1 = (bf16[512,256]{1,0:T(8,128)(2,1)S(1)}, bf16[512,256]{1,0:T(8,128)(2,1)S(1)}, u32[]{:S(2)}, u32[]{:S(2)}) collective-permute-start(bf16[512,256]{1,0:T(8,128)(2,1)S(1)} %convolution_convert_fusion.2), channel_id=1, source_target_pairs={{1,0},{2,1},{3,2},{4,3},{5,4},{6,5},{7,6},{8,7},{9,8},{10,9},{11,1... | collective-permute-start | bytes 786440 | tf_op jit(solution)/shard_map/ppermute | solution.py:17
  84.3 2.5 %collective-permute-start = (bf16[512,256]{1,0:T(8,128)(2,1)S(1)}, bf16[512,256]{1,0:T(8,128)(2,1)S(1)}, u32[]{:S(2)}, u32[]{:S(2)}) collective-permute-start(bf16[512,256]{1,0:T(8,128)(2,1)S(1)} %convolution_convert_fusion.2), channel_id=1, source_target_pairs={{0,1},{1,2},{2,3},{3,4},{4,5},{5,6},{6,7},{7,8},{8,9},{9,10},{10,1... | collective-permute-start | bytes 786440 | tf_op jit(solution)/shard_map/ppermute | solution.py:14
  86.9 2.0 %collective-permute-done.1 = bf16[512,256]{1,0:T(8,128)(2,1)S(1)} collective-permute-done((bf16[512,256]{1,0:T(8,128)(2,1)S(1)}, bf16[512,256]{1,0:T(8,128)(2,1)S(1)}, u32[]{:S(2)}, u32[]{:S(2)}) %collective-permute-start.1) | collective-permute-done | bytes 262176 | tf_op jit(solution)/shard_map/ppermute | solution.py:17
  88.9 1.2 collective-permute-done
  90.8 1.6 %fusion.15 = bf16[4,128,256]{2,1,0:T(8,128)(2,1)S(1)} fusion(bf16[4,6,128,256]{3,2,1,0:T(8,128)(2,1)S(1)} %bitcast.34, bf16[4,6,128,128]{3,2,1,0:T(8,128)(2,1)} %param.15, pred[4,6]{1,0:T(4,128)(4,1)S(1)} %iota_compare_fusion.10), kind=kOutput, calls=%fused_computation.31 | convolution fusion | flops 201981952 | bytes 2621464 | tf_op jit(solution)/shard_map/tkij,tkjf->tif/dot_general | solution.py:31
  92.7 1.9 %collective-permute-start.3 = (bf16[512,256]{1,0:T(8,128)(2,1)S(1)}, bf16[512,256]{1,0:T(8,128)(2,1)S(1)}, u32[]{:S(2)}, u32[]{:S(2)}) collective-permute-start(bf16[512,256]{1,0:T(8,128)(2,1)S(1)} %convolution_convert_fusion.1), channel_id=1, source_target_pairs={{1,0},{2,1},{3,2},{4,3},{5,4},{6,5},{7,6},{8,7},{9,8},{10,9},{11,1... | collective-permute-start | bytes 786440 | tf_op jit(solution)/shard_map/ppermute | solution.py:17
  94.6 4.4 %collective-permute-start.2 = (bf16[512,256]{1,0:T(8,128)(2,1)S(1)}, bf16[512,256]{1,0:T(8,128)(2,1)S(1)}, u32[]{:S(2)}, u32[]{:S(2)}) collective-permute-start(bf16[512,256]{1,0:T(8,128)(2,1)S(1)} %convolution_convert_fusion.1), channel_id=1, source_target_pairs={{0,1},{1,2},{2,3},{3,4},{4,5},{5,6},{6,7},{7,8},{8,9},{9,10},{10,1... | collective-permute-start | bytes 786440 | tf_op jit(solution)/shard_map/ppermute | solution.py:14
  99.0 2.1 %collective-permute-done.3 = bf16[512,256]{1,0:T(8,128)(2,1)S(1)} collective-permute-done((bf16[512,256]{1,0:T(8,128)(2,1)S(1)}, bf16[512,256]{1,0:T(8,128)(2,1)S(1)}, u32[]{:S(2)}, u32[]{:S(2)}) %collective-permute-start.3) | collective-permute-done | bytes 262176 | tf_op jit(solution)/shard_map/ppermute | solution.py:17
  101.2 1.2 collective-permute-done.2
  103.9 24.4 %all_to_all.10 = bf16[128,4,256]{2,1,0:T(4,128)(2,1)S(1)} all-to-all(bf16[128,4,256]{2,1,0:T(4,128)(2,1)S(1)} %reshape.153), channel_id=1, replica_groups=mesh['nodes'=128] {'nodes'}, dimensions={0} | all-to-all | bytes 524288 | tf_op jit(solution)/shard_map/all_to_all | solution.py:98
  128.4 9.6 %fusion.6 = bf16[8192,256]{1,0:T(8,128)(2,1)} fusion(s32[8192]{0:T(1024)S(1)} %fusion.30, bf16[8192,256]{1,0:T(8,128)(2,1)} %param.11, bf16[512,256]{1,0:T(8,128)(2,1)S(1)} %reshape.154, bf16[512,256]{1,0:T(8,128)(2,1)S(1)} %bitcast.42), kind=kOutput, calls=%fused_computation.13 | convolution fusion | flops 4310695936 | bytes 8945664 | tf_op jit(solution)/shard_map/dot_general | solution.py:102
  (42 shorter events, 8.0 us)
Async XLA Ops:
  0.0 80.9 %copy-start = (bf16[256,256]{1,0:T(8,128)(2,1)S(1)}, bf16[256,256]{1,0:T(8,128)(2,1)}, u32[]{:S(2)}) copy-start(bf16[256,256]{1,0:T(8,128)(2,1)} %param.16) | copy-start | bytes 393220
  49.3 13.8 %copy-start.2 = (s32[4,6]{1,0:T(4,128)S(1)}, s32[4,6]{1,0:T(4,128)}, u32[]{:S(2)}) copy-start(s32[4,6]{1,0:T(4,128)} %param.13) | copy-start | bytes 292
  50.4 36.4 %copy-start.4 = (s32[4]{0:T(128)S(1)}, s32[4]{0:T(128)}, u32[]{:S(2)}) copy-start(s32[4]{0:T(128)} %param.14) | copy-start | bytes 52
  51.5 27.7 %all-to-all-start = ((f32[128,4,384]{2,1,0:T(4,128)}), f32[128,4,384]{2,1,0:T(4,128)S(1)}, u32[]{:S(2)}, u32[]{:S(2)}) async-start(f32[128,4,384]{2,1,0:T(4,128)} %reshape.149), calls=%async_computation | async-start | bytes 1572864 | tf_op jit(solution)/shard_map/all_to_all | solution.py:77
  80.9 11.5 %copy-start.1 = (bf16[256,256]{1,0:T(8,128)(2,1)S(1)}, bf16[256,256]{1,0:T(8,128)(2,1)}, u32[]{:S(2)}) copy-start(bf16[256,256]{1,0:T(8,128)(2,1)} %param.17) | copy-start | bytes 393220
  81.2 7.7 %collective-permute-start.1 = (bf16[512,256]{1,0:T(8,128)(2,1)S(1)}, bf16[512,256]{1,0:T(8,128)(2,1)S(1)}, u32[]{:S(2)}, u32[]{:S(2)}) collective-permute-start(bf16[512,256]{1,0:T(8,128)(2,1)S(1)} %convolution_convert_fusion.2), channel_id=1, source_target_pairs={{1,0},{2,1},{3,2},{4,3},{5,4},{6,5},{7,6},{8,7},{9,8},{10,9},{11,1... | collective-permute-start | bytes 786440 | tf_op jit(solution)/shard_map/ppermute | solution.py:17
  84.3 5.8 %collective-permute-start = (bf16[512,256]{1,0:T(8,128)(2,1)S(1)}, bf16[512,256]{1,0:T(8,128)(2,1)S(1)}, u32[]{:S(2)}, u32[]{:S(2)}) collective-permute-start(bf16[512,256]{1,0:T(8,128)(2,1)S(1)} %convolution_convert_fusion.2), channel_id=1, source_target_pairs={{0,1},{1,2},{2,3},{3,4},{4,5},{5,6},{6,7},{7,8},{8,9},{9,10},{10,1... | collective-permute-start | bytes 786440 | tf_op jit(solution)/shard_map/ppermute | solution.py:14
  90.8 12.2 %copy-start.3 = (bf16[4,6,128,128]{3,2,1,0:T(8,128)(2,1)S(1)}, bf16[4,6,128,128]{3,2,1,0:T(8,128)(2,1)}, u32[]{:S(2)}) copy-start(bf16[4,6,128,128]{3,2,1,0:T(8,128)(2,1)} %param.15) | copy-start | bytes 2359300
  92.7 8.4 %collective-permute-start.3 = (bf16[512,256]{1,0:T(8,128)(2,1)S(1)}, bf16[512,256]{1,0:T(8,128)(2,1)S(1)}, u32[]{:S(2)}, u32[]{:S(2)}) collective-permute-start(bf16[512,256]{1,0:T(8,128)(2,1)S(1)} %convolution_convert_fusion.1), channel_id=1, source_target_pairs={{1,0},{2,1},{3,2},{4,3},{5,4},{6,5},{7,6},{8,7},{9,8},{10,9},{11,1... | collective-permute-start | bytes 786440 | tf_op jit(solution)/shard_map/ppermute | solution.py:17
  94.6 7.7 %collective-permute-start.2 = (bf16[512,256]{1,0:T(8,128)(2,1)S(1)}, bf16[512,256]{1,0:T(8,128)(2,1)S(1)}, u32[]{:S(2)}, u32[]{:S(2)}) collective-permute-start(bf16[512,256]{1,0:T(8,128)(2,1)S(1)} %convolution_convert_fusion.1), channel_id=1, source_target_pairs={{0,1},{1,2},{2,3},{3,4},{4,5},{5,6},{6,7},{7,8},{8,9},{9,10},{10,1... | collective-permute-start | bytes 786440 | tf_op jit(solution)/shard_map/ppermute | solution.py:14

commit v2 on v1

v2 whole, which is shorter than its diff:
```python
import jax
import jax.numpy as jnp
from jax import lax
from jax.sharding import PartitionSpec as P

DCAP = 4


def with_halo(block, sides, width):
    for axis, dim in sides:
        count = lax.axis_size(axis)
        forward = [(i, i + 1) for i in range(count - 1)]
        backward = [(target, source) for source, target in forward]
        low = lax.ppermute(
            lax.slice_in_dim(block, block.shape[dim] - width, None, axis=dim), axis, forward
        )
        high = lax.ppermute(lax.slice_in_dim(block, 0, width, axis=dim), axis, backward)
        block = jnp.concatenate([low, block, high], axis=dim)
    return block


def convolve(values, tile_cols, tile_counts, adjacency, myself):
    window = with_halo(values, (("nodes", 0),), values.shape[0])
    tile_size = adjacency.shape[2]
    per_device = tile_cols.shape[0]
    window_tiles = window.reshape(-1, tile_size, window.shape[1])
    offsets = tile_cols - (myself - 1) * per_device
    picked = window_tiles[offsets]
    live = jnp.arange(tile_cols.shape[1], dtype=jnp.int32)[None, :] < tile_counts[:, None]
    weights = jnp.where(live[:, :, None, None], adjacency, jnp.zeros((), adjacency.dtype))
    result = jnp.einsum("tkij,tkjf->tif", weights, picked, preferred_element_type=jnp.float32)
    return result.reshape(values.shape[0], values.shape[1])


def distinct_slots(owner_hot, lid_hot, clusters_here):
    contract_rows = (((0,), (0,)), ((), ()))
    presence = lax.dot_general(owner_hot, lid_hot, contract_rows, preferred_element_type=jnp.float32)
    named = (presence > 0).astype(jnp.bfloat16)
    lanes = jnp.arange(clusters_here, dtype=jnp.int32)
    before = (lanes[:, None] < lanes[None, :]).astype(jnp.bfloat16)
    rank = jnp.dot(named, before, preferred_element_type=jnp.float32)
    per_owner = jnp.dot(lid_hot, rank.T.astype(jnp.bfloat16), preferred_element_type=jnp.float32)
    slot = jnp.sum(per_owner * owner_hot.astype(jnp.float32), axis=1).astype(jnp.int32)
    return presence, rank, slot


def local(features, cluster_ids, tile_cols, tile_counts, adjacency, w_first, w_second):
    device_count = lax.axis_size("nodes")
    myself = lax.axis_index("nodes")
    fine_rows, width = features.shape
    clusters_here = adjacency.shape[0] * adjacency.shape[2]
    owners = cluster_ids // clusters_here
    lids = cluster_ids - owners * clusters_here
    remote = owners != myself
    peers = jnp.arange(device_count, dtype=jnp.int32)
    here = jnp.arange(clusters_here, dtype=jnp.int32)
    owner_hot = (owners[:, None] == peers[None, :]).astype(jnp.bfloat16)
    lid_hot = (lids[:, None] == here[None, :]).astype(jnp.bfloat16)
    presence, rank, slot = distinct_slots(owner_hot, lid_hot, clusters_here)
    remote_slots = device_count * DCAP
    slot_column = jnp.where(remote, owners * DCAP + slot, -1)
    slot_range = jnp.arange(remote_slots, dtype=jnp.int32)
    remote_hot = (slot_column[:, None] == slot_range[None, :]).astype(jnp.bfloat16)
    local_hot = jnp.where(remote[:, None], jnp.zeros((), jnp.bfloat16), lid_hot)
    contract_rows = (((0,), (0,)), ((), ()))
    remote_sums = lax.dot_general(
        remote_hot, features, contract_rows, preferred_element_type=jnp.float32
    )

    named = (presence > 0) & (peers != myself)[:, None]
    slot_counts = []
    slot_ids = []
    for k in range(DCAP):
        chosen = named & (rank == k)
        slot_counts.append(jnp.sum(jnp.where(chosen, presence, 0.0), axis=1))
        slot_ids.append(jnp.sum(jnp.where(chosen, here[None, :], 0), axis=1))
    slot_counts = jnp.stack(slot_counts, axis=1).reshape(-1)
    slot_ids = jnp.stack(slot_ids, axis=1).reshape(-1)
    meta_lanes = jnp.arange(128, dtype=jnp.int32)[None, :]
    meta = jnp.where(
        meta_lanes == 0,
        slot_counts[:, None],
        jnp.where(meta_lanes == 1, slot_ids[:, None].astype(jnp.float32), 0.0),
    )
    payload = jnp.concatenate([remote_sums, meta], axis=1)
    got = lax.all_to_all(
        payload.reshape(device_count, DCAP, -1), "nodes", split_axis=0, concat_axis=0, tiled=True
    ).reshape(remote_slots, -1)
    local_sums = lax.dot_general(
        local_hot, features, contract_rows, preferred_element_type=jnp.float32
    )
    local_counts = lax.dynamic_index_in_dim(presence, myself, axis=0, keepdims=False)
    got_ids = got[:, width + 1].astype(jnp.int32)
    got_hot = (got_ids[:, None] == here[None, :]).astype(jnp.float32)
    sums_all = local_sums + lax.dot_general(
        got_hot, got[:, :width], contract_rows,
        precision=lax.Precision.HIGHEST, preferred_element_type=jnp.float32,
    )
    counts_all = local_counts + jnp.sum(got_hot * got[:, width:width + 1], axis=0)
    pooled = (sums_all / jnp.sqrt(counts_all + 1.0)[:, None]).astype(jnp.bfloat16)
    first_proj = jnp.dot(pooled, w_first, preferred_element_type=jnp.float32).astype(jnp.bfloat16)
    hidden = jnp.maximum(
        convolve(first_proj, tile_cols, tile_counts, adjacency, myself), 0.0
    ).astype(jnp.bfloat16)
    second_proj = jnp.dot(hidden, w_second, preferred_element_type=jnp.float32).astype(jnp.bfloat16)
    coarse = convolve(second_proj, tile_cols, tile_counts, adjacency, myself).astype(jnp.bfloat16)
    answers = jnp.dot(
        got_hot.astype(jnp.bfloat16), coarse, preferred_element_type=jnp.float32
    ).astype(jnp.bfloat16)
    returned = lax.all_to_all(
        answers.reshape(device_count, DCAP, width), "nodes", split_axis=0, concat_axis=0, tiled=True
    ).reshape(remote_slots, width)
    value = (
        features.astype(jnp.float32)
        + jnp.dot(local_hot, coarse, preferred_element_type=jnp.float32)
        + jnp.dot(remote_hot, returned, preferred_element_type=jnp.float32)
    )
    return value.astype(jnp.bfloat16)


def solution(mesh):
    placed = (
        P("nodes", None),
        P("nodes"),
        P("nodes", None),
        P("nodes"),
        P("nodes", None, None, None),
        P(),
        P(),
    )
    return jax.shard_map(
        local, mesh=mesh, in_specs=placed, out_specs=P("nodes", None), check_vma=False
    )
```

time: 139 us -> 105 us (0.76)
  other arithmetic: 40.9 us -> 2.03 us
  blocking collectives: 24.4 us -> 0 us
  matrix products: 22.7 us -> 43.5 us
  starting transfers between devices: 23.4 us -> 37 us
  waiting for transfers between devices: 22.6 us -> 17 us
    reduce_min x4 -> x0, other arithmetic: 25.3 us -> none  [distinct_slots(): low = jnp.min(grid, axis=0)]
    all_to_all x1 -> x0, blocking collectives: 24.4 us -> none  [local(): lax.all_to_all(answers.reshape(device_count, DCAP, width), 'nodes', split...]
    dot_general x2 -> x7, matrix products: 19 us -> 38.4 us  [the longest x1 9.48 us: local(): jnp.dot(local_hot, coarse, preferred_element_type=jnp.float32)]
    all_to_all x0 -> x1, starting transfers between devices: none -> 13.7 us  [local(): lax.all_to_all(answers.reshape(device_count, DCAP, width), 'nodes', split...]
    reduce_sum x2, other arithmetic: 9.88 us -> 0.3 us  [local(): slot_ids.append(jnp.sum(jnp.where(chosen, here[None, :], 0), axis=1))]
    all_to_all x1, waiting for transfers between devices: 16.1 us -> 9.22 us  [local(): lax.all_to_all(payload.reshape(device_count, DCAP, -1), 'nodes', split_ax...]
    another operation x4 -> x1, other arithmetic: 2.71 us -> 0.01 us  [local(): slot_counts = jnp.stack(slot_counts, axis=1).reshape(-1)]
  transfers between devices with their start and end apart: 5 -> 6, of which waited for: 5 -> 6; matrix products, arithmetic and copies ran while one was open for 0% -> 16% of each run, Pallas kernels for 0% -> 0%
where the time goes in v2:
time: 105 us; the launch traced here: 104 us
  matrix products  43.5 us (41%)
  starting transfers between devices  37 us (35%)
  waiting for transfers between devices  17 us (16%)
  local copies, waits for them, and re-layouts  4.47 us (4%)
  other arithmetic  2.03 us (2%)
    all_to_all x1, starting transfers between devices, local(): lax.all_to_all(answers.reshape(device_count, DCAP, width), 'nodes', split...  13.7 us
    all_to_all x1, starting transfers between devices, local(): lax.all_to_all(payload.reshape(device_count, DCAP, -1), 'nodes', split_ax...  11.5 us
    dot_general x1, matrix products, local(): jnp.dot(local_hot, coarse, preferred_element_type=jnp.float32)  9.48 us
    all_to_all x1, waiting for transfers between devices, local(): lax.all_to_all(payload.reshape(device_count, DCAP, -1), 'nodes', split_ax...  9.22 us
    dot_general x1, matrix products, local(): jnp.dot(remote_hot, returned, preferred_element_type=jnp.float32)  7.61 us
    ppermute x2, starting transfers between devices, with_halo(): lax.ppermute(lax.slice_in_dim(block, block.shape[dim] - width, None, axis...  6.85 us
    dot_general x1, matrix products, local(): lax.dot_general(local_hot, features, contract_rows, preferred_element_typ...  6.81 us
    dot_general x1, matrix products, local(): lax.dot_general(remote_hot, features, contract_rows, preferred_element_ty...  5.94 us
  transfers between devices with their start and end apart: 6, of which 6 were waited for; matrix products, arithmetic and copies ran while one was open for 16% of the time, Pallas kernels for 0%

profile of v2, /device:TPU:1, one launch (start us, length us, event | category | flops | bytes accessed | tf_op | source)
XLA Modules:
  0.0 104.4 jit_solution(838454065711009383)
XLA Ops:
  0.0 0.8 add_select_fusion
  0.8 3.2 %broadcast_compare_fusion = (pred[128,512]{1,0:T(32,128)(4,1)S(1)}, f32[128,512]{1,0:T(8,128)S(1)}) fusion(s32[8192]{0:T(1024)S(1)} %get-tuple-element.14, s32[8192]{0:T(1024)S(1)} %get-tuple-element.13), kind=kOutput, calls=%fused_computation.71 | convolution fusion | flops 1079050240 | bytes 393216 | tf_op jit(solution)/shard_map/dot_general | solution.py:37
  4.6 4.8 %fusion.24 = f32[8192]{0:T(1024)S(1)} fusion(s32[8192]{0:T(1024)S(1)} %get-tuple-element.13, s32[8192]{0:T(1024)S(1)} %get-tuple-element.14, bf16[128,512]{1,0:T(8,128)(2,1)S(1)} %get-tuple-element.17), kind=kOutput, calls=%fused_computation.28 | convolution fusion | flops 1083170816 | bytes 229376 | tf_op jit(solution)/shard_map/dot_general | solution.py:42
  10.3 5.9 %fusion.1 = f32[512,256]{0,1:T(8,128)S(1)} fusion(bf16[8192,256]{1,0:T(8,128)(2,1)} %param.7, s32[8192]{0:T(1024)S(1)} %add_select_fusion.1), kind=kOutput, calls=%fused_computation.4 | convolution fusion | flops 2151677952 | bytes 4751360 | tf_op jit(solution)/shard_map/dot_general | solution.py:66
  16.7 1.1 %reshape.81 = f32[128,4,384]{2,1,0:T(4,128)} reshape(f32[512,384]{1,0:T(8,128)S(1)} %copy.16) | data formatting | bytes 1572864 | tf_op jit(solution)/shard_map/reshape | solution.py:87
  17.8 11.5 %all-to-all-start = ((f32[128,4,384]{2,1,0:T(4,128)}), f32[128,4,384]{2,1,0:T(4,128)S(1)}, u32[]{:S(2)}, u32[]{:S(2)}) async-start(f32[128,4,384]{2,1,0:T(4,128)} %reshape.81), calls=%async_computation | async-start | bytes 1572864 | tf_op jit(solution)/shard_map/all_to_all | solution.py:86
  29.4 6.8 %fusion.10 = f32[512,256]{1,0:T(8,128)S(1)} fusion(bf16[8192,256]{1,0:T(8,128)(2,1)} %param.7, s32[8192]{0:T(1024)S(1)} %get-tuple-element.14, pred[8192]{0:T(1024)(128)(4,1)S(1)} %broadcast_compare_fusion.1), kind=kOutput, calls=%fused_computation.14 | convolution fusion | flops 2160066560 | bytes 4759552 | tf_op jit(solution)/shard_map/dot_general | solution.py:89
  36.3 9.2 %all-to-all-done = f32[128,4,384]{2,1,0:T(4,128)S(1)} async-done(((f32[128,4,384]{2,1,0:T(4,128)}), f32[128,4,384]{2,1,0:T(4,128)S(1)}, u32[]{:S(2)}, u32[]{:S(2)}) %all-to-all-start) | async-done | bytes 786464 | tf_op jit(solution)/shard_map/all_to_all | solution.py:86
  46.4 1.1 %fusion.27 = bf16[512,256]{1,0:T(8,128)(2,1)S(1)} fusion(f32[512,256]{1,0:T(8,128)S(1)} %fusion.10, f32[512,384]{1,0:T(8,128)S(1)} %reshape.82, s32[512]{0:T(512)S(1)} %fusion.36, f32[512]{0:T(512)S(1)} %add_sqrt_fusion), kind=kOutput, calls=%fused_computation.34 | convolution fusion | flops 805961728 | bytes 1314816 | tf_op jit(solution)/shard_map/dot_general | solution.py:95
  47.8 3.1 %collective-permute-start.1 = (bf16[512,256]{1,0:T(8,128)(2,1)S(1)}, bf16[512,256]{1,0:T(8,128)(2,1)S(1)}, u32[]{:S(2)}, u32[]{:S(2)}) collective-permute-start(bf16[512,256]{1,0:T(8,128)(2,1)S(1)} %convolution_convert_fusion.2), channel_id=1, source_target_pairs={{1,0},{2,1},{3,2},{4,3},{5,4},{6,5},{7,6},{8,7},{9,8},{10,9},{11,1... | collective-permute-start | bytes 786440 | tf_op jit(solution)/shard_map/ppermute | solution.py:17
  50.9 2.5 %collective-permute-start = (bf16[512,256]{1,0:T(8,128)(2,1)S(1)}, bf16[512,256]{1,0:T(8,128)(2,1)S(1)}, u32[]{:S(2)}, u32[]{:S(2)}) collective-permute-start(bf16[512,256]{1,0:T(8,128)(2,1)S(1)} %convolution_convert_fusion.2), channel_id=1, source_target_pairs={{0,1},{1,2},{2,3},{3,4},{4,5},{5,6},{6,7},{7,8},{8,9},{9,10},{10,1... | collective-permute-start | bytes 786440 | tf_op jit(solution)/shard_map/ppermute | solution.py:14
  53.4 2.0 %collective-permute-done.1 = bf16[512,256]{1,0:T(8,128)(2,1)S(1)} collective-permute-done((bf16[512,256]{1,0:T(8,128)(2,1)S(1)}, bf16[512,256]{1,0:T(8,128)(2,1)S(1)}, u32[]{:S(2)}, u32[]{:S(2)}) %collective-permute-start.1) | collective-permute-done | bytes 262176 | tf_op jit(solution)/shard_map/ppermute | solution.py:17
  55.5 1.2 %collective-permute-done = bf16[512,256]{1,0:T(8,128)(2,1)S(1)} collective-permute-done((bf16[512,256]{1,0:T(8,128)(2,1)S(1)}, bf16[512,256]{1,0:T(8,128)(2,1)S(1)}, u32[]{:S(2)}, u32[]{:S(2)}) %collective-permute-start) | collective-permute-done | bytes 262176 | tf_op jit(solution)/shard_map/ppermute | solution.py:14
  57.4 1.6 %fusion.29 = bf16[4,128,256]{2,1,0:T(8,128)(2,1)S(1)} fusion(bf16[4,6,128,256]{3,2,1,0:T(8,128)(2,1)S(1)} %bitcast.43, bf16[4,6,128,128]{3,2,1,0:T(8,128)(2,1)} %param.11, pred[4,6]{1,0:T(4,128)(4,1)S(1)} %iota_compare_fusion.20), kind=kOutput, calls=%fused_computation.39 | convolution fusion | flops 201981952 | bytes 2621464 | tf_op jit(solution)/shard_map/tkij,tkjf->tif/dot_general | solution.py:31
  59.2 1.9 %collective-permute-start.3 = (bf16[512,256]{1,0:T(8,128)(2,1)S(1)}, bf16[512,256]{1,0:T(8,128)(2,1)S(1)}, u32[]{:S(2)}, u32[]{:S(2)}) collective-permute-start(bf16[512,256]{1,0:T(8,128)(2,1)S(1)} %convolution_convert_fusion.1), channel_id=1, source_target_pairs={{1,0},{2,1},{3,2},{4,3},{5,4},{6,5},{7,6},{8,7},{9,8},{10,9},{11,1... | collective-permute-start | bytes 786440 | tf_op jit(solution)/shard_map/ppermute | solution.py:17
  61.1 4.4 %collective-permute-start.2 = (bf16[512,256]{1,0:T(8,128)(2,1)S(1)}, bf16[512,256]{1,0:T(8,128)(2,1)S(1)}, u32[]{:S(2)}, u32[]{:S(2)}) collective-permute-start(bf16[512,256]{1,0:T(8,128)(2,1)S(1)} %convolution_convert_fusion.1), channel_id=1, source_target_pairs={{0,1},{1,2},{2,3},{3,4},{4,5},{5,6},{6,7},{7,8},{8,9},{9,10},{10,1... | collective-permute-start | bytes 786440 | tf_op jit(solution)/shard_map/ppermute | solution.py:14
  65.5 2.1 %collective-permute-done.3 = bf16[512,256]{1,0:T(8,128)(2,1)S(1)} collective-permute-done((bf16[512,256]{1,0:T(8,128)(2,1)S(1)}, bf16[512,256]{1,0:T(8,128)(2,1)S(1)}, u32[]{:S(2)}, u32[]{:S(2)}) %collective-permute-start.3) | collective-permute-done | bytes 262176 | tf_op jit(solution)/shard_map/ppermute | solution.py:17
  67.6 1.2 %collective-permute-done.2 = bf16[512,256]{1,0:T(8,128)(2,1)S(1)} collective-permute-done((bf16[512,256]{1,0:T(8,128)(2,1)S(1)}, bf16[512,256]{1,0:T(8,128)(2,1)S(1)}, u32[]{:S(2)}, u32[]{:S(2)}) %collective-permute-start.2) | collective-permute-done | bytes 262176 | tf_op jit(solution)/shard_map/ppermute | solution.py:14
  69.5 1.6 %fusion.28 = bf16[4,128,256]{2,1,0:T(8,128)(2,1)S(1)} fusion(bf16[4,6,128,256]{3,2,1,0:T(8,128)(2,1)S(1)} %bitcast.42, bf16[4,6,128,128]{3,2,1,0:T(8,128)(2,1)} %param.11, pred[4,6]{1,0:T(4,128)(4,1)S(1)} %iota_compare_fusion.20), kind=kOutput, calls=%fused_computation.35 | convolution fusion | flops 201850880 | bytes 2621464 | tf_op jit(solution)/shard_map/tkij,tkjf->tif/dot_general | solution.py:31
  71.4 0.8 reshape.85
  72.2 13.7 %all-to-all-start.1 = ((bf16[128,4,256]{2,1,0:T(4,128)(2,1)}), bf16[128,4,256]{2,1,0:T(4,128)(2,1)S(1)}, u32[]{:S(2)}, u32[]{:S(2)}) async-start(bf16[128,4,256]{2,1,0:T(4,128)(2,1)} %reshape.85), calls=%async_computation.1 | async-start | bytes 524288 | tf_op jit(solution)/shard_map/all_to_all | solution.py:110
  85.9 9.5 %convolution_add_fusion = f32[8192,256]{1,0:T(8,128)} fusion(bf16[512,256]{1,0:T(8,128)(2,1)S(1)} %bitcast.55, s32[8192]{0:T(1024)S(1)} %get-tuple-element.14, bf16[8192,256]{1,0:T(8,128)(2,1)} %param.7, pred[8192]{0:T(1024)(128)(4,1)S(1)} %broadcast_compare_fusion.1), kind=kOutput, calls=%fused_computation.12 | convolution fusion | flops 2164260864 | bytes 12886016 | tf_op jit(solution)/shard_map/dot_general | solution.py:115
  95.4 1.3 %all-to-all-done.1 = bf16[128,4,256]{2,1,0:T(4,128)(2,1)S(1)} async-done(((bf16[128,4,256]{2,1,0:T(4,128)(2,1)}), bf16[128,4,256]{2,1,0:T(4,128)(2,1)S(1)}, u32[]{:S(2)}, u32[]{:S(2)}) %all-to-all-start.1) | async-done | bytes 262176 | tf_op jit(solution)/shard_map/all_to_all | solution.py:110
  96.7 7.6 %fusion.7 = bf16[8192,256]{1,0:T(8,128)(2,1)} fusion(f32[8192,256]{1,0:T(8,128)} %convolution_add_fusion, bf16[512,256]{1,0:T(8,128)(2,1)S(1)} %reshape.86, s32[8192]{0:T(1024)S(1)} %add_select_fusion.1), kind=kOutput, calls=%fused_computation.11 | convolution fusion | flops 2155872256 | bytes 12877824 | tf_op jit(solution)/shard_map/dot_general | solution.py:116
  (44 shorter events, 5.2 us)
Async XLA Ops:
  0.0 47.5 %copy-start = (bf16[256,256]{1,0:T(8,128)(2,1)S(1)}, bf16[256,256]{1,0:T(8,128)(2,1)}, u32[]{:S(2)}) copy-start(bf16[256,256]{1,0:T(8,128)(2,1)} %param.12) | copy-start | bytes 393220
  4.6 4.9 %copy-start.1 = (s32[8192]{0:T(1024)S(1)}, s32[8192]{0:T(1024)}, u32[]{:S(2)}) copy-start(s32[8192]{0:T(1024)} %param.8) | copy-start | bytes 98308
  16.2 13.1 %copy-start.3 = (s32[4,6]{1,0:T(4,128)S(1)}, s32[4,6]{1,0:T(4,128)}, u32[]{:S(2)}) copy-start(s32[4,6]{1,0:T(4,128)} %param.9) | copy-start | bytes 292
  17.8 27.7 %all-to-all-start = ((f32[128,4,384]{2,1,0:T(4,128)}), f32[128,4,384]{2,1,0:T(4,128)S(1)}, u32[]{:S(2)}, u32[]{:S(2)}) async-start(f32[128,4,384]{2,1,0:T(4,128)} %reshape.81), calls=%async_computation | async-start | bytes 1572864 | tf_op jit(solution)/shard_map/all_to_all | solution.py:86
  36.3 17.1 %copy-start.4 = (s32[4]{0:T(128)S(1)}, s32[4]{0:T(128)}, u32[]{:S(2)}) copy-start(s32[4]{0:T(128)} %param.10) | copy-start | bytes 52
  47.5 11.4 %copy-start.2 = (bf16[256,256]{1,0:T(8,128)(2,1)S(1)}, bf16[256,256]{1,0:T(8,128)(2,1)}, u32[]{:S(2)}) copy-start(bf16[256,256]{1,0:T(8,128)(2,1)} %param.13) | copy-start | bytes 393220
  47.8 7.7 %collective-permute-start.1 = (bf16[512,256]{1,0:T(8,128)(2,1)S(1)}, bf16[512,256]{1,0:T(8,128)(2,1)S(1)}, u32[]{:S(2)}, u32[]{:S(2)}) collective-permute-start(bf16[512,256]{1,0:T(8,128)(2,1)S(1)} %convolution_convert_fusion.2), channel_id=1, source_target_pairs={{1,0},{2,1},{3,2},{4,3},{5,4},{6,5},{7,6},{8,7},{9,8},{10,9},{11,1... | collective-permute-start | bytes 786440 | tf_op jit(solution)/shard_map/ppermute | solution.py:17
  50.9 5.8 %collective-permute-start = (bf16[512,256]{1,0:T(8,128)(2,1)S(1)}, bf16[512,256]{1,0:T(8,128)(2,1)S(1)}, u32[]{:S(2)}, u32[]{:S(2)}) collective-permute-start(bf16[512,256]{1,0:T(8,128)(2,1)S(1)} %convolution_convert_fusion.2), channel_id=1, source_target_pairs={{0,1},{1,2},{2,3},{3,4},{4,5},{5,6},{6,7},{7,8},{8,9},{9,10},{10,1... | collective-permute-start | bytes 786440 | tf_op jit(solution)/shard_map/ppermute | solution.py:14
  59.2 8.4 %collective-permute-start.3 = (bf16[512,256]{1,0:T(8,128)(2,1)S(1)}, bf16[512,256]{1,0:T(8,128)(2,1)S(1)}, u32[]{:S(2)}, u32[]{:S(2)}) collective-permute-start(bf16[512,256]{1,0:T(8,128)(2,1)S(1)} %convolution_convert_fusion.1), channel_id=1, source_target_pairs={{1,0},{2,1},{3,2},{4,3},{5,4},{6,5},{7,6},{8,7},{9,8},{10,9},{11,1... | collective-permute-start | bytes 786440 | tf_op jit(solution)/shard_map/ppermute | solution.py:17
  61.1 7.7 %collective-permute-start.2 = (bf16[512,256]{1,0:T(8,128)(2,1)S(1)}, bf16[512,256]{1,0:T(8,128)(2,1)S(1)}, u32[]{:S(2)}, u32[]{:S(2)}) collective-permute-start(bf16[512,256]{1,0:T(8,128)(2,1)S(1)} %convolution_convert_fusion.1), channel_id=1, source_target_pairs={{0,1},{1,2},{2,3},{3,4},{4,5},{5,6},{6,7},{7,8},{8,9},{9,10},{10,1... | collective-permute-start | bytes 786440 | tf_op jit(solution)/shard_map/ppermute | solution.py:14
  72.2 24.5 %all-to-all-start.1 = ((bf16[128,4,256]{2,1,0:T(4,128)(2,1)}), bf16[128,4,256]{2,1,0:T(4,128)(2,1)S(1)}, u32[]{:S(2)}, u32[]{:S(2)}) async-start(bf16[128,4,256]{2,1,0:T(4,128)(2,1)} %reshape.85), calls=%async_computation.1 | async-start | bytes 524288 | tf_op jit(solution)/shard_map/all_to_all | solution.py:110

commit v3 on v2

--- a/solution.py
+++ b/solution.py
@@ -74,29 +74,28 @@
         chosen = named & (rank == k)
         slot_counts.append(jnp.sum(jnp.where(chosen, presence, 0.0), axis=1))
         slot_ids.append(jnp.sum(jnp.where(chosen, here[None, :], 0), axis=1))
-    slot_counts = jnp.stack(slot_counts, axis=1).reshape(-1)
-    slot_ids = jnp.stack(slot_ids, axis=1).reshape(-1)
-    meta_lanes = jnp.arange(128, dtype=jnp.int32)[None, :]
-    meta = jnp.where(
-        meta_lanes == 0,
-        slot_counts[:, None],
-        jnp.where(meta_lanes == 1, slot_ids[:, None].astype(jnp.float32), 0.0),
+    slot_counts = jnp.stack(slot_counts, axis=1)
+    slot_ids = jnp.stack(slot_ids, axis=1).astype(jnp.float32)
+    meta = jnp.concatenate(
+        [slot_counts, slot_ids, jnp.zeros((device_count, 128 - 2 * DCAP), jnp.float32)], axis=1
     )
-    payload = jnp.concatenate([remote_sums, meta], axis=1)
+    payload = jnp.concatenate([remote_sums.reshape(device_count, DCAP * width), meta], axis=1)
     got = lax.all_to_all(
-        payload.reshape(device_count, DCAP, -1), "nodes", split_axis=0, concat_axis=0, tiled=True
-    ).reshape(remote_slots, -1)
+        payload.reshape(device_count, 1, -1), "nodes", split_axis=0, concat_axis=0, tiled=True
+    ).reshape(device_count, -1)
+    got_sums = got[:, : DCAP * width].reshape(remote_slots, width)
+    got_counts = got[:, DCAP * width : DCAP * width + DCAP].reshape(remote_slots)
+    got_ids = got[:, DCAP * width + DCAP : DCAP * width + 2 * DCAP].reshape(remote_slots).astype(jnp.int32)
     local_sums = lax.dot_general(
         local_hot, features, contract_rows, preferred_element_type=jnp.float32
     )
     local_counts = lax.dynamic_index_in_dim(presence, myself, axis=0, keepdims=False)
-    got_ids = got[:, width + 1].astype(jnp.int32)
     got_hot = (got_ids[:, None] == here[None, :]).astype(jnp.float32)
     sums_all = local_sums + lax.dot_general(
-        got_hot, got[:, :width], contract_rows,
+        got_hot, got_sums, contract_rows,
         precision=lax.Precision.HIGHEST, preferred_element_type=jnp.float32,
     )
-    counts_all = local_counts + jnp.sum(got_hot * got[:, width:width + 1], axis=0)
+    counts_all = local_counts + jnp.sum(got_hot * got_counts[:, None], axis=0)
     pooled = (sums_all / jnp.sqrt(counts_all + 1.0)[:, None]).astype(jnp.bfloat16)
     first_proj = jnp.dot(pooled, w_first, preferred_element_type=jnp.float32).astype(jnp.bfloat16)
     hidden = jnp.maximum(

time: 105 us -> 102 us (0.971)
  waiting for transfers between devices: 17 us -> 15 us
    dot_general x2, matrix products: 3.15 us -> 0.86 us  [convolve(): jnp.einsum('tkij,tkjf->tif', weights, picked, preferred_element_type=jnp....]
    all_to_all x1, waiting for transfers between devices: 9.22 us -> 7.2 us  [local(): lax.all_to_all(payload.reshape(device_count, 1, -1), 'nodes', split_axis=...]
    dot_general x1, matrix products: 5.94 us -> 7.82 us  [local(): lax.dot_general(remote_hot, features, contract_rows, preferred_element_ty...]
where the time goes in v3:
time: 102 us
  matrix products  43.1 us (42%)
  starting transfers between devices  37 us (36%)
  waiting for transfers between devices  15 us (15%)
  local copies, waits for them, and re-layouts  4.8 us (5%)
  other arithmetic  1.61 us (2%)
    all_to_all x1, starting transfers between devices, local(): lax.all_to_all(answers.reshape(device_count, DCAP, width), 'nodes', split...  13.6 us
    all_to_all x1, starting transfers between devices, local(): lax.all_to_all(payload.reshape(device_count, 1, -1), 'nodes', split_axis=...  11.5 us
    dot_general x1, matrix products, local(): jnp.dot(local_hot, coarse, preferred_element_type=jnp.float32)  9.47 us
    dot_general x1, matrix products, local(): lax.dot_general(remote_hot, features, contract_rows, preferred_element_ty...  7.82 us
    dot_general x1, matrix products, local(): jnp.dot(remote_hot, returned, preferred_element_type=jnp.float32)  7.61 us
    all_to_all x1, waiting for transfers between devices, local(): lax.all_to_all(payload.reshape(device_count, 1, -1), 'nodes', split_axis=...  7.2 us
    ppermute x2, starting transfers between devices, with_halo(): lax.ppermute(lax.slice_in_dim(block, block.shape[dim] - width, None, axis...  6.94 us
    dot_general x1, matrix products, local(): lax.dot_general(local_hot, features, contract_rows, preferred_element_typ...  6.81 us
  transfers between devices with their start and end apart: 6, of which 6 were waited for; matrix products, arithmetic and copies ran while one was open for 16% of the time, Pallas kernels for 0%

profile of v3, /device:TPU:1, one launch (start us, length us, event | category | flops | bytes accessed | tf_op | source)
XLA Modules:
  0.0 101.8 jit_solution(7091945306230731593)
XLA Ops:
  0.0 0.8 add_select_fusion
  0.8 3.2 %broadcast_compare_fusion = (pred[128,512]{1,0:T(32,128)(4,1)S(1)}, f32[128,512]{1,0:T(8,128)S(1)}) fusion(s32[8192]{0:T(1024)S(1)} %get-tuple-element.26, s32[8192]{0:T(1024)S(1)} %get-tuple-element.25), kind=kOutput, calls=%fused_computation.66 | convolution fusion | flops 1079050240 | bytes 393216 | tf_op jit(solution)/shard_map/dot_general | solution.py:37
  4.6 4.9 %fusion.24 = f32[8192]{0:T(1024)S(1)} fusion(s32[8192]{0:T(1024)S(1)} %get-tuple-element.25, s32[8192]{0:T(1024)S(1)} %get-tuple-element.26, bf16[128,512]{1,0:T(8,128)(2,1)S(1)} %get-tuple-element.29), kind=kOutput, calls=%fused_computation.28 | convolution fusion | flops 1083170816 | bytes 229376 | tf_op jit(solution)/shard_map/dot_general | solution.py:42
  10.3 7.8 %fusion.1 = f32[512,256]{1,0:T(8,128)S(1)} fusion(bf16[8192,256]{1,0:T(8,128)(2,1)} %param.7, s32[8192]{0:T(1024)S(1)} %add_select_fusion.1), kind=kOutput, calls=%fused_computation.4 | convolution fusion | flops 2151677952 | bytes 4751360 | tf_op jit(solution)/shard_map/dot_general | solution.py:66
  18.5 1.2 %reshape.77 = f32[128,1,1152]{2,1,0:T(1,128)} reshape(f32[128,1152]{1,0:T(8,128)S(1)} %concatenate.9) | data formatting | bytes 1179648 | tf_op jit(solution)/shard_map/reshape | solution.py:84
  19.7 11.5 %all-to-all-start = ((f32[128,1,1152]{2,1,0:T(1,128)}), f32[128,1,1152]{2,1,0:T(1,128)S(1)}, u32[]{:S(2)}, u32[]{:S(2)}) async-start(f32[128,1,1152]{2,1,0:T(1,128)} %reshape.77), calls=%async_computation | async-start | bytes 1179648 | tf_op jit(solution)/shard_map/all_to_all | solution.py:83
  31.2 6.8 %fusion.10 = f32[512,256]{1,0:T(8,128)S(1)} fusion(bf16[8192,256]{1,0:T(8,128)(2,1)} %param.7, s32[8192]{0:T(1024)S(1)} %get-tuple-element.26, pred[8192]{0:T(1024)(128)(4,1)S(1)} %broadcast_compare_fusion.1), kind=kOutput, calls=%fused_computation.14 | convolution fusion | flops 2160066560 | bytes 4759552 | tf_op jit(solution)/shard_map/dot_general | solution.py:89
  38.2 7.2 %all-to-all-done = f32[128,1,1152]{2,1,0:T(1,128)S(1)} async-done(((f32[128,1,1152]{2,1,0:T(1,128)}), f32[128,1,1152]{2,1,0:T(1,128)S(1)}, u32[]{:S(2)}, u32[]{:S(2)}) %all-to-all-start) | async-done | bytes 589856 | tf_op jit(solution)/shard_map/all_to_all | solution.py:83
  46.2 1.1 %fusion.27 = bf16[512,256]{1,0:T(8,128)(2,1)S(1)} fusion(f32[512,256]{1,0:T(8,128)S(1)} %fusion.10, f32[512,256]{1,0:T(8,128)S(1)} %reshape.79, s32[512]{0:T(512)S(1)} %convert_element_type.76, f32[512]{0:T(512)S(1)} %add_sqrt_fusion), kind=kOutput, calls=%fused_computation.34 | convolution fusion | flops 805961728 | bytes 1314816 | tf_op jit(solution)/shard_map/dot_general | solution.py:94
  47.6 3.0 %collective-permute-start.1 = (bf16[512,256]{1,0:T(8,128)(2,1)S(1)}, bf16[512,256]{1,0:T(8,128)(2,1)S(1)}, u32[]{:S(2)}, u32[]{:S(2)}) collective-permute-start(bf16[512,256]{1,0:T(8,128)(2,1)S(1)} %convolution_convert_fusion.2), channel_id=1, source_target_pairs={{1,0},{2,1},{3,2},{4,3},{5,4},{6,5},{7,6},{8,7},{9,8},{10,9},{11,1... | collective-permute-start | bytes 786440 | tf_op jit(solution)/shard_map/ppermute | solution.py:17
  50.6 2.6 %collective-permute-start = (bf16[512,256]{1,0:T(8,128)(2,1)S(1)}, bf16[512,256]{1,0:T(8,128)(2,1)S(1)}, u32[]{:S(2)}, u32[]{:S(2)}) collective-permute-start(bf16[512,256]{1,0:T(8,128)(2,1)S(1)} %convolution_convert_fusion.2), channel_id=1, source_target_pairs={{0,1},{1,2},{2,3},{3,4},{4,5},{5,6},{6,7},{7,8},{8,9},{9,10},{10,1... | collective-permute-start | bytes 786440 | tf_op jit(solution)/shard_map/ppermute | solution.py:14
  53.2 2.0 %collective-permute-done.1 = bf16[512,256]{1,0:T(8,128)(2,1)S(1)} collective-permute-done((bf16[512,256]{1,0:T(8,128)(2,1)S(1)}, bf16[512,256]{1,0:T(8,128)(2,1)S(1)}, u32[]{:S(2)}, u32[]{:S(2)}) %collective-permute-start.1) | collective-permute-done | bytes 262176 | tf_op jit(solution)/shard_map/ppermute | solution.py:17
  55.3 1.2 %collective-permute-done = bf16[512,256]{1,0:T(8,128)(2,1)S(1)} collective-permute-done((bf16[512,256]{1,0:T(8,128)(2,1)S(1)}, bf16[512,256]{1,0:T(8,128)(2,1)S(1)}, u32[]{:S(2)}, u32[]{:S(2)}) %collective-permute-start) | collective-permute-done | bytes 262176 | tf_op jit(solution)/shard_map/ppermute | solution.py:14
  56.5 0.6 gather_fusion
  57.8 1.9 %collective-permute-start.3 = (bf16[512,256]{1,0:T(8,128)(2,1)S(1)}, bf16[512,256]{1,0:T(8,128)(2,1)S(1)}, u32[]{:S(2)}, u32[]{:S(2)}) collective-permute-start(bf16[512,256]{1,0:T(8,128)(2,1)S(1)} %convolution_convert_fusion.1), channel_id=1, source_target_pairs={{1,0},{2,1},{3,2},{4,3},{5,4},{6,5},{7,6},{8,7},{9,8},{10,9},{11,1... | collective-permute-start | bytes 786440 | tf_op jit(solution)/shard_map/ppermute | solution.py:17
  59.8 4.4 %collective-permute-start.2 = (bf16[512,256]{1,0:T(8,128)(2,1)S(1)}, bf16[512,256]{1,0:T(8,128)(2,1)S(1)}, u32[]{:S(2)}, u32[]{:S(2)}) collective-permute-start(bf16[512,256]{1,0:T(8,128)(2,1)S(1)} %convolution_convert_fusion.1), channel_id=1, source_target_pairs={{0,1},{1,2},{2,3},{3,4},{4,5},{5,6},{6,7},{7,8},{8,9},{9,10},{10,1... | collective-permute-start | bytes 786440 | tf_op jit(solution)/shard_map/ppermute | solution.py:14
  64.2 2.1 %collective-permute-done.3 = bf16[512,256]{1,0:T(8,128)(2,1)S(1)} collective-permute-done((bf16[512,256]{1,0:T(8,128)(2,1)S(1)}, bf16[512,256]{1,0:T(8,128)(2,1)S(1)}, u32[]{:S(2)}, u32[]{:S(2)}) %collective-permute-start.3) | collective-permute-done | bytes 262176 | tf_op jit(solution)/shard_map/ppermute | solution.py:17
  66.3 1.2 %collective-permute-done.2 = bf16[512,256]{1,0:T(8,128)(2,1)S(1)} collective-permute-done((bf16[512,256]{1,0:T(8,128)(2,1)S(1)}, bf16[512,256]{1,0:T(8,128)(2,1)S(1)}, u32[]{:S(2)}, u32[]{:S(2)}) %collective-permute-start.2) | collective-permute-done | bytes 262176 | tf_op jit(solution)/shard_map/ppermute | solution.py:14
  67.5 0.6 gather_fusion.1
  68.9 0.8 reshape.82
  69.7 13.6 %all-to-all-start.1 = ((bf16[128,4,256]{2,1,0:T(4,128)(2,1)}), bf16[128,4,256]{2,1,0:T(4,128)(2,1)S(1)}, u32[]{:S(2)}, u32[]{:S(2)}) async-start(bf16[128,4,256]{2,1,0:T(4,128)(2,1)} %reshape.82), calls=%async_computation.1 | async-start | bytes 524288 | tf_op jit(solution)/shard_map/all_to_all | solution.py:109
  83.3 9.5 %convolution_add_fusion = f32[8192,256]{1,0:T(8,128)} fusion(bf16[512,256]{1,0:T(8,128)(2,1)S(1)} %bitcast.61, s32[8192]{0:T(1024)S(1)} %get-tuple-element.26, bf16[8192,256]{1,0:T(8,128)(2,1)} %param.7, pred[8192]{0:T(1024)(128)(4,1)S(1)} %broadcast_compare_fusion.1), kind=kOutput, calls=%fused_computation.12 | convolution fusion | flops 2164260864 | bytes 12886016 | tf_op jit(solution)/shard_map/dot_general | solution.py:114
  92.8 1.3 %all-to-all-done.1 = bf16[128,4,256]{2,1,0:T(4,128)(2,1)S(1)} async-done(((bf16[128,4,256]{2,1,0:T(4,128)(2,1)}), bf16[128,4,256]{2,1,0:T(4,128)(2,1)S(1)}, u32[]{:S(2)}, u32[]{:S(2)}) %all-to-all-start.1) | async-done | bytes 262176 | tf_op jit(solution)/shard_map/all_to_all | solution.py:109
  94.2 7.6 %fusion.7 = bf16[8192,256]{1,0:T(8,128)(2,1)} fusion(f32[8192,256]{1,0:T(8,128)} %convolution_add_fusion, bf16[512,256]{1,0:T(8,128)(2,1)S(1)} %reshape.83, s32[8192]{0:T(1024)S(1)} %add_select_fusion.1), kind=kOutput, calls=%fused_computation.11 | convolution fusion | flops 2155872256 | bytes 12877824 | tf_op jit(solution)/shard_map/dot_general | solution.py:115
  (47 shorter events, 4.5 us)
Async XLA Ops:
  0.0 47.3 %copy-start = (bf16[256,256]{1,0:T(8,128)(2,1)S(1)}, bf16[256,256]{1,0:T(8,128)(2,1)}, u32[]{:S(2)}) copy-start(bf16[256,256]{1,0:T(8,128)(2,1)} %param.12) | copy-start | bytes 393220
  4.6 4.9 %copy-start.1 = (s32[8192]{0:T(1024)S(1)}, s32[8192]{0:T(1024)}, u32[]{:S(2)}) copy-start(s32[8192]{0:T(1024)} %param.8) | copy-start | bytes 98308
  19.7 25.7 %all-to-all-start = ((f32[128,1,1152]{2,1,0:T(1,128)}), f32[128,1,1152]{2,1,0:T(1,128)S(1)}, u32[]{:S(2)}, u32[]{:S(2)}) async-start(f32[128,1,1152]{2,1,0:T(1,128)} %reshape.77), calls=%async_computation | async-start | bytes 1179648 | tf_op jit(solution)/shard_map/all_to_all | solution.py:83
  31.2 6.8 %copy-start.3 = (s32[4,6]{1,0:T(4,128)S(1)}, s32[4,6]{1,0:T(4,128)}, u32[]{:S(2)}) copy-start(s32[4,6]{1,0:T(4,128)} %param.9) | copy-start | bytes 292
  38.1 15.1 %copy-start.5 = (s32[4]{0:T(128)S(1)}, s32[4]{0:T(128)}, u32[]{:S(2)}) copy-start(s32[4]{0:T(128)} %param.10) | copy-start | bytes 52
  45.7 11.4 %copy-start.4 = (bf16[4,6,128,128]{3,2,1,0:T(8,128)(2,1)S(1)}, bf16[4,6,128,128]{3,2,1,0:T(8,128)(2,1)}, u32[]{:S(2)}) copy-start(bf16[4,6,128,128]{3,2,1,0:T(8,128)(2,1)} %param.11) | copy-start | bytes 2359300
  47.3 10.3 %copy-start.2 = (bf16[256,256]{1,0:T(8,128)(2,1)S(1)}, bf16[256,256]{1,0:T(8,128)(2,1)}, u32[]{:S(2)}) copy-start(bf16[256,256]{1,0:T(8,128)(2,1)} %param.13) | copy-start | bytes 393220
  47.6 7.7 %collective-permute-start.1 = (bf16[512,256]{1,0:T(8,128)(2,1)S(1)}, bf16[512,256]{1,0:T(8,128)(2,1)S(1)}, u32[]{:S(2)}, u32[]{:S(2)}) collective-permute-start(bf16[512,256]{1,0:T(8,128)(2,1)S(1)} %convolution_convert_fusion.2), channel_id=1, source_target_pairs={{1,0},{2,1},{3,2},{4,3},{5,4},{6,5},{7,6},{8,7},{9,8},{10,9},{11,1... | collective-permute-start | bytes 786440 | tf_op jit(solution)/shard_map/ppermute | solution.py:17
  50.6 5.9 %collective-permute-start = (bf16[512,256]{1,0:T(8,128)(2,1)S(1)}, bf16[512,256]{1,0:T(8,128)(2,1)S(1)}, u32[]{:S(2)}, u32[]{:S(2)}) collective-permute-start(bf16[512,256]{1,0:T(8,128)(2,1)S(1)} %convolution_convert_fusion.2), channel_id=1, source_target_pairs={{0,1},{1,2},{2,3},{3,4},{4,5},{5,6},{6,7},{7,8},{8,9},{9,10},{10,1... | collective-permute-start | bytes 786440 | tf_op jit(solution)/shard_map/ppermute | solution.py:14
  57.8 8.4 %collective-permute-start.3 = (bf16[512,256]{1,0:T(8,128)(2,1)S(1)}, bf16[512,256]{1,0:T(8,128)(2,1)S(1)}, u32[]{:S(2)}, u32[]{:S(2)}) collective-permute-start(bf16[512,256]{1,0:T(8,128)(2,1)S(1)} %convolution_convert_fusion.1), channel_id=1, source_target_pairs={{1,0},{2,1},{3,2},{4,3},{5,4},{6,5},{7,6},{8,7},{9,8},{10,9},{11,1... | collective-permute-start | bytes 786440 | tf_op jit(solution)/shard_map/ppermute | solution.py:17
  59.8 7.7 %collective-permute-start.2 = (bf16[512,256]{1,0:T(8,128)(2,1)S(1)}, bf16[512,256]{1,0:T(8,128)(2,1)S(1)}, u32[]{:S(2)}, u32[]{:S(2)}) collective-permute-start(bf16[512,256]{1,0:T(8,128)(2,1)S(1)} %convolution_convert_fusion.1), channel_id=1, source_target_pairs={{0,1},{1,2},{2,3},{3,4},{4,5},{5,6},{6,7},{7,8},{8,9},{9,10},{10,1... | collective-permute-start | bytes 786440 | tf_op jit(solution)/shard_map/ppermute | solution.py:14
  69.7 24.4 %all-to-all-start.1 = ((bf16[128,4,256]{2,1,0:T(4,128)(2,1)}), bf16[128,4,256]{2,1,0:T(4,128)(2,1)S(1)}, u32[]{:S(2)}, u32[]{:S(2)}) async-start(bf16[128,4,256]{2,1,0:T(4,128)(2,1)} %reshape.82), calls=%async_computation.1 | async-start | bytes 524288 | tf_op jit(solution)/shard_map/all_to_all | solution.py:109

commit v4 on v3

--- a/solution.py
+++ b/solution.py
@@ -39,9 +39,7 @@
     lanes = jnp.arange(clusters_here, dtype=jnp.int32)
     before = (lanes[:, None] < lanes[None, :]).astype(jnp.bfloat16)
     rank = jnp.dot(named, before, preferred_element_type=jnp.float32)
-    per_owner = jnp.dot(lid_hot, rank.T.astype(jnp.bfloat16), preferred_element_type=jnp.float32)
-    slot = jnp.sum(per_owner * owner_hot.astype(jnp.float32), axis=1).astype(jnp.int32)
-    return presence, rank, slot
+    return presence, rank
 
 
 def local(features, cluster_ids, tile_cols, tile_counts, adjacency, w_first, w_second):
@@ -56,16 +54,9 @@
     here = jnp.arange(clusters_here, dtype=jnp.int32)
     owner_hot = (owners[:, None] == peers[None, :]).astype(jnp.bfloat16)
     lid_hot = (lids[:, None] == here[None, :]).astype(jnp.bfloat16)
-    presence, rank, slot = distinct_slots(owner_hot, lid_hot, clusters_here)
+    presence, rank = distinct_slots(owner_hot, lid_hot, clusters_here)
     remote_slots = device_count * DCAP
-    slot_column = jnp.where(remote, owners * DCAP + slot, -1)
-    slot_range = jnp.arange(remote_slots, dtype=jnp.int32)
-    remote_hot = (slot_column[:, None] == slot_range[None, :]).astype(jnp.bfloat16)
-    local_hot = jnp.where(remote[:, None], jnp.zeros((), jnp.bfloat16), lid_hot)
     contract_rows = (((0,), (0,)), ((), ()))
-    remote_sums = lax.dot_general(
-        remote_hot, features, contract_rows, preferred_element_type=jnp.float32
-    )
 
     named = (presence > 0) & (peers != myself)[:, None]
     slot_counts = []
@@ -73,19 +64,36 @@
     for k in range(DCAP):
         chosen = named & (rank == k)
         slot_counts.append(jnp.sum(jnp.where(chosen, presence, 0.0), axis=1))
-        slot_ids.append(jnp.sum(jnp.where(chosen, here[None, :], 0), axis=1))
+        found = jnp.sum(jnp.where(chosen, here[None, :], 0), axis=1)
+        slot_ids.append(jnp.where(jnp.any(chosen, axis=1), found, clusters_here))
     slot_counts = jnp.stack(slot_counts, axis=1)
-    slot_ids = jnp.stack(slot_ids, axis=1).astype(jnp.float32)
+    slot_ids = jnp.stack(slot_ids, axis=1)
+    split = jnp.concatenate([slot_ids // 32, slot_ids % 32], axis=1).astype(jnp.bfloat16)
+    parts = jnp.dot(owner_hot, split, preferred_element_type=jnp.float32).astype(jnp.int32)
+    lows = parts[:, :DCAP] * 32 + parts[:, DCAP:]
+    slot = jnp.sum((lids[:, None] >= lows[:, 1:]).astype(jnp.int32), axis=1)
+    slot = jnp.where(remote, slot, -1)
+    masked = jnp.concatenate(
+        [jnp.where((slot == k)[:, None], features, jnp.zeros((), features.dtype)) for k in range(DCAP)],
+        axis=1,
+    )
+    remote_sums = lax.dot_general(owner_hot, masked, contract_rows, preferred_element_type=jnp.float32)
     meta = jnp.concatenate(
-        [slot_counts, slot_ids, jnp.zeros((device_count, 128 - 2 * DCAP), jnp.float32)], axis=1
+        [slot_counts, jnp.where(slot_ids < clusters_here, slot_ids, 0).astype(jnp.float32),
+         jnp.zeros((device_count, 128 - 2 * DCAP), jnp.float32)],
+        axis=1,
     )
-    payload = jnp.concatenate([remote_sums.reshape(device_count, DCAP * width), meta], axis=1)
+    payload = jnp.concatenate([remote_sums, meta], axis=1)
     got = lax.all_to_all(
         payload.reshape(device_count, 1, -1), "nodes", split_axis=0, concat_axis=0, tiled=True
     ).reshape(device_count, -1)
     got_sums = got[:, : DCAP * width].reshape(remote_slots, width)
     got_counts = got[:, DCAP * width : DCAP * width + DCAP].reshape(remote_slots)
     got_ids = got[:, DCAP * width + DCAP : DCAP * width + 2 * DCAP].reshape(remote_slots).astype(jnp.int32)
+    local_hot = jnp.where(remote[:, None], jnp.zeros((), jnp.bfloat16), lid_hot)
+    slot_column = jnp.where(remote, owners * DCAP + slot, -1)
+    slot_range = jnp.arange(remote_slots, dtype=jnp.int32)
+    remote_hot = (slot_column[:, None] == slot_range[None, :]).astype(jnp.bfloat16)
     local_sums = lax.dot_general(
         local_hot, features, contract_rows, preferred_element_type=jnp.float32
     )
@@ -109,11 +117,10 @@
     returned = lax.all_to_all(
         answers.reshape(device_count, DCAP, width), "nodes", split_axis=0, concat_axis=0, tiled=True
     ).reshape(remote_slots, width)
-    value = (
-        features.astype(jnp.float32)
-        + jnp.dot(local_hot, coarse, preferred_element_type=jnp.float32)
-        + jnp.dot(remote_hot, returned, preferred_element_type=jnp.float32)
-    )
+    first = (
+        features.astype(jnp.float32) + jnp.dot(local_hot, coarse, preferred_element_type=jnp.float32)
+    ).astype(jnp.bfloat16)
+    value = first.astype(jnp.float32) + jnp.dot(remote_hot, returned, preferred_element_type=jnp.float32)
     return value.astype(jnp.bfloat16)
 
 

time: 102 us -> 119 us (1.17)
  other arithmetic: 1.61 us -> 11.4 us
  waiting for transfers between devices: 15 us -> 19.5 us
  matrix products: 43.1 us -> 46.2 us
    select_n x0 -> x5, other arithmetic: none -> 9.15 us  [the longest x1 9.13 us: local(): jnp.where((slot == k)[:, None], features, jnp.zeros((), features.dtype))]
    ppermute x2, waiting for transfers between devices: 4.13 us -> 8.79 us  [with_halo(): lax.ppermute(lax.slice_in_dim(block, 0, width, axis=dim), axis, backward)]
    all_to_all x1, starting transfers between devices: 13.6 us -> 15.8 us  [local(): lax.all_to_all(answers.reshape(device_count, DCAP, width), 'nodes', split...]
    ppermute x2, starting transfers between devices: 6.94 us -> 4.94 us  [with_halo(): lax.ppermute(lax.slice_in_dim(block, block.shape[dim] - width, None, axis...]
    dot_general x2, matrix products: 12.7 us -> 14.6 us  [the longest x1 13.3 us: local(): lax.dot_general(owner_hot, masked, contract_rows, preferred_element_type=...]
  transfers between devices with their start and end apart: 6 -> 6, of which waited for: 6 -> 6; matrix products, arithmetic and copies ran while one was open for 16% -> 14% of each run, Pallas kernels for 0% -> 0%
where the time goes in v4:
time: 119 us
  matrix products  46.2 us (39%)
  starting transfers between devices  36.6 us (31%)
  waiting for transfers between devices  19.5 us (16%)
  other arithmetic  11.4 us (10%)
  local copies, waits for them, and re-layouts  4.9 us (4%)
    all_to_all x1, starting transfers between devices, local(): lax.all_to_all(answers.reshape(device_count, DCAP, width), 'nodes', split...  15.8 us
    dot_general x1, matrix products, local(): lax.dot_general(owner_hot, masked, contract_rows, preferred_element_type=...  13.3 us
    all_to_all x1, starting transfers between devices, local(): lax.all_to_all(payload.reshape(device_count, 1, -1), 'nodes', split_axis=...  11.5 us
    dot_general x1, matrix products, local(): jnp.dot(local_hot, coarse, preferred_element_type=jnp.float32)  9.47 us
    select_n x1, other arithmetic, local(): jnp.where((slot == k)[:, None], features, jnp.zeros((), features.dtype))  9.13 us
    ppermute x2, waiting for transfers between devices, with_halo(): lax.ppermute(lax.slice_in_dim(block, 0, width, axis=dim), axis, backward)  8.79 us
    dot_general x1, matrix products, local(): jnp.dot(remote_hot, returned, preferred_element_type=jnp.float32)  7.61 us
    all_to_all x1, waiting for transfers between devices, local(): lax.all_to_all(payload.reshape(device_count, 1, -1), 'nodes', split_axis=...  7.23 us
  transfers between devices with their start and end apart: 6, of which 6 were waited for; matrix products, arithmetic and copies ran while one was open for 14% of the time, Pallas kernels for 0%

profile of v4, /device:TPU:1, one launch (start us, length us, event | category | flops | bytes accessed | tf_op | source)
XLA Modules:
  0.0 119.0 jit_solution(13133389448916662652)
XLA Ops:
  0.0 0.8 add_select_fusion
  0.8 4.3 %broadcast_compare_fusion = (pred[128,512]{1,0:T(32,128)(4,1)S(1)}, f32[128,512]{1,0:T(8,128)S(1)}) fusion(s32[8192]{0:T(1024)S(1)} %get-tuple-element.28, s32[8192]{0:T(1024)S(1)} %get-tuple-element.27), kind=kOutput, calls=%fused_computation.79 | convolution fusion | flops 1079050240 | bytes 393216 | tf_op jit(solution)/shard_map/dot_general | solution.py:37
  6.6 1.3 %convolution_convert_fusion = s32[8192,8]{0,1:T(8,128)S(1)} fusion(s32[8192]{0:T(1024)S(1)} %get-tuple-element.27, bf16[128,4]{0,1:T(4,128)(2,1)S(1)} %get-tuple-element.30, bf16[128,4]{0,1:T(4,128)(2,1)S(1)} %get-tuple-element.31), kind=kOutput, calls=%fused_computation.20 | convolution fusion | flops 17895424 | bytes 296960 | tf_op jit(solution)/shard_map/dot_general | solution.py:72
  8.7 9.1 %broadcast_select_fusion.3 = (bf16[8192,256]{1,0:T(8,128)(2,1)S(1)}, bf16[8192,256]{1,0:T(8,128)(2,1)S(1)}, bf16[8192,256]{1,0:T(8,128)(2,1)S(1)}, bf16[8192,256]{1,0:T(8,128)(2,1)S(1)}) fusion(bf16[8192,256]{1,0:T(8,128)(2,1)} %param.7, pred[8192]{0:T(1024)(128)(4,1)S(1)} %get-tuple-element.23, pred[8192]{0:T(1024)(128)(4,1)S(1)} %get-tuple-element.26, ...), kind=kLoop, calls=%fused_computation.35 | loop fusion | flops 8388608 | bytes 21004288 | tf_op jit(solution)/shard_map/jit(_where)/select_n | solution.py:77
  17.9 13.3 %fusion = f32[128,1024]{1,0:T(8,128)S(1)} fusion(bf16[8192,256]{1,0:T(8,128)(2,1)S(1)} %get-tuple-element.17, bf16[8192,256]{1,0:T(8,128)(2,1)S(1)} %get-tuple-element.18, bf16[8192,256]{1,0:T(8,128)(2,1)S(1)} %get-tuple-element.16, bf16[8192,256]{1,0:T(8,128)(2,1)S(1)} %get-tuple-element.15, s32[8192]{0:T(1024)S(1)} %get-tuple-element.27), kind=kOutput, calls=%fused_computation.2 | convolution fusion | flops 2215641088 | bytes 17334272 | tf_op jit(solution)/shard_map/dot_general | solution.py:80
  31.4 1.4 %copy.57 = f32[128,1,1152]{2,1,0:T(1,128)} copy(f32[128,1,1152]{2,0,1:T(8,128)S(1)} %bitcast.51) | data formatting | bytes 1179648 | tf_op jit(solution)/shard_map/reshape | solution.py:88
  32.8 11.5 %all-to-all-start = ((f32[128,1,1152]{2,1,0:T(1,128)}), f32[128,1,1152]{2,1,0:T(1,128)S(1)}, u32[]{:S(2)}, u32[]{:S(2)}) async-start(f32[128,1,1152]{2,1,0:T(1,128)} %copy.57), calls=%async_computation | async-start | bytes 1179648 | tf_op jit(solution)/shard_map/all_to_all | solution.py:87
  44.3 6.8 %fusion.17 = f32[512,256]{1,0:T(8,128)S(1)} fusion(bf16[8192,256]{1,0:T(8,128)(2,1)} %param.7, s32[8192]{0:T(1024)S(1)} %get-tuple-element.28, pred[8192]{0:T(1024)(128)(4,1)S(1)} %get-tuple-element.10), kind=kOutput, calls=%fused_computation.22 | convolution fusion | flops 2160066560 | bytes 4759552 | tf_op jit(solution)/shard_map/dot_general | solution.py:97
  51.3 7.2 %all-to-all-done = f32[128,1,1152]{2,1,0:T(1,128)S(1)} async-done(((f32[128,1,1152]{2,1,0:T(1,128)}), f32[128,1,1152]{2,1,0:T(1,128)S(1)}, u32[]{:S(2)}, u32[]{:S(2)}) %all-to-all-start) | async-done | bytes 589856 | tf_op jit(solution)/shard_map/all_to_all | solution.py:87
  59.3 1.1 fusion.32
  60.7 3.0 %collective-permute-start = (bf16[512,256]{1,0:T(8,128)(2,1)S(1)}, bf16[512,256]{1,0:T(8,128)(2,1)S(1)}, u32[]{:S(2)}, u32[]{:S(2)}) collective-permute-start(bf16[512,256]{1,0:T(8,128)(2,1)S(1)} %convolution_convert_fusion.3), channel_id=1, source_target_pairs={{0,1},{1,2},{2,3},{3,4},{4,5},{5,6},{6,7},{7,8},{8,9},{9,10},{10,1... | collective-permute-start | bytes 786440 | tf_op jit(solution)/shard_map/ppermute | solution.py:14
  63.7 1.9 %collective-permute-start.1 = (bf16[512,256]{1,0:T(8,128)(2,1)S(1)}, bf16[512,256]{1,0:T(8,128)(2,1)S(1)}, u32[]{:S(2)}, u32[]{:S(2)}) collective-permute-start(bf16[512,256]{1,0:T(8,128)(2,1)S(1)} %convolution_convert_fusion.3), channel_id=1, source_target_pairs={{1,0},{2,1},{3,2},{4,3},{5,4},{6,5},{7,6},{8,7},{9,8},{10,9},{11,1... | collective-permute-start | bytes 786440 | tf_op jit(solution)/shard_map/ppermute | solution.py:17
  65.7 1.3 %collective-permute-done = bf16[512,256]{1,0:T(8,128)(2,1)S(1)} collective-permute-done((bf16[512,256]{1,0:T(8,128)(2,1)S(1)}, bf16[512,256]{1,0:T(8,128)(2,1)S(1)}, u32[]{:S(2)}, u32[]{:S(2)}) %collective-permute-start) | collective-permute-done | bytes 262176 | tf_op jit(solution)/shard_map/ppermute | solution.py:14
  67.0 4.4 %collective-permute-done.1 = bf16[512,256]{1,0:T(8,128)(2,1)S(1)} collective-permute-done((bf16[512,256]{1,0:T(8,128)(2,1)S(1)}, bf16[512,256]{1,0:T(8,128)(2,1)S(1)}, u32[]{:S(2)}, u32[]{:S(2)}) %collective-permute-start.1) | collective-permute-done | bytes 262176 | tf_op jit(solution)/shard_map/ppermute | solution.py:17
  72.8 1.9 %collective-permute-start.2 = (bf16[512,256]{1,0:T(8,128)(2,1)S(1)}, bf16[512,256]{1,0:T(8,128)(2,1)S(1)}, u32[]{:S(2)}, u32[]{:S(2)}) collective-permute-start(bf16[512,256]{1,0:T(8,128)(2,1)S(1)} %convolution_convert_fusion.2), channel_id=1, source_target_pairs={{0,1},{1,2},{2,3},{3,4},{4,5},{5,6},{6,7},{7,8},{8,9},{9,10},{10,1... | collective-permute-start | bytes 786440 | tf_op jit(solution)/shard_map/ppermute | solution.py:14
  74.7 2.4 %collective-permute-start.3 = (bf16[512,256]{1,0:T(8,128)(2,1)S(1)}, bf16[512,256]{1,0:T(8,128)(2,1)S(1)}, u32[]{:S(2)}, u32[]{:S(2)}) collective-permute-start(bf16[512,256]{1,0:T(8,128)(2,1)S(1)} %convolution_convert_fusion.2), channel_id=1, source_target_pairs={{1,0},{2,1},{3,2},{4,3},{5,4},{6,5},{7,6},{8,7},{9,8},{10,9},{11,1... | collective-permute-start | bytes 786440 | tf_op jit(solution)/shard_map/ppermute | solution.py:17
  77.2 0.9 collective-permute-done.2
  78.0 4.4 %collective-permute-done.3 = bf16[512,256]{1,0:T(8,128)(2,1)S(1)} collective-permute-done((bf16[512,256]{1,0:T(8,128)(2,1)S(1)}, bf16[512,256]{1,0:T(8,128)(2,1)S(1)}, u32[]{:S(2)}, u32[]{:S(2)}) %collective-permute-start.3) | collective-permute-done | bytes 262176 | tf_op jit(solution)/shard_map/ppermute | solution.py:17
  82.5 0.6 gather_fusion.1
  83.9 0.8 reshape.134
  84.7 15.8 %all-to-all-start.1 = ((bf16[128,4,256]{2,1,0:T(4,128)(2,1)}), bf16[128,4,256]{2,1,0:T(4,128)(2,1)S(1)}, u32[]{:S(2)}, u32[]{:S(2)}) async-start(bf16[128,4,256]{2,1,0:T(4,128)(2,1)} %reshape.134), calls=%async_computation.1 | async-start | bytes 524288 | tf_op jit(solution)/shard_map/all_to_all | solution.py:117
  100.5 9.5 %fusion.14 = f32[8192,256]{1,0:T(8,128)} fusion(bf16[512,256]{1,0:T(8,128)(2,1)S(1)} %bitcast.61, s32[8192]{0:T(1024)S(1)} %get-tuple-element.28, bf16[8192,256]{1,0:T(8,128)(2,1)} %param.7, pred[8192]{0:T(1024)(128)(4,1)S(1)} %get-tuple-element.10), kind=kOutput, calls=%fused_computation.19 | convolution fusion | flops 2168455168 | bytes 12886016 | tf_op jit(solution)/shard_map/dot_general | solution.py:121
  110.0 1.3 %all-to-all-done.1 = bf16[128,4,256]{2,1,0:T(4,128)(2,1)S(1)} async-done(((bf16[128,4,256]{2,1,0:T(4,128)(2,1)}), bf16[128,4,256]{2,1,0:T(4,128)(2,1)S(1)}, u32[]{:S(2)}, u32[]{:S(2)}) %all-to-all-start.1) | async-done | bytes 262176 | tf_op jit(solution)/shard_map/all_to_all | solution.py:117
  111.4 7.6 %fusion.12 = bf16[8192,256]{1,0:T(8,128)(2,1)} fusion(f32[8192,256]{1,0:T(8,128)} %fusion.14, bf16[512,256]{1,0:T(8,128)(2,1)S(1)} %reshape.135, s32[8192]{0:T(1024)S(1)} %get-tuple-element.9), kind=kOutput, calls=%fused_computation.16 | convolution fusion | flops 2155872256 | bytes 12877824 | tf_op jit(solution)/shard_map/dot_general | solution.py:123
  (58 shorter events, 5.8 us)
Async XLA Ops:
  0.0 60.4 %copy-start = (bf16[256,256]{1,0:T(8,128)(2,1)S(1)}, bf16[256,256]{1,0:T(8,128)(2,1)}, u32[]{:S(2)}) copy-start(bf16[256,256]{1,0:T(8,128)(2,1)} %param.12) | copy-start | bytes 393220
  5.2 2.9 %copy-start.2 = (s32[8192]{0:T(1024)S(1)}, s32[8192]{0:T(1024)}, u32[]{:S(2)}) copy-start(s32[8192]{0:T(1024)} %param.8) | copy-start | bytes 98308
  32.8 25.7 %all-to-all-start = ((f32[128,1,1152]{2,1,0:T(1,128)}), f32[128,1,1152]{2,1,0:T(1,128)S(1)}, u32[]{:S(2)}, u32[]{:S(2)}) async-start(f32[128,1,1152]{2,1,0:T(1,128)} %copy.57), calls=%async_computation | async-start | bytes 1179648 | tf_op jit(solution)/shard_map/all_to_all | solution.py:87
  44.3 6.8 %copy-start.3 = (s32[4,6]{1,0:T(4,128)S(1)}, s32[4,6]{1,0:T(4,128)}, u32[]{:S(2)}) copy-start(s32[4,6]{1,0:T(4,128)} %param.9) | copy-start | bytes 292
  51.2 14.5 %copy-start.5 = (s32[4]{0:T(128)S(1)}, s32[4]{0:T(128)}, u32[]{:S(2)}) copy-start(s32[4]{0:T(128)} %param.10) | copy-start | bytes 52
  59.1 13.0 %copy-start.4 = (bf16[4,6,128,128]{3,2,1,0:T(8,128)(2,1)S(1)}, bf16[4,6,128,128]{3,2,1,0:T(8,128)(2,1)}, u32[]{:S(2)}) copy-start(bf16[4,6,128,128]{3,2,1,0:T(8,128)(2,1)} %param.11) | copy-start | bytes 2359300
  60.4 12.1 %copy-start.1 = (bf16[256,256]{1,0:T(8,128)(2,1)S(1)}, bf16[256,256]{1,0:T(8,128)(2,1)}, u32[]{:S(2)}) copy-start(bf16[256,256]{1,0:T(8,128)(2,1)} %param.13) | copy-start | bytes 393220
  60.7 6.3 %collective-permute-start = (bf16[512,256]{1,0:T(8,128)(2,1)S(1)}, bf16[512,256]{1,0:T(8,128)(2,1)S(1)}, u32[]{:S(2)}, u32[]{:S(2)}) collective-permute-start(bf16[512,256]{1,0:T(8,128)(2,1)S(1)} %convolution_convert_fusion.3), channel_id=1, source_target_pairs={{0,1},{1,2},{2,3},{3,4},{4,5},{5,6},{6,7},{7,8},{8,9},{9,10},{10,1... | collective-permute-start | bytes 786440 | tf_op jit(solution)/shard_map/ppermute | solution.py:14
  63.7 7.7 %collective-permute-start.1 = (bf16[512,256]{1,0:T(8,128)(2,1)S(1)}, bf16[512,256]{1,0:T(8,128)(2,1)S(1)}, u32[]{:S(2)}, u32[]{:S(2)}) collective-permute-start(bf16[512,256]{1,0:T(8,128)(2,1)S(1)} %convolution_convert_fusion.3), channel_id=1, source_target_pairs={{1,0},{2,1},{3,2},{4,3},{5,4},{6,5},{7,6},{8,7},{9,8},{10,9},{11,1... | collective-permute-start | bytes 786440 | tf_op jit(solution)/shard_map/ppermute | solution.py:17
  72.8 5.2 %collective-permute-start.2 = (bf16[512,256]{1,0:T(8,128)(2,1)S(1)}, bf16[512,256]{1,0:T(8,128)(2,1)S(1)}, u32[]{:S(2)}, u32[]{:S(2)}) collective-permute-start(bf16[512,256]{1,0:T(8,128)(2,1)S(1)} %convolution_convert_fusion.2), channel_id=1, source_target_pairs={{0,1},{1,2},{2,3},{3,4},{4,5},{5,6},{6,7},{7,8},{8,9},{9,10},{10,1... | collective-permute-start | bytes 786440 | tf_op jit(solution)/shard_map/ppermute | solution.py:14
  74.7 7.7 %collective-permute-start.3 = (bf16[512,256]{1,0:T(8,128)(2,1)S(1)}, bf16[512,256]{1,0:T(8,128)(2,1)S(1)}, u32[]{:S(2)}, u32[]{:S(2)}) collective-permute-start(bf16[512,256]{1,0:T(8,128)(2,1)S(1)} %convolution_convert_fusion.2), channel_id=1, source_target_pairs={{1,0},{2,1},{3,2},{4,3},{5,4},{6,5},{7,6},{8,7},{9,8},{10,9},{11,1... | collective-permute-start | bytes 786440 | tf_op jit(solution)/shard_map/ppermute | solution.py:17
  84.7 26.7 %all-to-all-start.1 = ((bf16[128,4,256]{2,1,0:T(4,128)(2,1)}), bf16[128,4,256]{2,1,0:T(4,128)(2,1)S(1)}, u32[]{:S(2)}, u32[]{:S(2)}) async-start(bf16[128,4,256]{2,1,0:T(4,128)(2,1)} %reshape.134), calls=%async_computation.1 | async-start | bytes 524288 | tf_op jit(solution)/shard_map/all_to_all | solution.py:117

commit v5 on v4

--- a/solution.py
+++ b/solution.py
@@ -73,11 +73,11 @@
     lows = parts[:, :DCAP] * 32 + parts[:, DCAP:]
     slot = jnp.sum((lids[:, None] >= lows[:, 1:]).astype(jnp.int32), axis=1)
     slot = jnp.where(remote, slot, -1)
-    masked = jnp.concatenate(
-        [jnp.where((slot == k)[:, None], features, jnp.zeros((), features.dtype)) for k in range(DCAP)],
+    slot_hot = [jnp.where((slot == k)[:, None], owner_hot, jnp.zeros((), owner_hot.dtype)) for k in range(DCAP)]
+    remote_sums = jnp.concatenate(
+        [lax.dot_general(hot, features, contract_rows, preferred_element_type=jnp.float32) for hot in slot_hot],
         axis=1,
     )
-    remote_sums = lax.dot_general(owner_hot, masked, contract_rows, preferred_element_type=jnp.float32)
     meta = jnp.concatenate(
         [slot_counts, jnp.where(slot_ids < clusters_here, slot_ids, 0).astype(jnp.float32),
          jnp.zeros((device_count, 128 - 2 * DCAP), jnp.float32)],
@@ -91,9 +91,6 @@
     got_counts = got[:, DCAP * width : DCAP * width + DCAP].reshape(remote_slots)
     got_ids = got[:, DCAP * width + DCAP : DCAP * width + 2 * DCAP].reshape(remote_slots).astype(jnp.int32)
     local_hot = jnp.where(remote[:, None], jnp.zeros((), jnp.bfloat16), lid_hot)
-    slot_column = jnp.where(remote, owners * DCAP + slot, -1)
-    slot_range = jnp.arange(remote_slots, dtype=jnp.int32)
-    remote_hot = (slot_column[:, None] == slot_range[None, :]).astype(jnp.bfloat16)
     local_sums = lax.dot_general(
         local_hot, features, contract_rows, preferred_element_type=jnp.float32
     )
@@ -116,11 +113,13 @@
     ).astype(jnp.bfloat16)
     returned = lax.all_to_all(
         answers.reshape(device_count, DCAP, width), "nodes", split_axis=0, concat_axis=0, tiled=True
-    ).reshape(remote_slots, width)
+    )
     first = (
         features.astype(jnp.float32) + jnp.dot(local_hot, coarse, preferred_element_type=jnp.float32)
     ).astype(jnp.bfloat16)
-    value = first.astype(jnp.float32) + jnp.dot(remote_hot, returned, preferred_element_type=jnp.float32)
+    value = first.astype(jnp.float32)
+    for k in range(DCAP):
+        value = value + jnp.dot(slot_hot[k], returned[:, k, :], preferred_element_type=jnp.float32)
     return value.astype(jnp.bfloat16)
 
 

time: 119 us -> 124 us (1.042)
  matrix products: 46.2 us -> 63.2 us
  other arithmetic: 11.4 us -> 2.33 us
  waiting for transfers between devices: 19.5 us -> 15.1 us
    dot_general x2 -> x8, matrix products: 21 us -> 35.7 us  [the longest x4 18.8 us: local(): jnp.dot(slot_hot[k], returned[:, k, :], preferred_element_type=jnp.float32)]
    select_n x2 -> x0, other arithmetic: 9.16 us -> none  [the longest x1 9.13 us: local(): jnp.where((slot == k)[:, None], features, jnp.zeros((), features.dtype))]
    ppermute x2, waiting for transfers between devices: 8.79 us -> 4.13 us  [with_halo(): lax.ppermute(lax.slice_in_dim(block, 0, width, axis=dim), axis, backward)]
    dot_general x2, matrix products: 0.86 us -> 3.14 us  [convolve(): jnp.einsum('tkij,tkjf->tif', weights, picked, preferred_element_type=jnp....]
    all_to_all x1, starting transfers between devices: 15.8 us -> 13.6 us  [local(): lax.all_to_all(answers.reshape(device_count, DCAP, width), 'nodes', split...]
    ppermute x2, starting transfers between devices: 4.94 us -> 6.95 us  [with_halo(): lax.ppermute(lax.slice_in_dim(block, block.shape[dim] - width, None, axis...]
  transfers between devices with their start and end apart: 6 -> 6, of which waited for: 6 -> 6; matrix products, arithmetic and copies ran while one was open for 14% -> 13% of each run, Pallas kernels for 0% -> 0%
where the time goes in v5:
time: 124 us; the launch traced here: 123 us
  matrix products  63.2 us (51%)
  starting transfers between devices  37 us (30%)
  waiting for transfers between devices  15.1 us (12%)
  local copies, waits for them, and re-layouts  5.21 us (4%)
  other arithmetic  2.33 us (2%)
    dot_general x4, matrix products, local(): jnp.dot(slot_hot[k], returned[:, k, :], preferred_element_type=jnp.float32)  18.8 us
    dot_general x4, matrix products, local(): lax.dot_general(hot, features, contract_rows, preferred_element_type=jnp....  16.9 us
    all_to_all x1, starting transfers between devices, local(): lax.all_to_all(answers.reshape(device_count, DCAP, width), 'nodes', split...  13.6 us
    all_to_all x1, starting transfers between devices, local(): lax.all_to_all(payload.reshape(device_count, 1, -1), 'nodes', split_axis=...  11.5 us
    dot_general x1, matrix products, local(): jnp.dot(local_hot, coarse, preferred_element_type=jnp.float32)  9.46 us
    all_to_all x1, waiting for transfers between devices, local(): lax.all_to_all(payload.reshape(device_count, 1, -1), 'nodes', split_axis=...  7.23 us
    ppermute x2, starting transfers between devices, with_halo(): lax.ppermute(lax.slice_in_dim(block, block.shape[dim] - width, None, axis...  6.95 us
    dot_general x1, matrix products, local(): lax.dot_general(local_hot, features, contract_rows, preferred_element_typ...  6.81 us
  transfers between devices with their start and end apart: 6, of which 6 were waited for; matrix products, arithmetic and copies ran while one was open for 13% of the time, Pallas kernels for 0%

profile of v5, /device:TPU:1, one launch (start us, length us, event | category | flops | bytes accessed | tf_op | source)
XLA Modules:
  0.0 123.1 jit_solution(7026578965112895923)
XLA Ops:
  0.8 4.3 %broadcast_compare_fusion = (pred[128,512]{1,0:T(32,128)(4,1)S(1)}, f32[128,512]{1,0:T(8,128)S(1)}) fusion(s32[8192]{0:T(1024)S(1)} %get-tuple-element.27, s32[8192]{0:T(1024)S(1)} %get-tuple-element.26), kind=kOutput, calls=%fused_computation.99 | convolution fusion | flops 1079050240 | bytes 393216 | tf_op jit(solution)/shard_map/dot_general | solution.py:37
  8.7 7.6 %fusion.28 = f32[128,256]{1,0:T(8,128)S(1)} fusion(bf16[8192,256]{1,0:T(8,128)(2,1)} %param.7, s32[8192]{0:T(1024)S(1)} %get-tuple-element.26, pred[8192]{0:T(1024)(128)(4,1)S(1)} %get-tuple-element.23), kind=kOutput, calls=%fused_computation.31 | convolution fusion | flops 540016640 | bytes 4366336 | tf_op jit(solution)/shard_map/dot_general | solution.py:78
  16.3 3.1 %fusion.25 = f32[128,256]{1,0:T(8,128)S(1)} fusion(bf16[8192,256]{1,0:T(8,128)(2,1)S(1)} %copy-done.4, s32[8192]{0:T(1024)S(1)} %get-tuple-element.26, pred[8192]{0:T(1024)(128)(4,1)S(1)} %get-tuple-element.24), kind=kOutput, calls=%fused_computation.30 | convolution fusion | flops 540016640 | bytes 4366336 | tf_op jit(solution)/shard_map/dot_general | solution.py:78
  19.4 3.1 %fusion.22 = f32[128,256]{1,0:T(8,128)S(1)} fusion(bf16[8192,256]{1,0:T(8,128)(2,1)S(1)} %copy-done.4, s32[8192]{0:T(1024)S(1)} %get-tuple-element.26, pred[8192]{0:T(1024)(128)(4,1)S(1)} %get-tuple-element.25), kind=kOutput, calls=%fused_computation.29 | convolution fusion | flops 540016640 | bytes 4366336 | tf_op jit(solution)/shard_map/dot_general | solution.py:78
  22.5 3.1 %fusion.31 = f32[128,256]{1,0:T(8,128)S(1)} fusion(bf16[8192,256]{1,0:T(8,128)(2,1)S(1)} %copy-done.4, s32[8192]{0:T(1024)S(1)} %get-tuple-element.26, pred[8192]{0:T(1024)(128)(4,1)S(1)} %get-tuple-element.13), kind=kOutput, calls=%fused_computation.32 | convolution fusion | flops 540016640 | bytes 4366336 | tf_op jit(solution)/shard_map/dot_general | solution.py:78
  25.8 1.4 %copy.66 = f32[128,1,1152]{2,1,0:T(1,128)} copy(f32[128,1,1152]{2,0,1:T(8,128)S(1)} %bitcast.66) | data formatting | bytes 1179648 | tf_op jit(solution)/shard_map/reshape | solution.py:88
  27.3 11.5 %all-to-all-start = ((f32[128,1,1152]{2,1,0:T(1,128)}), f32[128,1,1152]{2,1,0:T(1,128)S(1)}, u32[]{:S(2)}, u32[]{:S(2)}) async-start(f32[128,1,1152]{2,1,0:T(1,128)} %copy.66), calls=%async_computation | async-start | bytes 1179648 | tf_op jit(solution)/shard_map/all_to_all | solution.py:87
  38.8 6.8 %fusion.7 = f32[512,256]{1,0:T(8,128)S(1)} fusion(bf16[8192,256]{1,0:T(8,128)(2,1)} %param.7, s32[8192]{0:T(1024)S(1)} %get-tuple-element.27, pred[8192]{0:T(1024)(128)(4,1)S(1)} %get-tuple-element.14), kind=kOutput, calls=%fused_computation.15 | convolution fusion | flops 2160066560 | bytes 4759552 | tf_op jit(solution)/shard_map/dot_general | solution.py:94
  45.7 7.2 %all-to-all-done = f32[128,1,1152]{2,1,0:T(1,128)S(1)} async-done(((f32[128,1,1152]{2,1,0:T(1,128)}), f32[128,1,1152]{2,1,0:T(1,128)S(1)}, u32[]{:S(2)}, u32[]{:S(2)}) %all-to-all-start) | async-done | bytes 589856 | tf_op jit(solution)/shard_map/all_to_all | solution.py:87
  55.1 3.0 %collective-permute-start.1 = (bf16[512,256]{1,0:T(8,128)(2,1)S(1)}, bf16[512,256]{1,0:T(8,128)(2,1)S(1)}, u32[]{:S(2)}, u32[]{:S(2)}) collective-permute-start(bf16[512,256]{1,0:T(8,128)(2,1)S(1)} %convolution_convert_fusion.3), channel_id=1, source_target_pairs={{1,0},{2,1},{3,2},{4,3},{5,4},{6,5},{7,6},{8,7},{9,8},{10,9},{11,1... | collective-permute-start | bytes 786440 | tf_op jit(solution)/shard_map/ppermute | solution.py:17
  58.1 2.6 %collective-permute-start = (bf16[512,256]{1,0:T(8,128)(2,1)S(1)}, bf16[512,256]{1,0:T(8,128)(2,1)S(1)}, u32[]{:S(2)}, u32[]{:S(2)}) collective-permute-start(bf16[512,256]{1,0:T(8,128)(2,1)S(1)} %convolution_convert_fusion.3), channel_id=1, source_target_pairs={{0,1},{1,2},{2,3},{3,4},{4,5},{5,6},{6,7},{7,8},{8,9},{9,10},{10,1... | collective-permute-start | bytes 786440 | tf_op jit(solution)/shard_map/ppermute | solution.py:14
  60.8 2.0 %collective-permute-done.1 = bf16[512,256]{1,0:T(8,128)(2,1)S(1)} collective-permute-done((bf16[512,256]{1,0:T(8,128)(2,1)S(1)}, bf16[512,256]{1,0:T(8,128)(2,1)S(1)}, u32[]{:S(2)}, u32[]{:S(2)}) %collective-permute-start.1) | collective-permute-done | bytes 262176 | tf_op jit(solution)/shard_map/ppermute | solution.py:17
  64.7 1.6 %fusion.55 = bf16[4,128,256]{2,1,0:T(8,128)(2,1)S(1)} fusion(bf16[4,6,128,256]{3,2,1,0:T(8,128)(2,1)S(1)} %bitcast.68, bf16[4,6,128,128]{3,2,1,0:T(8,128)(2,1)} %param.11, pred[4,6]{1,0:T(4,128)(4,1)S(1)} %iota_compare_fusion.9), kind=kOutput, calls=%fused_computation.61 | convolution fusion | flops 201981952 | bytes 2621464 | tf_op jit(solution)/shard_map/tkij,tkjf->tif/dot_general | solution.py:31
  66.5 1.9 %collective-permute-start.3 = (bf16[512,256]{1,0:T(8,128)(2,1)S(1)}, bf16[512,256]{1,0:T(8,128)(2,1)S(1)}, u32[]{:S(2)}, u32[]{:S(2)}) collective-permute-start(bf16[512,256]{1,0:T(8,128)(2,1)S(1)} %convolution_convert_fusion.2), channel_id=1, source_target_pairs={{1,0},{2,1},{3,2},{4,3},{5,4},{6,5},{7,6},{8,7},{9,8},{10,9},{11,1... | collective-permute-start | bytes 786440 | tf_op jit(solution)/shard_map/ppermute | solution.py:17
  68.4 4.4 %collective-permute-start.2 = (bf16[512,256]{1,0:T(8,128)(2,1)S(1)}, bf16[512,256]{1,0:T(8,128)(2,1)S(1)}, u32[]{:S(2)}, u32[]{:S(2)}) collective-permute-start(bf16[512,256]{1,0:T(8,128)(2,1)S(1)} %convolution_convert_fusion.2), channel_id=1, source_target_pairs={{0,1},{1,2},{2,3},{3,4},{4,5},{5,6},{6,7},{7,8},{8,9},{9,10},{10,1... | collective-permute-start | bytes 786440 | tf_op jit(solution)/shard_map/ppermute | solution.py:14
  72.8 2.1 %collective-permute-done.3 = bf16[512,256]{1,0:T(8,128)(2,1)S(1)} collective-permute-done((bf16[512,256]{1,0:T(8,128)(2,1)S(1)}, bf16[512,256]{1,0:T(8,128)(2,1)S(1)}, u32[]{:S(2)}, u32[]{:S(2)}) %collective-permute-start.3) | collective-permute-done | bytes 262176 | tf_op jit(solution)/shard_map/ppermute | solution.py:17
  76.8 1.6 %fusion.54 = bf16[4,128,256]{2,1,0:T(8,128)(2,1)S(1)} fusion(bf16[4,6,128,256]{3,2,1,0:T(8,128)(2,1)S(1)} %bitcast.67, bf16[4,6,128,128]{3,2,1,0:T(8,128)(2,1)} %param.11, pred[4,6]{1,0:T(4,128)(4,1)S(1)} %iota_compare_fusion.9), kind=kOutput, calls=%fused_computation.57 | convolution fusion | flops 201850880 | bytes 2621464 | tf_op jit(solution)/shard_map/tkij,tkjf->tif/dot_general | solution.py:31
  79.5 13.6 %all-to-all-start.1 = ((bf16[128,4,256]{2,1,0:T(4,128)(2,1)}), bf16[128,4,256]{2,1,0:T(4,128)(2,1)S(1)}, u32[]{:S(2)}, u32[]{:S(2)}) async-start(bf16[128,4,256]{2,1,0:T(4,128)(2,1)} %reshape.130), calls=%async_computation.1 | async-start | bytes 524288 | tf_op jit(solution)/shard_map/all_to_all | solution.py:114
  93.2 9.5 %fusion.4 = f32[8192,256]{1,0:T(8,128)} fusion(bf16[512,256]{1,0:T(8,128)(2,1)S(1)} %bitcast.76, s32[8192]{0:T(1024)S(1)} %get-tuple-element.27, bf16[8192,256]{1,0:T(8,128)(2,1)} %param.7, pred[8192]{0:T(1024)(128)(4,1)S(1)} %get-tuple-element.14), kind=kOutput, calls=%fused_computation.12 | convolution fusion | flops 2168455168 | bytes 12886016 | tf_op jit(solution)/shard_map/dot_general | solution.py:118
  102.6 1.3 %all-to-all-done.1 = bf16[128,4,256]{2,1,0:T(4,128)(2,1)S(1)} async-done(((bf16[128,4,256]{2,1,0:T(4,128)(2,1)}), bf16[128,4,256]{2,1,0:T(4,128)(2,1)S(1)}, u32[]{:S(2)}, u32[]{:S(2)}) %all-to-all-start.1) | async-done | bytes 262176 | tf_op jit(solution)/shard_map/all_to_all | solution.py:114
  104.3 8.5 %convolution_add_fusion.3 = f32[8192,256]{1,0:T(8,128)S(1)} fusion(f32[8192,256]{1,0:T(8,128)} %fusion.4, s32[8192]{0:T(1024)S(1)} %get-tuple-element.26, pred[8192]{0:T(1024)(128)(4,1)S(1)} %get-tuple-element.25, bf16[128,1,256]{2,1,0:T(2,128)(2,1)S(1)} %get-tuple-element.20), kind=kOutput, calls=%fused_computation.8 | convolution fusion | flops 542113792 | bytes 16883712 | tf_op jit(solution)/shard_map/dot_general | solution.py:122
  112.9 2.4 %convolution_add_fusion.2 = f32[8192,256]{1,0:T(8,128)S(1)} fusion(f32[8192,256]{1,0:T(8,128)S(1)} %convolution_add_fusion.3, s32[8192]{0:T(1024)S(1)} %get-tuple-element.26, pred[8192]{0:T(1024)(128)(4,1)S(1)} %get-tuple-element.24, bf16[128,1,256]{2,1,0:T(2,128)(2,1)S(1)} %get-tuple-element.19), kind=kOutput, calls=%fused_computation.7 | convolution fusion | flops 542113792 | bytes 16883712 | tf_op jit(solution)/shard_map/dot_general | solution.py:122
  115.2 2.4 %convolution_add_fusion.1 = f32[8192,256]{1,0:T(8,128)S(1)} fusion(f32[8192,256]{1,0:T(8,128)S(1)} %convolution_add_fusion.2, s32[8192]{0:T(1024)S(1)} %get-tuple-element.26, pred[8192]{0:T(1024)(128)(4,1)S(1)} %get-tuple-element.23, bf16[128,1,256]{2,1,0:T(2,128)(2,1)S(1)} %get-tuple-element.18), kind=kOutput, calls=%fused_computation.6 | convolution fusion | flops 542113792 | bytes 16883712 | tf_op jit(solution)/shard_map/dot_general | solution.py:122
  117.6 5.5 %fusion.2 = bf16[8192,256]{1,0:T(8,128)(2,1)} fusion(f32[8192,256]{1,0:T(8,128)S(1)} %convolution_add_fusion.1, s32[8192]{0:T(1024)S(1)} %get-tuple-element.26, pred[8192]{0:T(1024)(128)(4,1)S(1)} %get-tuple-element.13, bf16[128,1,256]{2,1,0:T(2,128)(2,1)S(1)} %get-tuple-element.17), kind=kOutput, calls=%fused_computation.9 | convolution fusion | flops 544210944 | bytes 12689408 | tf_op jit(solution)/shard_map/dot_general | solution.py:122
  (63 shorter events, 12.2 us)
Async XLA Ops:
  0.0 54.9 %copy-start = (bf16[256,256]{1,0:T(8,128)(2,1)S(1)}, bf16[256,256]{1,0:T(8,128)(2,1)}, u32[]{:S(2)}) copy-start(bf16[256,256]{1,0:T(8,128)(2,1)} %param.12) | copy-start | bytes 393220
  5.2 3.5 %copy-start.2 = (s32[8192]{0:T(1024)S(1)}, s32[8192]{0:T(1024)}, u32[]{:S(2)}) copy-start(s32[8192]{0:T(1024)} %param.8) | copy-start | bytes 98308
  8.7 7.6 %copy-start.4 = (bf16[8192,256]{1,0:T(8,128)(2,1)S(1)}, bf16[8192,256]{1,0:T(8,128)(2,1)}, u32[]{:S(2)}) copy-start(bf16[8192,256]{1,0:T(8,128)(2,1)} %param.7) | copy-start | bytes 12582916
  27.3 25.7 %all-to-all-start = ((f32[128,1,1152]{2,1,0:T(1,128)}), f32[128,1,1152]{2,1,0:T(1,128)S(1)}, u32[]{:S(2)}, u32[]{:S(2)}) async-start(f32[128,1,1152]{2,1,0:T(1,128)} %copy.66), calls=%async_computation | async-start | bytes 1179648 | tf_op jit(solution)/shard_map/all_to_all | solution.py:87
  38.8 6.8 %copy-start.3 = (s32[4,6]{1,0:T(4,128)S(1)}, s32[4,6]{1,0:T(4,128)}, u32[]{:S(2)}) copy-start(s32[4,6]{1,0:T(4,128)} %param.9) | copy-start | bytes 292
  45.6 15.1 %copy-start.5 = (s32[4]{0:T(128)S(1)}, s32[4]{0:T(128)}, u32[]{:S(2)}) copy-start(s32[4]{0:T(128)} %param.10) | copy-start | bytes 52
  54.9 11.4 %copy-start.1 = (bf16[256,256]{1,0:T(8,128)(2,1)S(1)}, bf16[256,256]{1,0:T(8,128)(2,1)}, u32[]{:S(2)}) copy-start(bf16[256,256]{1,0:T(8,128)(2,1)} %param.13) | copy-start | bytes 393220
  55.1 7.7 %collective-permute-start.1 = (bf16[512,256]{1,0:T(8,128)(2,1)S(1)}, bf16[512,256]{1,0:T(8,128)(2,1)S(1)}, u32[]{:S(2)}, u32[]{:S(2)}) collective-permute-start(bf16[512,256]{1,0:T(8,128)(2,1)S(1)} %convolution_convert_fusion.3), channel_id=1, source_target_pairs={{1,0},{2,1},{3,2},{4,3},{5,4},{6,5},{7,6},{8,7},{9,8},{10,9},{11,1... | collective-permute-start | bytes 786440 | tf_op jit(solution)/shard_map/ppermute | solution.py:17
  58.1 5.9 %collective-permute-start = (bf16[512,256]{1,0:T(8,128)(2,1)S(1)}, bf16[512,256]{1,0:T(8,128)(2,1)S(1)}, u32[]{:S(2)}, u32[]{:S(2)}) collective-permute-start(bf16[512,256]{1,0:T(8,128)(2,1)S(1)} %convolution_convert_fusion.3), channel_id=1, source_target_pairs={{0,1},{1,2},{2,3},{3,4},{4,5},{5,6},{6,7},{7,8},{8,9},{9,10},{10,1... | collective-permute-start | bytes 786440 | tf_op jit(solution)/shard_map/ppermute | solution.py:14
  66.5 8.4 %collective-permute-start.3 = (bf16[512,256]{1,0:T(8,128)(2,1)S(1)}, bf16[512,256]{1,0:T(8,128)(2,1)S(1)}, u32[]{:S(2)}, u32[]{:S(2)}) collective-permute-start(bf16[512,256]{1,0:T(8,128)(2,1)S(1)} %convolution_convert_fusion.2), channel_id=1, source_target_pairs={{1,0},{2,1},{3,2},{4,3},{5,4},{6,5},{7,6},{8,7},{9,8},{10,9},{11,1... | collective-permute-start | bytes 786440 | tf_op jit(solution)/shard_map/ppermute | solution.py:17
  68.4 7.7 %collective-permute-start.2 = (bf16[512,256]{1,0:T(8,128)(2,1)S(1)}, bf16[512,256]{1,0:T(8,128)(2,1)S(1)}, u32[]{:S(2)}, u32[]{:S(2)}) collective-permute-start(bf16[512,256]{1,0:T(8,128)(2,1)S(1)} %convolution_convert_fusion.2), channel_id=1, source_target_pairs={{0,1},{1,2},{2,3},{3,4},{4,5},{5,6},{6,7},{7,8},{8,9},{9,10},{10,1... | collective-permute-start | bytes 786440 | tf_op jit(solution)/shard_map/ppermute | solution.py:14
  79.5 24.4 %all-to-all-start.1 = ((bf16[128,4,256]{2,1,0:T(4,128)(2,1)}), bf16[128,4,256]{2,1,0:T(4,128)(2,1)S(1)}, u32[]{:S(2)}, u32[]{:S(2)}) async-start(bf16[128,4,256]{2,1,0:T(4,128)(2,1)} %reshape.130), calls=%async_computation.1 | async-start | bytes 524288 | tf_op jit(solution)/shard_map/all_to_all | solution.py:114

commit v6 on v4

--- a/solution.py
+++ b/solution.py
@@ -73,27 +73,19 @@
     lows = parts[:, :DCAP] * 32 + parts[:, DCAP:]
     slot = jnp.sum((lids[:, None] >= lows[:, 1:]).astype(jnp.int32), axis=1)
     slot = jnp.where(remote, slot, -1)
-    masked = jnp.concatenate(
-        [jnp.where((slot == k)[:, None], features, jnp.zeros((), features.dtype)) for k in range(DCAP)],
-        axis=1,
-    )
-    remote_sums = lax.dot_general(owner_hot, masked, contract_rows, preferred_element_type=jnp.float32)
-    meta = jnp.concatenate(
-        [slot_counts, jnp.where(slot_ids < clusters_here, slot_ids, 0).astype(jnp.float32),
-         jnp.zeros((device_count, 128 - 2 * DCAP), jnp.float32)],
-        axis=1,
-    )
-    payload = jnp.concatenate([remote_sums, meta], axis=1)
-    got = lax.all_to_all(
-        payload.reshape(device_count, 1, -1), "nodes", split_axis=0, concat_axis=0, tiled=True
-    ).reshape(device_count, -1)
-    got_sums = got[:, : DCAP * width].reshape(remote_slots, width)
-    got_counts = got[:, DCAP * width : DCAP * width + DCAP].reshape(remote_slots)
-    got_ids = got[:, DCAP * width + DCAP : DCAP * width + 2 * DCAP].reshape(remote_slots).astype(jnp.int32)
-    local_hot = jnp.where(remote[:, None], jnp.zeros((), jnp.bfloat16), lid_hot)
     slot_column = jnp.where(remote, owners * DCAP + slot, -1)
     slot_range = jnp.arange(remote_slots, dtype=jnp.int32)
     remote_hot = (slot_column[:, None] == slot_range[None, :]).astype(jnp.bfloat16)
+    remote_sums = lax.dot_general(remote_hot, features, contract_rows, preferred_element_type=jnp.float32)
+    got_sums = lax.all_to_all(
+        remote_sums.reshape(device_count, DCAP, width), "nodes", split_axis=0, concat_axis=0, tiled=True
+    ).reshape(remote_slots, width)
+    meta = jnp.concatenate([slot_counts, slot_ids.astype(jnp.float32)], axis=1)
+    every_meta = lax.all_gather(meta[None], "nodes", axis=0, tiled=True)
+    mine = lax.dynamic_index_in_dim(every_meta, myself, axis=1, keepdims=False)
+    got_counts = mine[:, :DCAP].reshape(remote_slots)
+    got_ids = jnp.where(mine[:, DCAP:] < clusters_here, mine[:, DCAP:], 0).reshape(remote_slots).astype(jnp.int32)
+    local_hot = jnp.where(remote[:, None], jnp.zeros((), jnp.bfloat16), lid_hot)
     local_sums = lax.dot_general(
         local_hot, features, contract_rows, preferred_element_type=jnp.float32
     )
@@ -116,11 +108,13 @@
     ).astype(jnp.bfloat16)
     returned = lax.all_to_all(
         answers.reshape(device_count, DCAP, width), "nodes", split_axis=0, concat_axis=0, tiled=True
-    ).reshape(remote_slots, width)
+    )
     first = (
         features.astype(jnp.float32) + jnp.dot(local_hot, coarse, preferred_element_type=jnp.float32)
     ).astype(jnp.bfloat16)
-    value = first.astype(jnp.float32) + jnp.dot(remote_hot, returned, preferred_element_type=jnp.float32)
+    value = first.astype(jnp.float32) + jnp.dot(
+        remote_hot, returned.reshape(remote_slots, width), preferred_element_type=jnp.float32
+    )
     return value.astype(jnp.bfloat16)
 
 

time: 119 us -> 134 us (1.13)
  blocking collectives: 0 us -> 38.3 us
  waiting for transfers between devices: 19.5 us -> 7.84 us
  other arithmetic: 11.4 us -> 2.25 us
  matrix products: 46.2 us -> 42.9 us
    all_gather x0 -> x1, blocking collectives: none -> 38.3 us  [local(): every_meta = lax.all_gather(meta[None], 'nodes', axis=0, tiled=True)]
    select_n x1 -> x0, other arithmetic: 9.13 us -> none  [local(): jnp.where((slot == k)[:, None], features, jnp.zeros((), features.dtype))]
    all_to_all x1, waiting for transfers between devices: 7.23 us -> 0.01 us  [local(): lax.all_to_all(remote_sums.reshape(device_count, DCAP, width), 'nodes', s...]
    dot_general x2, matrix products: 21 us -> 15.4 us  [the longest x1 7.82 us: local(): lax.dot_general(remote_hot, features, contract_rows, preferred_element_ty...]
    ppermute x2, waiting for transfers between devices: 8.79 us -> 4.13 us  [with_halo(): lax.ppermute(lax.slice_in_dim(block, 0, width, axis=dim), axis, backward)]
    ppermute x2, starting transfers between devices: 4.94 us -> 7.87 us  [with_halo(): lax.ppermute(lax.slice_in_dim(block, block.shape[dim] - width, None, axis...]
    dot_general x2, matrix products: 0.86 us -> 3.14 us  [convolve(): jnp.einsum('tkij,tkjf->tif', weights, picked, preferred_element_type=jnp....]
    all_to_all x1, starting transfers between devices: 15.8 us -> 14.2 us  [local(): lax.all_to_all(answers.reshape(device_count, DCAP, width), 'nodes', split...]
  transfers between devices with their start and end apart: 6 -> 6, of which waited for: 6 -> 5; matrix products, arithmetic and copies ran while one was open for 14% -> 13% of each run, Pallas kernels for 0% -> 0%
where the time goes in v6:
time: 134 us
  matrix products  42.9 us (32%)
  blocking collectives  38.3 us (29%)
  starting transfers between devices  37.5 us (28%)
  waiting for transfers between devices  7.84 us (6%)
  local copies, waits for them, and re-layouts  4.48 us (3%)
  other arithmetic  2.25 us (2%)
    all_gather x1, blocking collectives, local(): every_meta = lax.all_gather(meta[None], 'nodes', axis=0, tiled=True)  38.3 us
    all_to_all x1, starting transfers between devices, local(): lax.all_to_all(answers.reshape(device_count, DCAP, width), 'nodes', split...  14.2 us
    all_to_all x1, starting transfers between devices, local(): lax.all_to_all(remote_sums.reshape(device_count, DCAP, width), 'nodes', s...  11.5 us
    dot_general x1, matrix products, local(): jnp.dot(local_hot, coarse, preferred_element_type=jnp.float32)  9.46 us
    ppermute x2, starting transfers between devices, with_halo(): lax.ppermute(lax.slice_in_dim(block, block.shape[dim] - width, None, axis...  7.87 us
    dot_general x1, matrix products, local(): lax.dot_general(remote_hot, features, contract_rows, preferred_element_ty...  7.82 us
    dot_general x1, matrix products, local(): jnp.dot(remote_hot, returned.reshape(remote_slots, width), preferred_elem...  7.61 us
    dot_general x1, matrix products, local(): lax.dot_general(local_hot, features, contract_rows, preferred_element_typ...  6.82 us
  transfers between devices with their start and end apart: 6, of which 5 were waited for; matrix products, arithmetic and copies ran while one was open for 13% of the time, Pallas kernels for 0%

profile of v6, /device:TPU:1, one launch (start us, length us, event | category | flops | bytes accessed | tf_op | source)
XLA Modules:
  0.0 133.7 jit_solution(280779880372053715)
XLA Ops:
  0.0 0.8 add_select_fusion
  0.8 4.3 %broadcast_compare_fusion = (pred[128,512]{1,0:T(32,128)(4,1)S(1)}, f32[128,512]{1,0:T(8,128)S(1)}) fusion(s32[8192]{0:T(1024)S(1)} %get-tuple-element.16, s32[8192]{0:T(1024)S(1)} %get-tuple-element.15), kind=kOutput, calls=%fused_computation.67 | convolution fusion | flops 1079050240 | bytes 393216 | tf_op jit(solution)/shard_map/dot_general | solution.py:37
  6.6 1.3 convolution_convert_fusion
  8.1 7.8 %fusion.1 = f32[512,256]{1,0:T(8,128)S(1)} fusion(bf16[8192,256]{1,0:T(8,128)(2,1)} %param.7, s32[8192]{0:T(1024)S(1)} %add_select_fusion.1), kind=kOutput, calls=%fused_computation.4 | convolution fusion | flops 2151677952 | bytes 4751360 | tf_op jit(solution)/shard_map/dot_general | solution.py:79
  15.9 1.1 reshape.122
  17.1 11.5 %all-to-all-start = ((f32[128,4,256]{2,1,0:T(4,128)}), f32[128,4,256]{2,1,0:T(4,128)S(1)}, u32[]{:S(2)}, u32[]{:S(2)}) async-start(f32[128,4,256]{2,1,0:T(4,128)} %reshape.122), calls=%async_computation | async-start | bytes 1048576 | tf_op jit(solution)/shard_map/all_to_all | solution.py:80
  28.6 38.3 %all-gather = f32[16384,8]{0,1:T(8,128)S(1)} all-gather(f32[128,8]{0,1:T(8,128)S(1)} %concatenate.13), channel_id=2, replica_groups=mesh['nodes'=128] {'nodes'}, dimensions={0}, use_global_device_ids=true | all-gather | bytes 528384 | tf_op jit(solution)/shard_map/all_gather | solution.py:84
  67.4 6.8 %fusion.10 = f32[512,256]{1,0:T(8,128)S(1)} fusion(bf16[8192,256]{1,0:T(8,128)(2,1)} %param.7, s32[8192]{0:T(1024)S(1)} %get-tuple-element.16, pred[8192]{0:T(1024)(128)(4,1)S(1)} %broadcast_compare_fusion.1), kind=kOutput, calls=%fused_computation.15 | convolution fusion | flops 2160066560 | bytes 4759552 | tf_op jit(solution)/shard_map/dot_general | solution.py:89
  75.3 1.1 fusion.25
  76.6 2.1 %collective-permute-start.1 = (bf16[512,256]{1,0:T(8,128)(2,1)S(1)}, bf16[512,256]{1,0:T(8,128)(2,1)S(1)}, u32[]{:S(2)}, u32[]{:S(2)}) collective-permute-start(bf16[512,256]{1,0:T(8,128)(2,1)S(1)} %convolution_convert_fusion.3), channel_id=1, source_target_pairs={{1,0},{2,1},{3,2},{4,3},{5,4},{6,5},{7,6},{8,7},{9,8},{10,9},{11,1... | collective-permute-start | bytes 786440 | tf_op jit(solution)/shard_map/ppermute | solution.py:17
  78.7 3.5 %collective-permute-start = (bf16[512,256]{1,0:T(8,128)(2,1)S(1)}, bf16[512,256]{1,0:T(8,128)(2,1)S(1)}, u32[]{:S(2)}, u32[]{:S(2)}) collective-permute-start(bf16[512,256]{1,0:T(8,128)(2,1)S(1)} %convolution_convert_fusion.3), channel_id=1, source_target_pairs={{0,1},{1,2},{2,3},{3,4},{4,5},{5,6},{6,7},{7,8},{8,9},{9,10},{10,1... | collective-permute-start | bytes 786440 | tf_op jit(solution)/shard_map/ppermute | solution.py:14
  82.3 2.0 %collective-permute-done.1 = bf16[512,256]{1,0:T(8,128)(2,1)S(1)} collective-permute-done((bf16[512,256]{1,0:T(8,128)(2,1)S(1)}, bf16[512,256]{1,0:T(8,128)(2,1)S(1)}, u32[]{:S(2)}, u32[]{:S(2)}) %collective-permute-start.1) | collective-permute-done | bytes 262176 | tf_op jit(solution)/shard_map/ppermute | solution.py:17
  84.3 1.2 collective-permute-done
  86.2 1.6 %fusion.27 = bf16[4,128,256]{2,1,0:T(8,128)(2,1)S(1)} fusion(bf16[4,6,128,256]{3,2,1,0:T(8,128)(2,1)S(1)} %bitcast.50, bf16[4,6,128,128]{3,2,1,0:T(8,128)(2,1)} %param.11, pred[4,6]{1,0:T(4,128)(4,1)S(1)} %iota_compare_fusion.16), kind=kOutput, calls=%fused_computation.38 | convolution fusion | flops 201981952 | bytes 2621464 | tf_op jit(solution)/shard_map/tkij,tkjf->tif/dot_general | solution.py:31
  88.0 1.9 %collective-permute-start.3 = (bf16[512,256]{1,0:T(8,128)(2,1)S(1)}, bf16[512,256]{1,0:T(8,128)(2,1)S(1)}, u32[]{:S(2)}, u32[]{:S(2)}) collective-permute-start(bf16[512,256]{1,0:T(8,128)(2,1)S(1)} %convolution_convert_fusion.2), channel_id=1, source_target_pairs={{1,0},{2,1},{3,2},{4,3},{5,4},{6,5},{7,6},{8,7},{9,8},{10,9},{11,1... | collective-permute-start | bytes 786440 | tf_op jit(solution)/shard_map/ppermute | solution.py:17
  90.0 4.4 %collective-permute-start.2 = (bf16[512,256]{1,0:T(8,128)(2,1)S(1)}, bf16[512,256]{1,0:T(8,128)(2,1)S(1)}, u32[]{:S(2)}, u32[]{:S(2)}) collective-permute-start(bf16[512,256]{1,0:T(8,128)(2,1)S(1)} %convolution_convert_fusion.2), channel_id=1, source_target_pairs={{0,1},{1,2},{2,3},{3,4},{4,5},{5,6},{6,7},{7,8},{8,9},{9,10},{10,1... | collective-permute-start | bytes 786440 | tf_op jit(solution)/shard_map/ppermute | solution.py:14
  94.4 2.1 %collective-permute-done.3 = bf16[512,256]{1,0:T(8,128)(2,1)S(1)} collective-permute-done((bf16[512,256]{1,0:T(8,128)(2,1)S(1)}, bf16[512,256]{1,0:T(8,128)(2,1)S(1)}, u32[]{:S(2)}, u32[]{:S(2)}) %collective-permute-start.3) | collective-permute-done | bytes 262176 | tf_op jit(solution)/shard_map/ppermute | solution.py:17
  96.5 1.2 collective-permute-done.2
  98.4 1.6 %fusion.26 = bf16[4,128,256]{2,1,0:T(8,128)(2,1)S(1)} fusion(bf16[4,6,128,256]{3,2,1,0:T(8,128)(2,1)S(1)} %bitcast.49, bf16[4,6,128,128]{3,2,1,0:T(8,128)(2,1)} %param.11, pred[4,6]{1,0:T(4,128)(4,1)S(1)} %iota_compare_fusion.16), kind=kOutput, calls=%fused_computation.34 | convolution fusion | flops 201850880 | bytes 2621464 | tf_op jit(solution)/shard_map/tkij,tkjf->tif/dot_general | solution.py:31
  100.3 0.8 reshape.126
  101.1 14.2 %all-to-all-start.1 = ((bf16[128,4,256]{2,1,0:T(4,128)(2,1)}), bf16[128,4,256]{2,1,0:T(4,128)(2,1)S(1)}, u32[]{:S(2)}, u32[]{:S(2)}) async-start(bf16[128,4,256]{2,1,0:T(4,128)(2,1)} %reshape.126), calls=%async_computation.1 | async-start | bytes 524288 | tf_op jit(solution)/shard_map/all_to_all | solution.py:109
  115.2 9.5 %fusion.7 = f32[8192,256]{1,0:T(8,128)} fusion(bf16[512,256]{1,0:T(8,128)(2,1)S(1)} %bitcast.59, s32[8192]{0:T(1024)S(1)} %get-tuple-element.16, bf16[8192,256]{1,0:T(8,128)(2,1)} %param.7, pred[8192]{0:T(1024)(128)(4,1)S(1)} %broadcast_compare_fusion.1), kind=kOutput, calls=%fused_computation.12 | convolution fusion | flops 2168455168 | bytes 12886016 | tf_op jit(solution)/shard_map/dot_general | solution.py:113
  124.7 1.3 %all-to-all-done.1 = bf16[128,4,256]{2,1,0:T(4,128)(2,1)S(1)} async-done(((bf16[128,4,256]{2,1,0:T(4,128)(2,1)}), bf16[128,4,256]{2,1,0:T(4,128)(2,1)S(1)}, u32[]{:S(2)}, u32[]{:S(2)}) %all-to-all-start.1) | async-done | bytes 262176 | tf_op jit(solution)/shard_map/all_to_all | solution.py:109
  126.1 7.6 %fusion.5 = bf16[8192,256]{1,0:T(8,128)(2,1)} fusion(f32[8192,256]{1,0:T(8,128)} %fusion.7, bf16[512,256]{1,0:T(8,128)(2,1)S(1)} %reshape.127, s32[8192]{0:T(1024)S(1)} %add_select_fusion.1), kind=kOutput, calls=%fused_computation.9 | convolution fusion | flops 2155872256 | bytes 12877824 | tf_op jit(solution)/shard_map/dot_general | solution.py:115
  (52 shorter events, 5.4 us)
Async XLA Ops:
  0.0 76.4 %copy-start = (bf16[256,256]{1,0:T(8,128)(2,1)S(1)}, bf16[256,256]{1,0:T(8,128)(2,1)}, u32[]{:S(2)}) copy-start(bf16[256,256]{1,0:T(8,128)(2,1)} %param.12) | copy-start | bytes 393220
  5.2 2.9 %copy-start.1 = (s32[8192]{0:T(1024)S(1)}, s32[8192]{0:T(1024)}, u32[]{:S(2)}) copy-start(s32[8192]{0:T(1024)} %param.8) | copy-start | bytes 98308
  17.1 58.0 %all-to-all-start = ((f32[128,4,256]{2,1,0:T(4,128)}), f32[128,4,256]{2,1,0:T(4,128)S(1)}, u32[]{:S(2)}, u32[]{:S(2)}) async-start(f32[128,4,256]{2,1,0:T(4,128)} %reshape.122), calls=%async_computation | async-start | bytes 1048576 | tf_op jit(solution)/shard_map/all_to_all | solution.py:80
  67.4 6.9 %copy-start.3 = (s32[4,6]{1,0:T(4,128)S(1)}, s32[4,6]{1,0:T(4,128)}, u32[]{:S(2)}) copy-start(s32[4,6]{1,0:T(4,128)} %param.9) | copy-start | bytes 292
  74.2 8.0 %copy-start.4 = (s32[4]{0:T(128)S(1)}, s32[4]{0:T(128)}, u32[]{:S(2)}) copy-start(s32[4]{0:T(128)} %param.10) | copy-start | bytes 52
  76.4 11.4 %copy-start.2 = (bf16[256,256]{1,0:T(8,128)(2,1)S(1)}, bf16[256,256]{1,0:T(8,128)(2,1)}, u32[]{:S(2)}) copy-start(bf16[256,256]{1,0:T(8,128)(2,1)} %param.13) | copy-start | bytes 393220
  76.6 7.7 %collective-permute-start.1 = (bf16[512,256]{1,0:T(8,128)(2,1)S(1)}, bf16[512,256]{1,0:T(8,128)(2,1)S(1)}, u32[]{:S(2)}, u32[]{:S(2)}) collective-permute-start(bf16[512,256]{1,0:T(8,128)(2,1)S(1)} %convolution_convert_fusion.3), channel_id=1, source_target_pairs={{1,0},{2,1},{3,2},{4,3},{5,4},{6,5},{7,6},{8,7},{9,8},{10,9},{11,1... | collective-permute-start | bytes 786440 | tf_op jit(solution)/shard_map/ppermute | solution.py:17
  78.7 6.8 %collective-permute-start = (bf16[512,256]{1,0:T(8,128)(2,1)S(1)}, bf16[512,256]{1,0:T(8,128)(2,1)S(1)}, u32[]{:S(2)}, u32[]{:S(2)}) collective-permute-start(bf16[512,256]{1,0:T(8,128)(2,1)S(1)} %convolution_convert_fusion.3), channel_id=1, source_target_pairs={{0,1},{1,2},{2,3},{3,4},{4,5},{5,6},{6,7},{7,8},{8,9},{9,10},{10,1... | collective-permute-start | bytes 786440 | tf_op jit(solution)/shard_map/ppermute | solution.py:14
  88.0 8.4 %collective-permute-start.3 = (bf16[512,256]{1,0:T(8,128)(2,1)S(1)}, bf16[512,256]{1,0:T(8,128)(2,1)S(1)}, u32[]{:S(2)}, u32[]{:S(2)}) collective-permute-start(bf16[512,256]{1,0:T(8,128)(2,1)S(1)} %convolution_convert_fusion.2), channel_id=1, source_target_pairs={{1,0},{2,1},{3,2},{4,3},{5,4},{6,5},{7,6},{8,7},{9,8},{10,9},{11,1... | collective-permute-start | bytes 786440 | tf_op jit(solution)/shard_map/ppermute | solution.py:17
  90.0 7.7 %collective-permute-start.2 = (bf16[512,256]{1,0:T(8,128)(2,1)S(1)}, bf16[512,256]{1,0:T(8,128)(2,1)S(1)}, u32[]{:S(2)}, u32[]{:S(2)}) collective-permute-start(bf16[512,256]{1,0:T(8,128)(2,1)S(1)} %convolution_convert_fusion.2), channel_id=1, source_target_pairs={{0,1},{1,2},{2,3},{3,4},{4,5},{5,6},{6,7},{7,8},{8,9},{9,10},{10,1... | collective-permute-start | bytes 786440 | tf_op jit(solution)/shard_map/ppermute | solution.py:14
  101.1 25.0 %all-to-all-start.1 = ((bf16[128,4,256]{2,1,0:T(4,128)(2,1)}), bf16[128,4,256]{2,1,0:T(4,128)(2,1)S(1)}, u32[]{:S(2)}, u32[]{:S(2)}) async-start(bf16[128,4,256]{2,1,0:T(4,128)(2,1)} %reshape.126), calls=%async_computation.1 | async-start | bytes 524288 | tf_op jit(solution)/shard_map/all_to_all | solution.py:109

commit v7 on v5

--- a/solution.py
+++ b/solution.py
@@ -55,8 +55,6 @@
     owner_hot = (owners[:, None] == peers[None, :]).astype(jnp.bfloat16)
     lid_hot = (lids[:, None] == here[None, :]).astype(jnp.bfloat16)
     presence, rank = distinct_slots(owner_hot, lid_hot, clusters_here)
-    remote_slots = device_count * DCAP
-    contract_rows = (((0,), (0,)), ((), ()))
 
     named = (presence > 0) & (peers != myself)[:, None]
     slot_counts = []
@@ -72,25 +70,28 @@
     parts = jnp.dot(owner_hot, split, preferred_element_type=jnp.float32).astype(jnp.int32)
     lows = parts[:, :DCAP] * 32 + parts[:, DCAP:]
     slot = jnp.sum((lids[:, None] >= lows[:, 1:]).astype(jnp.int32), axis=1)
-    slot = jnp.where(remote, slot, -1)
-    slot_hot = [jnp.where((slot == k)[:, None], owner_hot, jnp.zeros((), owner_hot.dtype)) for k in range(DCAP)]
-    remote_sums = jnp.concatenate(
-        [lax.dot_general(hot, features, contract_rows, preferred_element_type=jnp.float32) for hot in slot_hot],
-        axis=1,
+    remote_slots = device_count * DCAP
+    slot_column = jnp.where(remote, owners * DCAP + slot, -1)
+    slot_range = jnp.arange(remote_slots, dtype=jnp.int32)
+    remote_hot = (slot_column[:, None] == slot_range[None, :]).astype(jnp.bfloat16)
+    local_hot = jnp.where(remote[:, None], jnp.zeros((), jnp.bfloat16), lid_hot)
+    contract_rows = (((0,), (0,)), ((), ()))
+    remote_sums = lax.dot_general(
+        remote_hot, features, contract_rows, preferred_element_type=jnp.float32
     )
+
     meta = jnp.concatenate(
         [slot_counts, jnp.where(slot_ids < clusters_here, slot_ids, 0).astype(jnp.float32),
          jnp.zeros((device_count, 128 - 2 * DCAP), jnp.float32)],
         axis=1,
     )
-    payload = jnp.concatenate([remote_sums, meta], axis=1)
+    payload = jnp.concatenate([remote_sums.reshape(device_count, DCAP * width), meta], axis=1)
     got = lax.all_to_all(
         payload.reshape(device_count, 1, -1), "nodes", split_axis=0, concat_axis=0, tiled=True
     ).reshape(device_count, -1)
     got_sums = got[:, : DCAP * width].reshape(remote_slots, width)
     got_counts = got[:, DCAP * width : DCAP * width + DCAP].reshape(remote_slots)
     got_ids = got[:, DCAP * width + DCAP : DCAP * width + 2 * DCAP].reshape(remote_slots).astype(jnp.int32)
-    local_hot = jnp.where(remote[:, None], jnp.zeros((), jnp.bfloat16), lid_hot)
     local_sums = lax.dot_general(
         local_hot, features, contract_rows, preferred_element_type=jnp.float32
     )
@@ -113,13 +114,12 @@
     ).astype(jnp.bfloat16)
     returned = lax.all_to_all(
         answers.reshape(device_count, DCAP, width), "nodes", split_axis=0, concat_axis=0, tiled=True
+    ).reshape(remote_slots, width)
+    value = (
+        features.astype(jnp.float32)
+        + jnp.dot(local_hot, coarse, preferred_element_type=jnp.float32)
+        + jnp.dot(remote_hot, returned, preferred_element_type=jnp.float32)
     )
-    first = (
-        features.astype(jnp.float32) + jnp.dot(local_hot, coarse, preferred_element_type=jnp.float32)
-    ).astype(jnp.bfloat16)
-    value = first.astype(jnp.float32)
-    for k in range(DCAP):
-        value = value + jnp.dot(slot_hot[k], returned[:, k, :], preferred_element_type=jnp.float32)
     return value.astype(jnp.bfloat16)
 
 

time: 124 us -> 103 us (0.83)
  matrix products: 63.2 us -> 43.1 us
    dot_general x8 -> x2, matrix products: 35.7 us -> 15.6 us  [the longest x1 8 us: local(): lax.dot_general(remote_hot, features, contract_rows, preferred_element_ty...]
  transfers between devices with their start and end apart: 6 -> 6, of which waited for: 6 -> 6; matrix products, arithmetic and copies ran while one was open for 13% -> 16% of each run, Pallas kernels for 0% -> 0%
where the time goes in v7:
time: 103 us
  matrix products  43.1 us (42%)
  starting transfers between devices  37 us (36%)
  waiting for transfers between devices  15 us (15%)
  local copies, waits for them, and re-layouts  4.84 us (5%)
  other arithmetic  2.33 us (2%)
    all_to_all x1, starting transfers between devices, local(): lax.all_to_all(answers.reshape(device_count, DCAP, width), 'nodes', split...  13.6 us
    all_to_all x1, starting transfers between devices, local(): lax.all_to_all(payload.reshape(device_count, 1, -1), 'nodes', split_axis=...  11.5 us
    dot_general x1, matrix products, local(): jnp.dot(local_hot, coarse, preferred_element_type=jnp.float32)  9.48 us
    dot_general x1, matrix products, local(): lax.dot_general(remote_hot, features, contract_rows, preferred_element_ty...  8 us
    dot_general x1, matrix products, local(): jnp.dot(remote_hot, returned, preferred_element_type=jnp.float32)  7.61 us
    all_to_all x1, waiting for transfers between devices, local(): lax.all_to_all(payload.reshape(device_count, 1, -1), 'nodes', split_axis=...  7.2 us
    ppermute x2, starting transfers between devices, with_halo(): lax.ppermute(lax.slice_in_dim(block, block.shape[dim] - width, None, axis...  6.94 us
    dot_general x1, matrix products, local(): lax.dot_general(local_hot, features, contract_rows, preferred_element_typ...  6.81 us
  transfers between devices with their start and end apart: 6, of which 6 were waited for; matrix products, arithmetic and copies ran while one was open for 16% of the time, Pallas kernels for 0%

profile of v7, /device:TPU:1, one launch (start us, length us, event | category | flops | bytes accessed | tf_op | source)
XLA Modules:
  0.0 102.6 jit_solution(1203259451139289467)
XLA Ops:
  0.0 0.8 add_select_fusion
  0.8 4.3 %broadcast_compare_fusion = (pred[128,512]{1,0:T(32,128)(4,1)S(1)}, f32[128,512]{1,0:T(8,128)S(1)}) fusion(s32[8192]{0:T(1024)S(1)} %get-tuple-element.18, s32[8192]{0:T(1024)S(1)} %get-tuple-element.17), kind=kOutput, calls=%fused_computation.66 | convolution fusion | flops 1079050240 | bytes 393216 | tf_op jit(solution)/shard_map/dot_general | solution.py:37
  7.2 1.3 %convolution_convert_fusion = s32[8192,8]{0,1:T(8,128)S(1)} fusion(s32[8192]{0:T(1024)S(1)} %get-tuple-element.17, bf16[128,4]{0,1:T(4,128)(2,1)S(1)} %get-tuple-element.20, bf16[128,4]{0,1:T(4,128)(2,1)S(1)} %get-tuple-element.21), kind=kOutput, calls=%fused_computation.11 | convolution fusion | flops 17895424 | bytes 296960 | tf_op jit(solution)/shard_map/dot_general | solution.py:70
  8.7 8.0 %fusion.1 = f32[512,256]{1,0:T(8,128)S(1)} fusion(bf16[8192,256]{1,0:T(8,128)(2,1)} %param.7, s32[8192]{0:T(1024)S(1)} %add_select_fusion.1), kind=kOutput, calls=%fused_computation.4 | convolution fusion | flops 2151677952 | bytes 4751360 | tf_op jit(solution)/shard_map/dot_general | solution.py:79
  17.0 1.2 %reshape.129 = f32[128,1,1152]{2,1,0:T(1,128)} reshape(f32[128,1152]{1,0:T(8,128)S(1)} %concatenate.14) | data formatting | bytes 1179648 | tf_op jit(solution)/shard_map/reshape | solution.py:90
  18.3 11.5 %all-to-all-start = ((f32[128,1,1152]{2,1,0:T(1,128)}), f32[128,1,1152]{2,1,0:T(1,128)S(1)}, u32[]{:S(2)}, u32[]{:S(2)}) async-start(f32[128,1,1152]{2,1,0:T(1,128)} %reshape.129), calls=%async_computation | async-start | bytes 1179648 | tf_op jit(solution)/shard_map/all_to_all | solution.py:89
  29.8 6.8 %fusion.8 = f32[512,256]{1,0:T(8,128)S(1)} fusion(bf16[8192,256]{1,0:T(8,128)(2,1)} %param.7, s32[8192]{0:T(1024)S(1)} %get-tuple-element.18, pred[8192]{0:T(1024)(128)(4,1)S(1)} %broadcast_compare_fusion.1), kind=kOutput, calls=%fused_computation.13 | convolution fusion | flops 2160066560 | bytes 4759552 | tf_op jit(solution)/shard_map/dot_general | solution.py:95
  36.7 7.2 %all-to-all-done = f32[128,1,1152]{2,1,0:T(1,128)S(1)} async-done(((f32[128,1,1152]{2,1,0:T(1,128)}), f32[128,1,1152]{2,1,0:T(1,128)S(1)}, u32[]{:S(2)}, u32[]{:S(2)}) %all-to-all-start) | async-done | bytes 589856 | tf_op jit(solution)/shard_map/all_to_all | solution.py:89
  44.7 1.1 %fusion.23 = bf16[512,256]{1,0:T(8,128)(2,1)S(1)} fusion(f32[512,256]{1,0:T(8,128)S(1)} %fusion.8, f32[512,256]{1,0:T(8,128)S(1)} %reshape.131, s32[512]{0:T(512)S(1)} %convert_element_type.69, f32[512]{0:T(512)S(1)} %add_sqrt_fusion), kind=kOutput, calls=%fused_computation.31 | convolution fusion | flops 805961728 | bytes 1314816 | tf_op jit(solution)/shard_map/dot_general | solution.py:100
  46.1 3.0 %collective-permute-start.1 = (bf16[512,256]{1,0:T(8,128)(2,1)S(1)}, bf16[512,256]{1,0:T(8,128)(2,1)S(1)}, u32[]{:S(2)}, u32[]{:S(2)}) collective-permute-start(bf16[512,256]{1,0:T(8,128)(2,1)S(1)} %convolution_convert_fusion.3), channel_id=1, source_target_pairs={{1,0},{2,1},{3,2},{4,3},{5,4},{6,5},{7,6},{8,7},{9,8},{10,9},{11,1... | collective-permute-start | bytes 786440 | tf_op jit(solution)/shard_map/ppermute | solution.py:17
  49.1 2.6 %collective-permute-start = (bf16[512,256]{1,0:T(8,128)(2,1)S(1)}, bf16[512,256]{1,0:T(8,128)(2,1)S(1)}, u32[]{:S(2)}, u32[]{:S(2)}) collective-permute-start(bf16[512,256]{1,0:T(8,128)(2,1)S(1)} %convolution_convert_fusion.3), channel_id=1, source_target_pairs={{0,1},{1,2},{2,3},{3,4},{4,5},{5,6},{6,7},{7,8},{8,9},{9,10},{10,1... | collective-permute-start | bytes 786440 | tf_op jit(solution)/shard_map/ppermute | solution.py:14
  51.8 2.0 %collective-permute-done.1 = bf16[512,256]{1,0:T(8,128)(2,1)S(1)} collective-permute-done((bf16[512,256]{1,0:T(8,128)(2,1)S(1)}, bf16[512,256]{1,0:T(8,128)(2,1)S(1)}, u32[]{:S(2)}, u32[]{:S(2)}) %collective-permute-start.1) | collective-permute-done | bytes 262176 | tf_op jit(solution)/shard_map/ppermute | solution.py:17
  53.8 1.2 %collective-permute-done = bf16[512,256]{1,0:T(8,128)(2,1)S(1)} collective-permute-done((bf16[512,256]{1,0:T(8,128)(2,1)S(1)}, bf16[512,256]{1,0:T(8,128)(2,1)S(1)}, u32[]{:S(2)}, u32[]{:S(2)}) %collective-permute-start) | collective-permute-done | bytes 262176 | tf_op jit(solution)/shard_map/ppermute | solution.py:14
  55.7 1.6 %fusion.25 = bf16[4,128,256]{2,1,0:T(8,128)(2,1)S(1)} fusion(bf16[4,6,128,256]{3,2,1,0:T(8,128)(2,1)S(1)} %bitcast.52, bf16[4,6,128,128]{3,2,1,0:T(8,128)(2,1)} %param.11, pred[4,6]{1,0:T(4,128)(4,1)S(1)} %iota_compare_fusion.16), kind=kOutput, calls=%fused_computation.36 | convolution fusion | flops 201981952 | bytes 2621464 | tf_op jit(solution)/shard_map/tkij,tkjf->tif/dot_general | solution.py:31
  57.5 1.9 %collective-permute-start.3 = (bf16[512,256]{1,0:T(8,128)(2,1)S(1)}, bf16[512,256]{1,0:T(8,128)(2,1)S(1)}, u32[]{:S(2)}, u32[]{:S(2)}) collective-permute-start(bf16[512,256]{1,0:T(8,128)(2,1)S(1)} %convolution_convert_fusion.2), channel_id=1, source_target_pairs={{1,0},{2,1},{3,2},{4,3},{5,4},{6,5},{7,6},{8,7},{9,8},{10,9},{11,1... | collective-permute-start | bytes 786440 | tf_op jit(solution)/shard_map/ppermute | solution.py:17
  59.5 4.4 %collective-permute-start.2 = (bf16[512,256]{1,0:T(8,128)(2,1)S(1)}, bf16[512,256]{1,0:T(8,128)(2,1)S(1)}, u32[]{:S(2)}, u32[]{:S(2)}) collective-permute-start(bf16[512,256]{1,0:T(8,128)(2,1)S(1)} %convolution_convert_fusion.2), channel_id=1, source_target_pairs={{0,1},{1,2},{2,3},{3,4},{4,5},{5,6},{6,7},{7,8},{8,9},{9,10},{10,1... | collective-permute-start | bytes 786440 | tf_op jit(solution)/shard_map/ppermute | solution.py:14
  63.8 2.1 %collective-permute-done.3 = bf16[512,256]{1,0:T(8,128)(2,1)S(1)} collective-permute-done((bf16[512,256]{1,0:T(8,128)(2,1)S(1)}, bf16[512,256]{1,0:T(8,128)(2,1)S(1)}, u32[]{:S(2)}, u32[]{:S(2)}) %collective-permute-start.3) | collective-permute-done | bytes 262176 | tf_op jit(solution)/shard_map/ppermute | solution.py:17
  66.0 1.2 %collective-permute-done.2 = bf16[512,256]{1,0:T(8,128)(2,1)S(1)} collective-permute-done((bf16[512,256]{1,0:T(8,128)(2,1)S(1)}, bf16[512,256]{1,0:T(8,128)(2,1)S(1)}, u32[]{:S(2)}, u32[]{:S(2)}) %collective-permute-start.2) | collective-permute-done | bytes 262176 | tf_op jit(solution)/shard_map/ppermute | solution.py:14
  67.8 1.6 %fusion.24 = bf16[4,128,256]{2,1,0:T(8,128)(2,1)S(1)} fusion(bf16[4,6,128,256]{3,2,1,0:T(8,128)(2,1)S(1)} %bitcast.51, bf16[4,6,128,128]{3,2,1,0:T(8,128)(2,1)} %param.11, pred[4,6]{1,0:T(4,128)(4,1)S(1)} %iota_compare_fusion.16), kind=kOutput, calls=%fused_computation.32 | convolution fusion | flops 201850880 | bytes 2621464 | tf_op jit(solution)/shard_map/tkij,tkjf->tif/dot_general | solution.py:31
  69.8 0.8 reshape.134
  70.5 13.6 %all-to-all-start.1 = ((bf16[128,4,256]{2,1,0:T(4,128)(2,1)}), bf16[128,4,256]{2,1,0:T(4,128)(2,1)S(1)}, u32[]{:S(2)}, u32[]{:S(2)}) async-start(bf16[128,4,256]{2,1,0:T(4,128)(2,1)} %reshape.134), calls=%async_computation.1 | async-start | bytes 524288 | tf_op jit(solution)/shard_map/all_to_all | solution.py:115
  84.2 9.5 %convolution_add_fusion = f32[8192,256]{1,0:T(8,128)} fusion(bf16[512,256]{1,0:T(8,128)(2,1)S(1)} %bitcast.60, s32[8192]{0:T(1024)S(1)} %get-tuple-element.18, bf16[8192,256]{1,0:T(8,128)(2,1)} %param.7, pred[8192]{0:T(1024)(128)(4,1)S(1)} %broadcast_compare_fusion.1), kind=kOutput, calls=%fused_computation.10 | convolution fusion | flops 2164260864 | bytes 12886016 | tf_op jit(solution)/shard_map/dot_general | solution.py:120
  93.6 1.3 %all-to-all-done.1 = bf16[128,4,256]{2,1,0:T(4,128)(2,1)S(1)} async-done(((bf16[128,4,256]{2,1,0:T(4,128)(2,1)}), bf16[128,4,256]{2,1,0:T(4,128)(2,1)S(1)}, u32[]{:S(2)}, u32[]{:S(2)}) %all-to-all-start.1) | async-done | bytes 262176 | tf_op jit(solution)/shard_map/all_to_all | solution.py:115
  95.0 7.6 %fusion.5 = bf16[8192,256]{1,0:T(8,128)(2,1)} fusion(f32[8192,256]{1,0:T(8,128)} %convolution_add_fusion, bf16[512,256]{1,0:T(8,128)(2,1)S(1)} %reshape.135, s32[8192]{0:T(1024)S(1)} %add_select_fusion.1), kind=kOutput, calls=%fused_computation.9 | convolution fusion | flops 2155872256 | bytes 12877824 | tf_op jit(solution)/shard_map/dot_general | solution.py:121
  (56 shorter events, 5.7 us)
Async XLA Ops:
  0.0 45.9 %copy-start = (bf16[256,256]{1,0:T(8,128)(2,1)S(1)}, bf16[256,256]{1,0:T(8,128)(2,1)}, u32[]{:S(2)}) copy-start(bf16[256,256]{1,0:T(8,128)(2,1)} %param.12) | copy-start | bytes 393220
  5.2 3.5 %copy-start.1 = (s32[8192]{0:T(1024)S(1)}, s32[8192]{0:T(1024)}, u32[]{:S(2)}) copy-start(s32[8192]{0:T(1024)} %param.8) | copy-start | bytes 98308
  18.3 25.7 %all-to-all-start = ((f32[128,1,1152]{2,1,0:T(1,128)}), f32[128,1,1152]{2,1,0:T(1,128)S(1)}, u32[]{:S(2)}, u32[]{:S(2)}) async-start(f32[128,1,1152]{2,1,0:T(1,128)} %reshape.129), calls=%async_computation | async-start | bytes 1179648 | tf_op jit(solution)/shard_map/all_to_all | solution.py:89
  29.8 6.9 %copy-start.3 = (s32[4,6]{1,0:T(4,128)S(1)}, s32[4,6]{1,0:T(4,128)}, u32[]{:S(2)}) copy-start(s32[4,6]{1,0:T(4,128)} %param.9) | copy-start | bytes 292
  36.6 15.1 %copy-start.4 = (s32[4]{0:T(128)S(1)}, s32[4]{0:T(128)}, u32[]{:S(2)}) copy-start(s32[4]{0:T(128)} %param.10) | copy-start | bytes 52
  45.9 11.4 %copy-start.2 = (bf16[256,256]{1,0:T(8,128)(2,1)S(1)}, bf16[256,256]{1,0:T(8,128)(2,1)}, u32[]{:S(2)}) copy-start(bf16[256,256]{1,0:T(8,128)(2,1)} %param.13) | copy-start | bytes 393220
  46.1 7.7 %collective-permute-start.1 = (bf16[512,256]{1,0:T(8,128)(2,1)S(1)}, bf16[512,256]{1,0:T(8,128)(2,1)S(1)}, u32[]{:S(2)}, u32[]{:S(2)}) collective-permute-start(bf16[512,256]{1,0:T(8,128)(2,1)S(1)} %convolution_convert_fusion.3), channel_id=1, source_target_pairs={{1,0},{2,1},{3,2},{4,3},{5,4},{6,5},{7,6},{8,7},{9,8},{10,9},{11,1... | collective-permute-start | bytes 786440 | tf_op jit(solution)/shard_map/ppermute | solution.py:17
  49.1 5.9 %collective-permute-start = (bf16[512,256]{1,0:T(8,128)(2,1)S(1)}, bf16[512,256]{1,0:T(8,128)(2,1)S(1)}, u32[]{:S(2)}, u32[]{:S(2)}) collective-permute-start(bf16[512,256]{1,0:T(8,128)(2,1)S(1)} %convolution_convert_fusion.3), channel_id=1, source_target_pairs={{0,1},{1,2},{2,3},{3,4},{4,5},{5,6},{6,7},{7,8},{8,9},{9,10},{10,1... | collective-permute-start | bytes 786440 | tf_op jit(solution)/shard_map/ppermute | solution.py:14
  57.5 8.4 %collective-permute-start.3 = (bf16[512,256]{1,0:T(8,128)(2,1)S(1)}, bf16[512,256]{1,0:T(8,128)(2,1)S(1)}, u32[]{:S(2)}, u32[]{:S(2)}) collective-permute-start(bf16[512,256]{1,0:T(8,128)(2,1)S(1)} %convolution_convert_fusion.2), channel_id=1, source_target_pairs={{1,0},{2,1},{3,2},{4,3},{5,4},{6,5},{7,6},{8,7},{9,8},{10,9},{11,1... | collective-permute-start | bytes 786440 | tf_op jit(solution)/shard_map/ppermute | solution.py:17
  59.5 7.7 %collective-permute-start.2 = (bf16[512,256]{1,0:T(8,128)(2,1)S(1)}, bf16[512,256]{1,0:T(8,128)(2,1)S(1)}, u32[]{:S(2)}, u32[]{:S(2)}) collective-permute-start(bf16[512,256]{1,0:T(8,128)(2,1)S(1)} %convolution_convert_fusion.2), channel_id=1, source_target_pairs={{0,1},{1,2},{2,3},{3,4},{4,5},{5,6},{6,7},{7,8},{8,9},{9,10},{10,1... | collective-permute-start | bytes 786440 | tf_op jit(solution)/shard_map/ppermute | solution.py:14
  70.5 24.4 %all-to-all-start.1 = ((bf16[128,4,256]{2,1,0:T(4,128)(2,1)}), bf16[128,4,256]{2,1,0:T(4,128)(2,1)S(1)}, u32[]{:S(2)}, u32[]{:S(2)}) async-start(bf16[128,4,256]{2,1,0:T(4,128)(2,1)} %reshape.134), calls=%async_computation.1 | async-start | bytes 524288 | tf_op jit(solution)/shard_map/all_to_all | solution.py:115

commit v8 on v7

--- a/solution.py
+++ b/solution.py
@@ -115,11 +115,11 @@
     returned = lax.all_to_all(
         answers.reshape(device_count, DCAP, width), "nodes", split_axis=0, concat_axis=0, tiled=True
     ).reshape(remote_slots, width)
-    value = (
-        features.astype(jnp.float32)
-        + jnp.dot(local_hot, coarse, preferred_element_type=jnp.float32)
-        + jnp.dot(remote_hot, returned, preferred_element_type=jnp.float32)
-    )
+    table = jnp.concatenate([coarse, returned], axis=0)
+    column = jnp.where(remote, clusters_here + slot_column, lids)
+    columns = jnp.arange(clusters_here + remote_slots, dtype=jnp.int32)
+    one_hot = (column[:, None] == columns[None, :]).astype(jnp.bfloat16)
+    value = features.astype(jnp.float32) + jnp.dot(one_hot, table, preferred_element_type=jnp.float32)
     return value.astype(jnp.bfloat16)
 
 

time: 103 us -> 104 us (level)
  blocking collectives: 0 us -> 24.3 us
  starting transfers between devices: 37 us -> 23.4 us
  matrix products: 43.1 us -> 35.6 us
  waiting for transfers between devices: 15 us -> 13.7 us
    all_to_all x0 -> x1, blocking collectives: none -> 24.3 us  [local(): lax.all_to_all(answers.reshape(device_count, DCAP, width), 'nodes', split...]
    all_to_all x1 -> x0, starting transfers between devices: 13.6 us -> none  [local(): lax.all_to_all(answers.reshape(device_count, DCAP, width), 'nodes', split...]
    dot_general x2 -> x1, matrix products: 17.1 us -> 9.57 us  [local(): jnp.dot(one_hot, table, preferred_element_type=jnp.float32)]
    all_to_all x1 -> x0, waiting for transfers between devices: 1.32 us -> none  [local(): lax.all_to_all(answers.reshape(device_count, DCAP, width), 'nodes', split...]
  transfers between devices with their start and end apart: 6 -> 5, of which waited for: 6 -> 5; matrix products, arithmetic and copies ran while one was open for 16% -> 7% of each run, Pallas kernels for 0% -> 0%
where the time goes in v8:
time: 104 us
  matrix products  35.6 us (34%)
  blocking collectives  24.3 us (23%)
  starting transfers between devices  23.4 us (22%)
  waiting for transfers between devices  13.7 us (13%)
  local copies, waits for them, and re-layouts  4.14 us (4%)
  other arithmetic  2.31 us (2%)
    all_to_all x1, blocking collectives, local(): lax.all_to_all(answers.reshape(device_count, DCAP, width), 'nodes', split...  24.3 us
    all_to_all x1, starting transfers between devices, local(): lax.all_to_all(payload.reshape(device_count, 1, -1), 'nodes', split_axis=...  11.5 us
    dot_general x1, matrix products, local(): jnp.dot(one_hot, table, preferred_element_type=jnp.float32)  9.57 us
    dot_general x1, matrix products, local(): lax.dot_general(remote_hot, features, contract_rows, preferred_element_ty...  8 us
    all_to_all x1, waiting for transfers between devices, local(): lax.all_to_all(payload.reshape(device_count, 1, -1), 'nodes', split_axis=...  7.24 us
    ppermute x2, starting transfers between devices, with_halo(): lax.ppermute(lax.slice_in_dim(block, block.shape[dim] - width, None, axis...  6.95 us
    dot_general x1, matrix products, local(): lax.dot_general(local_hot, features, contract_rows, preferred_element_typ...  6.81 us
    ppermute x2, starting transfers between devices, with_halo(): lax.ppermute(lax.slice_in_dim(block, 0, width, axis=dim), axis, backward)  4.93 us
  transfers between devices with their start and end apart: 5, of which 5 were waited for; matrix products, arithmetic and copies ran while one was open for 7% of the time, Pallas kernels for 0%

profile of v8, /device:TPU:1, one launch (start us, length us, event | category | flops | bytes accessed | tf_op | source)
XLA Modules:
  0.0 103.8 jit_solution(16676749263319488082)
XLA Ops:
  0.0 0.8 multiply_subtract_fusion
  0.8 4.3 %broadcast_compare_fusion = (pred[128,512]{1,0:T(32,128)(4,1)S(1)}, f32[128,512]{1,0:T(8,128)S(1)}) fusion(s32[8192]{0:T(1024)S(1)} %get-tuple-element.20, s32[8192]{0:T(1024)S(1)} %get-tuple-element.21), kind=kOutput, calls=%fused_computation.66 | convolution fusion | flops 1079050240 | bytes 393216 | tf_op jit(solution)/shard_map/dot_general | solution.py:37
  5.2 0.6 select_reduce_fusion.1
  7.2 1.3 %convolution_convert_fusion = s32[8192,8]{0,1:T(8,128)S(1)} fusion(s32[8192]{0:T(1024)S(1)} %get-tuple-element.21, bf16[128,4]{0,1:T(4,128)(2,1)S(1)} %get-tuple-element.23, bf16[128,4]{0,1:T(4,128)(2,1)S(1)} %get-tuple-element.24), kind=kOutput, calls=%fused_computation.12 | convolution fusion | flops 17895424 | bytes 296960 | tf_op jit(solution)/shard_map/dot_general | solution.py:70
  8.7 8.0 %fusion.4 = f32[512,256]{1,0:T(8,128)S(1)} fusion(bf16[8192,256]{1,0:T(8,128)(2,1)} %param.7, s32[8192]{0:T(1024)S(1)} %get-tuple-element.14), kind=kOutput, calls=%fused_computation.9 | convolution fusion | flops 2151677952 | bytes 4751360 | tf_op jit(solution)/shard_map/dot_general | solution.py:79
  17.0 1.2 %reshape.130 = f32[128,1,1152]{2,1,0:T(1,128)} reshape(f32[128,1152]{1,0:T(8,128)S(1)} %concatenate.17) | data formatting | bytes 1179648 | tf_op jit(solution)/shard_map/reshape | solution.py:90
  18.3 11.5 %all-to-all-start = ((f32[128,1,1152]{2,1,0:T(1,128)}), f32[128,1,1152]{2,1,0:T(1,128)S(1)}, u32[]{:S(2)}, u32[]{:S(2)}) async-start(f32[128,1,1152]{2,1,0:T(1,128)} %reshape.130), calls=%async_computation | async-start | bytes 1179648 | tf_op jit(solution)/shard_map/all_to_all | solution.py:89
  29.8 6.8 %fusion.8 = f32[512,256]{1,0:T(8,128)S(1)} fusion(bf16[8192,256]{1,0:T(8,128)(2,1)} %param.7, s32[8192]{0:T(1024)S(1)} %get-tuple-element.20, pred[8192]{0:T(1024)(128)(4,1)S(1)} %get-tuple-element.15), kind=kOutput, calls=%fused_computation.14 | convolution fusion | flops 2160066560 | bytes 4759552 | tf_op jit(solution)/shard_map/dot_general | solution.py:95
  36.7 7.2 %all-to-all-done = f32[128,1,1152]{2,1,0:T(1,128)S(1)} async-done(((f32[128,1,1152]{2,1,0:T(1,128)}), f32[128,1,1152]{2,1,0:T(1,128)S(1)}, u32[]{:S(2)}, u32[]{:S(2)}) %all-to-all-start) | async-done | bytes 589856 | tf_op jit(solution)/shard_map/all_to_all | solution.py:89
  44.7 1.1 %fusion.19 = bf16[512,256]{1,0:T(8,128)(2,1)S(1)} fusion(f32[512,256]{1,0:T(8,128)S(1)} %fusion.8, f32[512,256]{1,0:T(8,128)S(1)} %reshape.132, s32[512]{0:T(512)S(1)} %convert_element_type.70, f32[512]{0:T(512)S(1)} %add_sqrt_fusion), kind=kOutput, calls=%fused_computation.28 | convolution fusion | flops 805961728 | bytes 1314816 | tf_op jit(solution)/shard_map/dot_general | solution.py:100
  46.1 3.0 %collective-permute-start.1 = (bf16[512,256]{1,0:T(8,128)(2,1)S(1)}, bf16[512,256]{1,0:T(8,128)(2,1)S(1)}, u32[]{:S(2)}, u32[]{:S(2)}) collective-permute-start(bf16[512,256]{1,0:T(8,128)(2,1)S(1)} %convolution_convert_fusion.3), channel_id=1, source_target_pairs={{1,0},{2,1},{3,2},{4,3},{5,4},{6,5},{7,6},{8,7},{9,8},{10,9},{11,1... | collective-permute-start | bytes 786440 | tf_op jit(solution)/shard_map/ppermute | solution.py:17
  49.1 2.6 %collective-permute-start = (bf16[512,256]{1,0:T(8,128)(2,1)S(1)}, bf16[512,256]{1,0:T(8,128)(2,1)S(1)}, u32[]{:S(2)}, u32[]{:S(2)}) collective-permute-start(bf16[512,256]{1,0:T(8,128)(2,1)S(1)} %convolution_convert_fusion.3), channel_id=1, source_target_pairs={{0,1},{1,2},{2,3},{3,4},{4,5},{5,6},{6,7},{7,8},{8,9},{9,10},{10,1... | collective-permute-start | bytes 786440 | tf_op jit(solution)/shard_map/ppermute | solution.py:14
  51.8 2.0 %collective-permute-done.1 = bf16[512,256]{1,0:T(8,128)(2,1)S(1)} collective-permute-done((bf16[512,256]{1,0:T(8,128)(2,1)S(1)}, bf16[512,256]{1,0:T(8,128)(2,1)S(1)}, u32[]{:S(2)}, u32[]{:S(2)}) %collective-permute-start.1) | collective-permute-done | bytes 262176 | tf_op jit(solution)/shard_map/ppermute | solution.py:17
  53.8 1.2 %collective-permute-done = bf16[512,256]{1,0:T(8,128)(2,1)S(1)} collective-permute-done((bf16[512,256]{1,0:T(8,128)(2,1)S(1)}, bf16[512,256]{1,0:T(8,128)(2,1)S(1)}, u32[]{:S(2)}, u32[]{:S(2)}) %collective-permute-start) | collective-permute-done | bytes 262176 | tf_op jit(solution)/shard_map/ppermute | solution.py:14
  55.1 0.6 gather_fusion
  55.7 1.6 %fusion.21 = bf16[4,128,256]{2,1,0:T(8,128)(2,1)S(1)} fusion(bf16[4,6,128,256]{3,2,1,0:T(8,128)(2,1)S(1)} %bitcast.50, bf16[4,6,128,128]{3,2,1,0:T(8,128)(2,1)} %param.11, pred[4,6]{1,0:T(4,128)(4,1)S(1)} %iota_compare_fusion.17), kind=kOutput, calls=%fused_computation.33 | convolution fusion | flops 201981952 | bytes 2621464 | tf_op jit(solution)/shard_map/tkij,tkjf->tif/dot_general | solution.py:31
  57.5 1.9 %collective-permute-start.3 = (bf16[512,256]{1,0:T(8,128)(2,1)S(1)}, bf16[512,256]{1,0:T(8,128)(2,1)S(1)}, u32[]{:S(2)}, u32[]{:S(2)}) collective-permute-start(bf16[512,256]{1,0:T(8,128)(2,1)S(1)} %convolution_convert_fusion.2), channel_id=1, source_target_pairs={{1,0},{2,1},{3,2},{4,3},{5,4},{6,5},{7,6},{8,7},{9,8},{10,9},{11,1... | collective-permute-start | bytes 786440 | tf_op jit(solution)/shard_map/ppermute | solution.py:17
  59.4 4.4 %collective-permute-start.2 = (bf16[512,256]{1,0:T(8,128)(2,1)S(1)}, bf16[512,256]{1,0:T(8,128)(2,1)S(1)}, u32[]{:S(2)}, u32[]{:S(2)}) collective-permute-start(bf16[512,256]{1,0:T(8,128)(2,1)S(1)} %convolution_convert_fusion.2), channel_id=1, source_target_pairs={{0,1},{1,2},{2,3},{3,4},{4,5},{5,6},{6,7},{7,8},{8,9},{9,10},{10,1... | collective-permute-start | bytes 786440 | tf_op jit(solution)/shard_map/ppermute | solution.py:14
  63.8 2.1 %collective-permute-done.3 = bf16[512,256]{1,0:T(8,128)(2,1)S(1)} collective-permute-done((bf16[512,256]{1,0:T(8,128)(2,1)S(1)}, bf16[512,256]{1,0:T(8,128)(2,1)S(1)}, u32[]{:S(2)}, u32[]{:S(2)}) %collective-permute-start.3) | collective-permute-done | bytes 262176 | tf_op jit(solution)/shard_map/ppermute | solution.py:17
  66.0 1.2 %collective-permute-done.2 = bf16[512,256]{1,0:T(8,128)(2,1)S(1)} collective-permute-done((bf16[512,256]{1,0:T(8,128)(2,1)S(1)}, bf16[512,256]{1,0:T(8,128)(2,1)S(1)}, u32[]{:S(2)}, u32[]{:S(2)}) %collective-permute-start.2) | collective-permute-done | bytes 262176 | tf_op jit(solution)/shard_map/ppermute | solution.py:14
  67.2 0.6 gather_fusion.1
  67.9 1.6 %fusion.20 = bf16[4,128,256]{2,1,0:T(8,128)(2,1)S(1)} fusion(bf16[4,6,128,256]{3,2,1,0:T(8,128)(2,1)S(1)} %bitcast.49, bf16[4,6,128,128]{3,2,1,0:T(8,128)(2,1)} %param.11, pred[4,6]{1,0:T(4,128)(4,1)S(1)} %iota_compare_fusion.17), kind=kOutput, calls=%fused_computation.29 | convolution fusion | flops 201850880 | bytes 2621464 | tf_op jit(solution)/shard_map/tkij,tkjf->tif/dot_general | solution.py:31
  69.8 24.3 %all_to_all.10 = bf16[128,4,256]{2,1,0:T(4,128)(2,1)S(1)} all-to-all(bf16[128,4,256]{2,1,0:T(4,128)(2,1)S(1)} %reshape.135), channel_id=1, replica_groups=mesh['nodes'=128] {'nodes'}, dimensions={0} | all-to-all | bytes 524288 | tf_op jit(solution)/shard_map/all_to_all | solution.py:115
  94.2 9.6 %fusion.6 = bf16[8192,256]{1,0:T(8,128)(2,1)} fusion(s32[8192]{0:T(1024)S(1)} %get-tuple-element.13, bf16[8192,256]{1,0:T(8,128)(2,1)} %param.7, bf16[512,256]{1,0:T(8,128)(2,1)S(1)} %reshape.136, bf16[512,256]{1,0:T(8,128)(2,1)S(1)} %bitcast.58), kind=kOutput, calls=%fused_computation.11 | convolution fusion | flops 4310695936 | bytes 8945664 | tf_op jit(solution)/shard_map/dot_general | solution.py:122
  (53 shorter events, 3.9 us)
Async XLA Ops:
  0.0 45.9 %copy-start = (bf16[256,256]{1,0:T(8,128)(2,1)S(1)}, bf16[256,256]{1,0:T(8,128)(2,1)}, u32[]{:S(2)}) copy-start(bf16[256,256]{1,0:T(8,128)(2,1)} %param.12) | copy-start | bytes 393220
  5.2 3.5 %copy-start.2 = (s32[8192]{0:T(1024)S(1)}, s32[8192]{0:T(1024)}, u32[]{:S(2)}) copy-start(s32[8192]{0:T(1024)} %param.8) | copy-start | bytes 98308
  18.3 25.7 %all-to-all-start = ((f32[128,1,1152]{2,1,0:T(1,128)}), f32[128,1,1152]{2,1,0:T(1,128)S(1)}, u32[]{:S(2)}, u32[]{:S(2)}) async-start(f32[128,1,1152]{2,1,0:T(1,128)} %reshape.130), calls=%async_computation | async-start | bytes 1179648 | tf_op jit(solution)/shard_map/all_to_all | solution.py:89
  29.8 6.9 %copy-start.3 = (s32[4,6]{1,0:T(4,128)S(1)}, s32[4,6]{1,0:T(4,128)}, u32[]{:S(2)}) copy-start(s32[4,6]{1,0:T(4,128)} %param.9) | copy-start | bytes 292
  36.6 15.1 %copy-start.4 = (s32[4]{0:T(128)S(1)}, s32[4]{0:T(128)}, u32[]{:S(2)}) copy-start(s32[4]{0:T(128)} %param.10) | copy-start | bytes 52
  45.9 11.4 %copy-start.1 = (bf16[256,256]{1,0:T(8,128)(2,1)S(1)}, bf16[256,256]{1,0:T(8,128)(2,1)}, u32[]{:S(2)}) copy-start(bf16[256,256]{1,0:T(8,128)(2,1)} %param.13) | copy-start | bytes 393220
  46.1 7.7 %collective-permute-start.1 = (bf16[512,256]{1,0:T(8,128)(2,1)S(1)}, bf16[512,256]{1,0:T(8,128)(2,1)S(1)}, u32[]{:S(2)}, u32[]{:S(2)}) collective-permute-start(bf16[512,256]{1,0:T(8,128)(2,1)S(1)} %convolution_convert_fusion.3), channel_id=1, source_target_pairs={{1,0},{2,1},{3,2},{4,3},{5,4},{6,5},{7,6},{8,7},{9,8},{10,9},{11,1... | collective-permute-start | bytes 786440 | tf_op jit(solution)/shard_map/ppermute | solution.py:17
  49.1 5.9 %collective-permute-start = (bf16[512,256]{1,0:T(8,128)(2,1)S(1)}, bf16[512,256]{1,0:T(8,128)(2,1)S(1)}, u32[]{:S(2)}, u32[]{:S(2)}) collective-permute-start(bf16[512,256]{1,0:T(8,128)(2,1)S(1)} %convolution_convert_fusion.3), channel_id=1, source_target_pairs={{0,1},{1,2},{2,3},{3,4},{4,5},{5,6},{6,7},{7,8},{8,9},{9,10},{10,1... | collective-permute-start | bytes 786440 | tf_op jit(solution)/shard_map/ppermute | solution.py:14
  57.5 8.4 %collective-permute-start.3 = (bf16[512,256]{1,0:T(8,128)(2,1)S(1)}, bf16[512,256]{1,0:T(8,128)(2,1)S(1)}, u32[]{:S(2)}, u32[]{:S(2)}) collective-permute-start(bf16[512,256]{1,0:T(8,128)(2,1)S(1)} %convolution_convert_fusion.2), channel_id=1, source_target_pairs={{1,0},{2,1},{3,2},{4,3},{5,4},{6,5},{7,6},{8,7},{9,8},{10,9},{11,1... | collective-permute-start | bytes 786440 | tf_op jit(solution)/shard_map/ppermute | solution.py:17
  59.4 7.7 %collective-permute-start.2 = (bf16[512,256]{1,0:T(8,128)(2,1)S(1)}, bf16[512,256]{1,0:T(8,128)(2,1)S(1)}, u32[]{:S(2)}, u32[]{:S(2)}) collective-permute-start(bf16[512,256]{1,0:T(8,128)(2,1)S(1)} %convolution_convert_fusion.2), channel_id=1, source_target_pairs={{0,1},{1,2},{2,3},{3,4},{4,5},{5,6},{6,7},{7,8},{8,9},{9,10},{10,1... | collective-permute-start | bytes 786440 | tf_op jit(solution)/shard_map/ppermute | solution.py:14

commit v9 on v8

--- a/solution.py
+++ b/solution.py
@@ -1,9 +1,37 @@
 import jax
 import jax.numpy as jnp
 from jax import lax
+from jax.experimental import pallas as pl
 from jax.sharding import PartitionSpec as P
 
 DCAP = 4
+
+
+def unpool_kernel(col_ref, x_ref, table_ref, out_ref):
+    cols = lax.broadcasted_iota(jnp.int32, (col_ref.shape[0], table_ref.shape[0]), 1)
+    one_hot = (col_ref[...] == cols).astype(table_ref.dtype)
+    picked = jnp.dot(one_hot, table_ref[...], preferred_element_type=jnp.float32)
+    out_ref[...] = (x_ref[...].astype(jnp.float32) + picked).astype(out_ref.dtype)
+
+
+def add_rows(column, rows, table, block=512):
+    count, width = rows.shape
+    return pl.pallas_call(
+        unpool_kernel,
+        grid=(count // block,),
+        in_specs=[
+            pl.BlockSpec((block, 1), lambda i: (i, 0)),
+            pl.BlockSpec((block, width), lambda i: (i, 0)),
+            pl.BlockSpec(table.shape, lambda i: (0, 0)),
+        ],
+        out_specs=pl.BlockSpec((block, width), lambda i: (i, 0)),
+        out_shape=jax.ShapeDtypeStruct(rows.shape, rows.dtype),
+        cost_estimate=pl.CostEstimate(
+            flops=2 * count * table.shape[0] * width,
+            transcendentals=0,
+            bytes_accessed=4 * count * width + 4 * count + 2 * table.size,
+        ),
+    )(column.reshape(count, 1), rows, table)
 
 
 def with_halo(block, sides, width):
@@ -115,12 +143,8 @@
     returned = lax.all_to_all(
         answers.reshape(device_count, DCAP, width), "nodes", split_axis=0, concat_axis=0, tiled=True
     ).reshape(remote_slots, width)
-    table = jnp.concatenate([coarse, returned], axis=0)
-    column = jnp.where(remote, clusters_here + slot_column, lids)
-    columns = jnp.arange(clusters_here + remote_slots, dtype=jnp.int32)
-    one_hot = (column[:, None] == columns[None, :]).astype(jnp.bfloat16)
-    value = features.astype(jnp.float32) + jnp.dot(one_hot, table, preferred_element_type=jnp.float32)
-    return value.astype(jnp.bfloat16)
+    first = add_rows(jnp.where(remote, -1, lids), features, coarse)
+    return add_rows(slot_column, first, returned)
 
 
 def solution(mesh):

time: 104 us -> 116 us (1.12)
  Pallas kernels: 0 us -> 26.8 us
  blocking collectives: 24.3 us -> 0 us
  starting transfers between devices: 23.4 us -> 37 us
  matrix products: 35.6 us -> 23.8 us
  local copies, waits for them, and re-layouts: 4.14 us -> 10.8 us
    pallas_call x0 -> x2, Pallas kernels: none -> 26.8 us  [add_rows(): pl.pallas_call(unpool_kernel, grid=(count // block,), in_specs=[pl.BlockS...]
    all_to_all x1 -> x0, blocking collectives: 24.3 us -> none  [local(): lax.all_to_all(answers.reshape(device_count, DCAP, width), 'nodes', split...]
    all_to_all x0 -> x1, starting transfers between devices: none -> 13.6 us  [local(): lax.all_to_all(answers.reshape(device_count, DCAP, width), 'nodes', split...]
    dot_general x1 -> x0, matrix products: 9.57 us -> none  [local(): jnp.dot(one_hot, table, preferred_element_type=jnp.float32)]
    reshape x0 -> x2, local copies, waits for them, and re-layouts: none -> 5.27 us  [add_rows(): column.reshape(count, 1)]
    dot_general x2, matrix products: 3.13 us -> 0.87 us  [convolve(): jnp.einsum('tkij,tkjf->tif', weights, picked, preferred_element_type=jnp....]
  transfers between devices with their start and end apart: 5 -> 6, of which waited for: 5 -> 5; matrix products, arithmetic and copies ran while one was open for 7% -> 11% of each run, Pallas kernels for 0% -> 12%
where the time goes in v9:
time: 116 us; the launch traced here: 115 us
  starting transfers between devices  37 us (32%)
  Pallas kernels  26.8 us (23%)
  matrix products  23.8 us (21%)
  waiting for transfers between devices  13.7 us (12%)
  local copies, waits for them, and re-layouts  10.8 us (9%)
  other arithmetic  2.3 us (2%)
    pallas_call x2, Pallas kernels, add_rows(): pl.pallas_call(unpool_kernel, grid=(count // block,), in_specs=[pl.BlockS...  26.8 us
    all_to_all x1, starting transfers between devices, local(): lax.all_to_all(answers.reshape(device_count, DCAP, width), 'nodes', split...  13.6 us
    all_to_all x1, starting transfers between devices, local(): lax.all_to_all(payload.reshape(device_count, 1, -1), 'nodes', split_axis=...  11.5 us
    dot_general x1, matrix products, local(): lax.dot_general(remote_hot, features, contract_rows, preferred_element_ty...  8 us
    all_to_all x1, waiting for transfers between devices, local(): lax.all_to_all(payload.reshape(device_count, 1, -1), 'nodes', split_axis=...  7.24 us
    ppermute x2, starting transfers between devices, with_halo(): lax.ppermute(lax.slice_in_dim(block, block.shape[dim] - width, None, axis...  6.93 us
    dot_general x1, matrix products, local(): lax.dot_general(local_hot, features, contract_rows, preferred_element_typ...  6.81 us
    reshape x2, local copies, waits for them, and re-layouts, add_rows(): column.reshape(count, 1)  5.27 us
  transfers between devices with their start and end apart: 6, of which 5 were waited for; matrix products, arithmetic and copies ran while one was open for 11% of the time, Pallas kernels for 12%

profile of v9, /device:TPU:1, one launch (start us, length us, event | category | flops | bytes accessed | tf_op | source)
XLA Modules:
  0.0 114.8 jit_solution(16415688199177876169)
XLA Ops:
  0.0 0.8 broadcast_select_fusion.3
  0.8 4.3 %broadcast_compare_fusion = (pred[128,512]{1,0:T(32,128)(4,1)S(1)}, f32[128,512]{1,0:T(8,128)S(1)}) fusion(s32[8192]{0:T(1024)S(1)} %get-tuple-element.19, s32[8192]{0:T(1024)S(1)} %get-tuple-element.20), kind=kOutput, calls=%fused_computation.58 | convolution fusion | flops 1079050240 | bytes 393216 | tf_op jit(solution)/shard_map/dot_general | solution.py:65
  7.2 1.3 %convolution_convert_fusion = s32[8192,8]{0,1:T(8,128)S(1)} fusion(s32[8192]{0:T(1024)S(1)} %get-tuple-element.20, bf16[128,4]{0,1:T(4,128)(2,1)S(1)} %get-tuple-element.22, bf16[128,4]{0,1:T(4,128)(2,1)S(1)} %get-tuple-element.23), kind=kOutput, calls=%fused_computation.7 | convolution fusion | flops 17895424 | bytes 296960 | tf_op jit(solution)/shard_map/dot_general | solution.py:98
  8.7 8.0 %fusion.2 = f32[512,256]{1,0:T(8,128)S(1)} fusion(bf16[8192,256]{1,0:T(8,128)(2,1)} %x_ref.1, s32[8192]{0:T(1024)S(1)} %add_select_fusion.1), kind=kOutput, calls=%fused_computation.6 | convolution fusion | flops 2151677952 | bytes 4751360 | tf_op jit(solution)/shard_map/dot_general | solution.py:107
  17.0 1.2 %reshape.137 = f32[128,1,1152]{2,1,0:T(1,128)} reshape(f32[128,1152]{1,0:T(8,128)S(1)} %concatenate.14) | data formatting | bytes 1179648 | tf_op jit(solution)/shard_map/reshape | solution.py:118
  18.3 11.5 %all-to-all-start = ((f32[128,1,1152]{2,1,0:T(1,128)}), f32[128,1,1152]{2,1,0:T(1,128)S(1)}, u32[]{:S(2)}, u32[]{:S(2)}) async-start(f32[128,1,1152]{2,1,0:T(1,128)} %reshape.137), calls=%async_computation | async-start | bytes 1179648 | tf_op jit(solution)/shard_map/all_to_all | solution.py:117
  29.8 6.8 %fusion.4 = f32[512,256]{1,0:T(8,128)S(1)} fusion(bf16[8192,256]{1,0:T(8,128)(2,1)} %x_ref.1, s32[8192]{0:T(1024)S(1)} %get-tuple-element.19, pred[8192]{0:T(1024)(128)(4,1)S(1)} %get-tuple-element.14), kind=kOutput, calls=%fused_computation.9 | convolution fusion | flops 2160066560 | bytes 4759552 | tf_op jit(solution)/shard_map/dot_general | solution.py:123
  36.7 7.2 %all-to-all-done = f32[128,1,1152]{2,1,0:T(1,128)S(1)} async-done(((f32[128,1,1152]{2,1,0:T(1,128)}), f32[128,1,1152]{2,1,0:T(1,128)S(1)}, u32[]{:S(2)}, u32[]{:S(2)}) %all-to-all-start) | async-done | bytes 589856 | tf_op jit(solution)/shard_map/all_to_all | solution.py:117
  44.8 1.1 fusion.15
  46.1 3.0 %collective-permute-start.1 = (bf16[512,256]{1,0:T(8,128)(2,1)S(1)}, bf16[512,256]{1,0:T(8,128)(2,1)S(1)}, u32[]{:S(2)}, u32[]{:S(2)}) collective-permute-start(bf16[512,256]{1,0:T(8,128)(2,1)S(1)} %convolution_convert_fusion.3), channel_id=1, source_target_pairs={{1,0},{2,1},{3,2},{4,3},{5,4},{6,5},{7,6},{8,7},{9,8},{10,9},{11,1... | collective-permute-start | bytes 786440 | tf_op jit(solution)/shard_map/ppermute | solution.py:45
  49.2 2.5 %collective-permute-start = (bf16[512,256]{1,0:T(8,128)(2,1)S(1)}, bf16[512,256]{1,0:T(8,128)(2,1)S(1)}, u32[]{:S(2)}, u32[]{:S(2)}) collective-permute-start(bf16[512,256]{1,0:T(8,128)(2,1)S(1)} %convolution_convert_fusion.3), channel_id=1, source_target_pairs={{0,1},{1,2},{2,3},{3,4},{4,5},{5,6},{6,7},{7,8},{8,9},{9,10},{10,1... | collective-permute-start | bytes 786440 | tf_op jit(solution)/shard_map/ppermute | solution.py:42
  51.8 2.0 %collective-permute-done.1 = bf16[512,256]{1,0:T(8,128)(2,1)S(1)} collective-permute-done((bf16[512,256]{1,0:T(8,128)(2,1)S(1)}, bf16[512,256]{1,0:T(8,128)(2,1)S(1)}, u32[]{:S(2)}, u32[]{:S(2)}) %collective-permute-start.1) | collective-permute-done | bytes 262176 | tf_op jit(solution)/shard_map/ppermute | solution.py:45
  53.8 1.2 %collective-permute-done = bf16[512,256]{1,0:T(8,128)(2,1)S(1)} collective-permute-done((bf16[512,256]{1,0:T(8,128)(2,1)S(1)}, bf16[512,256]{1,0:T(8,128)(2,1)S(1)}, u32[]{:S(2)}, u32[]{:S(2)}) %collective-permute-start) | collective-permute-done | bytes 262176 | tf_op jit(solution)/shard_map/ppermute | solution.py:42
  56.4 1.9 %collective-permute-start.3 = (bf16[512,256]{1,0:T(8,128)(2,1)S(1)}, bf16[512,256]{1,0:T(8,128)(2,1)S(1)}, u32[]{:S(2)}, u32[]{:S(2)}) collective-permute-start(bf16[512,256]{1,0:T(8,128)(2,1)S(1)} %convolution_convert_fusion.2), channel_id=1, source_target_pairs={{1,0},{2,1},{3,2},{4,3},{5,4},{6,5},{7,6},{8,7},{9,8},{10,9},{11,1... | collective-permute-start | bytes 786440 | tf_op jit(solution)/shard_map/ppermute | solution.py:45
  58.3 4.4 %collective-permute-start.2 = (bf16[512,256]{1,0:T(8,128)(2,1)S(1)}, bf16[512,256]{1,0:T(8,128)(2,1)S(1)}, u32[]{:S(2)}, u32[]{:S(2)}) collective-permute-start(bf16[512,256]{1,0:T(8,128)(2,1)S(1)} %convolution_convert_fusion.2), channel_id=1, source_target_pairs={{0,1},{1,2},{2,3},{3,4},{4,5},{5,6},{6,7},{7,8},{8,9},{9,10},{10,1... | collective-permute-start | bytes 786440 | tf_op jit(solution)/shard_map/ppermute | solution.py:42
  62.7 2.1 %collective-permute-done.3 = bf16[512,256]{1,0:T(8,128)(2,1)S(1)} collective-permute-done((bf16[512,256]{1,0:T(8,128)(2,1)S(1)}, bf16[512,256]{1,0:T(8,128)(2,1)S(1)}, u32[]{:S(2)}, u32[]{:S(2)}) %collective-permute-start.3) | collective-permute-done | bytes 262176 | tf_op jit(solution)/shard_map/ppermute | solution.py:45
  64.8 1.2 %collective-permute-done.2 = bf16[512,256]{1,0:T(8,128)(2,1)S(1)} collective-permute-done((bf16[512,256]{1,0:T(8,128)(2,1)S(1)}, bf16[512,256]{1,0:T(8,128)(2,1)S(1)}, u32[]{:S(2)}, u32[]{:S(2)}) %collective-permute-start.2) | collective-permute-done | bytes 262176 | tf_op jit(solution)/shard_map/ppermute | solution.py:42
  67.5 0.8 reshape.142
  68.3 13.6 %all-to-all-start.1 = ((bf16[128,4,256]{2,1,0:T(4,128)(2,1)}), bf16[128,4,256]{2,1,0:T(4,128)(2,1)S(1)}, u32[]{:S(2)}, u32[]{:S(2)}) async-start(bf16[128,4,256]{2,1,0:T(4,128)(2,1)} %reshape.142), calls=%async_computation.1 | async-start | bytes 524288 | tf_op jit(solution)/shard_map/all_to_all | solution.py:143
  81.9 2.7 %copy.32.col_ref = s32[8192,1]{1,0:T(8,128)} copy(s32[8192,1]{0,1:T(1,128)S(1)} %bitcast.56) | data formatting | bytes 65536 | tf_op jit(solution)/shard_map/reshape | solution.py:34
  84.6 2.6 %copy.33.col_ref = s32[8192,1]{1,0:T(8,128)} copy(s32[8192,1]{0,1:T(1,128)S(1)} %bitcast.57) | data formatting | bytes 65536 | tf_op jit(solution)/shard_map/reshape | solution.py:34
  87.2 13.4 %shard_map.73.x_ref = bf16[8192,256]{1,0:T(8,128)(2,1)} custom-call(s32[8192,1]{1,0:T(8,128)} %copy.32.col_ref, bf16[8192,256]{1,0:T(8,128)(2,1)} %x_ref.1, bf16[512,256]{1,0:T(8,128)(2,1)} %bitcast.54), custom_call_target="tpu_custom_call" | custom-call | flops 2147483648 | bytes 8683520 | tf_op jit(solution)/shard_map/pallas_call | solution.py:19
  100.6 0.8 reshape.143.table_ref
  101.4 13.4 %shard_map.74 = bf16[8192,256]{1,0:T(8,128)(2,1)} custom-call(s32[8192,1]{1,0:T(8,128)} %copy.33.col_ref, bf16[8192,256]{1,0:T(8,128)(2,1)} %shard_map.73.x_ref, bf16[512,256]{1,0:T(8,128)(2,1)} %reshape.143.table_ref), custom_call_target="tpu_custom_call" | custom-call | flops 2147483648 | bytes 8683520 | tf_op jit(solution)/shard_map/pallas_call | solution.py:19
  (61 shorter events, 6.5 us)
Async XLA Ops:
  0.0 45.9 %copy-start = (bf16[256,256]{1,0:T(8,128)(2,1)S(1)}, bf16[256,256]{1,0:T(8,128)(2,1)}, u32[]{:S(2)}) copy-start(bf16[256,256]{1,0:T(8,128)(2,1)} %param.12) | copy-start | bytes 393220
  5.2 3.5 %copy-start.3 = (s32[8192]{0:T(1024)S(1)}, s32[8192]{0:T(1024)}, u32[]{:S(2)}) copy-start(s32[8192]{0:T(1024)} %param.8) | copy-start | bytes 98308
  18.3 25.7 %all-to-all-start = ((f32[128,1,1152]{2,1,0:T(1,128)}), f32[128,1,1152]{2,1,0:T(1,128)S(1)}, u32[]{:S(2)}, u32[]{:S(2)}) async-start(f32[128,1,1152]{2,1,0:T(1,128)} %reshape.137), calls=%async_computation | async-start | bytes 1179648 | tf_op jit(solution)/shard_map/all_to_all | solution.py:117
  29.8 6.8 %copy-start.4 = (s32[4,6]{1,0:T(4,128)S(1)}, s32[4,6]{1,0:T(4,128)}, u32[]{:S(2)}) copy-start(s32[4,6]{1,0:T(4,128)} %param.9) | copy-start | bytes 292
  36.6 15.1 %copy-start.6 = (s32[4]{0:T(128)S(1)}, s32[4]{0:T(128)}, u32[]{:S(2)}) copy-start(s32[4]{0:T(128)} %param.10) | copy-start | bytes 52
  44.3 11.4 %copy-start.5 = (bf16[4,6,128,128]{3,2,1,0:T(8,128)(2,1)S(1)}, bf16[4,6,128,128]{3,2,1,0:T(8,128)(2,1)}, u32[]{:S(2)}) copy-start(bf16[4,6,128,128]{3,2,1,0:T(8,128)(2,1)} %param.11) | copy-start | bytes 2359300
  45.9 10.3 %copy-start.2 = (bf16[256,256]{1,0:T(8,128)(2,1)S(1)}, bf16[256,256]{1,0:T(8,128)(2,1)}, u32[]{:S(2)}) copy-start(bf16[256,256]{1,0:T(8,128)(2,1)} %param.13) | copy-start | bytes 393220
  46.1 7.7 %collective-permute-start.1 = (bf16[512,256]{1,0:T(8,128)(2,1)S(1)}, bf16[512,256]{1,0:T(8,128)(2,1)S(1)}, u32[]{:S(2)}, u32[]{:S(2)}) collective-permute-start(bf16[512,256]{1,0:T(8,128)(2,1)S(1)} %convolution_convert_fusion.3), channel_id=1, source_target_pairs={{1,0},{2,1},{3,2},{4,3},{5,4},{6,5},{7,6},{8,7},{9,8},{10,9},{11,1... | collective-permute-start | bytes 786440 | tf_op jit(solution)/shard_map/ppermute | solution.py:45
  49.2 5.8 %collective-permute-start = (bf16[512,256]{1,0:T(8,128)(2,1)S(1)}, bf16[512,256]{1,0:T(8,128)(2,1)S(1)}, u32[]{:S(2)}, u32[]{:S(2)}) collective-permute-start(bf16[512,256]{1,0:T(8,128)(2,1)S(1)} %convolution_convert_fusion.3), channel_id=1, source_target_pairs={{0,1},{1,2},{2,3},{3,4},{4,5},{5,6},{6,7},{7,8},{8,9},{9,10},{10,1... | collective-permute-start | bytes 786440 | tf_op jit(solution)/shard_map/ppermute | solution.py:42
  56.4 8.4 %collective-permute-start.3 = (bf16[512,256]{1,0:T(8,128)(2,1)S(1)}, bf16[512,256]{1,0:T(8,128)(2,1)S(1)}, u32[]{:S(2)}, u32[]{:S(2)}) collective-permute-start(bf16[512,256]{1,0:T(8,128)(2,1)S(1)} %convolution_convert_fusion.2), channel_id=1, source_target_pairs={{1,0},{2,1},{3,2},{4,3},{5,4},{6,5},{7,6},{8,7},{9,8},{10,9},{11,1... | collective-permute-start | bytes 786440 | tf_op jit(solution)/shard_map/ppermute | solution.py:45
  58.3 7.7 %collective-permute-start.2 = (bf16[512,256]{1,0:T(8,128)(2,1)S(1)}, bf16[512,256]{1,0:T(8,128)(2,1)S(1)}, u32[]{:S(2)}, u32[]{:S(2)}) collective-permute-start(bf16[512,256]{1,0:T(8,128)(2,1)S(1)} %convolution_convert_fusion.2), channel_id=1, source_target_pairs={{0,1},{1,2},{2,3},{3,4},{4,5},{5,6},{6,7},{7,8},{8,9},{9,10},{10,1... | collective-permute-start | bytes 786440 | tf_op jit(solution)/shard_map/ppermute | solution.py:42
  67.2 20.0 %copy-start.1 = (bf16[4,128,256]{2,1,0:T(8,128)(2,1)}, bf16[4,128,256]{2,1,0:T(8,128)(2,1)S(1)}, u32[]{:S(2)}) copy-start(bf16[4,128,256]{2,1,0:T(8,128)(2,1)S(1)} %fusion.16) | copy-start | bytes 786436
  68.3 32.3 %all-to-all-start.1 = ((bf16[128,4,256]{2,1,0:T(4,128)(2,1)}), bf16[128,4,256]{2,1,0:T(4,128)(2,1)S(1)}, u32[]{:S(2)}, u32[]{:S(2)}) async-start(bf16[128,4,256]{2,1,0:T(4,128)(2,1)} %reshape.142), calls=%async_computation.1 | async-start | bytes 524288 | tf_op jit(solution)/shard_map/all_to_all | solution.py:143

commit v10 on v3

--- a/solution.py
+++ b/solution.py
@@ -20,15 +20,25 @@
 
 
 def convolve(values, tile_cols, tile_counts, adjacency, myself):
-    window = with_halo(values, (("nodes", 0),), values.shape[0])
+    count = lax.axis_size("nodes")
+    forward = [(i, i + 1) for i in range(count - 1)]
+    backward = [(target, source) for source, target in forward]
+    low = lax.ppermute(values, "nodes", forward)
+    high = lax.ppermute(values, "nodes", backward)
     tile_size = adjacency.shape[2]
     per_device = tile_cols.shape[0]
-    window_tiles = window.reshape(-1, tile_size, window.shape[1])
-    offsets = tile_cols - (myself - 1) * per_device
-    picked = window_tiles[offsets]
+    offsets = tile_cols - myself * per_device
     live = jnp.arange(tile_cols.shape[1], dtype=jnp.int32)[None, :] < tile_counts[:, None]
-    weights = jnp.where(live[:, :, None, None], adjacency, jnp.zeros((), adjacency.dtype))
-    result = jnp.einsum("tkij,tkjf->tif", weights, picked, preferred_element_type=jnp.float32)
+
+    def term(block, shift):
+        tiles = block.reshape(-1, tile_size, block.shape[1])
+        place = offsets - shift
+        inside = live & (place >= 0) & (place < per_device)
+        picked = tiles[jnp.clip(place, 0, per_device - 1)]
+        weights = jnp.where(inside[:, :, None, None], adjacency, jnp.zeros((), adjacency.dtype))
+        return jnp.einsum("tkij,tkjf->tif", weights, picked, preferred_element_type=jnp.float32)
+
+    result = term(values, 0) + term(low, -per_device) + term(high, per_device)
     return result.reshape(values.shape[0], values.shape[1])
 
 

time: 102 us -> 115 us (1.13)
  matrix products: 43.1 us -> 50.9 us
  local copies, waits for them, and re-layouts: 4.8 us -> 10.3 us
  waiting for transfers between devices: 15 us -> 11.6 us
  starting transfers between devices: 37 us -> 39.4 us
    dot_general x2 -> x6, matrix products: 0.86 us -> 8.67 us  [term(): jnp.einsum('tkij,tkjf->tif', weights, picked, preferred_element_type=jnp....]
    gather x2 -> x6, local copies, waits for them, and re-layouts: 1.3 us -> 6.27 us  [term(): picked = tiles[jnp.clip(place, 0, per_device - 1)]]
    ppermute x4, waiting for transfers between devices: 6.49 us -> 3.99 us  [the longest x2 2.61 us: convolve(): high = lax.ppermute(values, 'nodes', backward)]
    all_to_all x1, starting transfers between devices: 13.6 us -> 16.1 us  [local(): lax.all_to_all(answers.reshape(device_count, DCAP, width), 'nodes', split...]
  transfers between devices with their start and end apart: 6 -> 6, of which waited for: 6 -> 4; matrix products, arithmetic and copies ran while one was open for 16% -> 20% of each run, Pallas kernels for 0% -> 0%
where the time goes in v10:
time: 115 us
  matrix products  50.9 us (44%)
  starting transfers between devices  39.4 us (34%)
  waiting for transfers between devices  11.6 us (10%)
  local copies, waits for them, and re-layouts  10.3 us (9%)
  other arithmetic  2.03 us (2%)
    all_to_all x1, starting transfers between devices, local(): lax.all_to_all(answers.reshape(device_count, DCAP, width), 'nodes', split...  16.1 us
    all_to_all x1, starting transfers between devices, local(): lax.all_to_all(payload.reshape(device_count, 1, -1), 'nodes', split_axis=...  11.5 us
    dot_general x1, matrix products, local(): jnp.dot(local_hot, coarse, preferred_element_type=jnp.float32)  9.5 us
    dot_general x6, matrix products, term(): jnp.einsum('tkij,tkjf->tif', weights, picked, preferred_element_type=jnp....  8.67 us
    dot_general x1, matrix products, local(): lax.dot_general(remote_hot, features, contract_rows, preferred_element_ty...  7.82 us
    dot_general x1, matrix products, local(): jnp.dot(remote_hot, returned, preferred_element_type=jnp.float32)  7.61 us
    ppermute x2, starting transfers between devices, convolve(): low = lax.ppermute(values, 'nodes', forward)  6.94 us
    dot_general x1, matrix products, local(): lax.dot_general(local_hot, features, contract_rows, preferred_element_typ...  6.82 us
  transfers between devices with their start and end apart: 6, of which 4 were waited for; matrix products, arithmetic and copies ran while one was open for 20% of the time, Pallas kernels for 0%

profile of v10, /device:TPU:1, one launch (start us, length us, event | category | flops | bytes accessed | tf_op | source)
XLA Modules:
  0.0 114.9 jit_solution(2217017346233333523)
XLA Ops:
  0.8 3.2 %broadcast_compare_fusion = (pred[128,512]{1,0:T(32,128)(4,1)S(1)}, f32[128,512]{1,0:T(8,128)S(1)}) fusion(s32[8192]{0:T(1024)S(1)} %get-tuple-element.26, s32[8192]{0:T(1024)S(1)} %get-tuple-element.25), kind=kOutput, calls=%fused_computation.82 | convolution fusion | flops 1079050240 | bytes 393216 | tf_op jit(solution)/shard_map/dot_general | solution.py:47
  4.6 4.8 %fusion.24 = f32[8192]{0:T(1024)S(1)} fusion(s32[8192]{0:T(1024)S(1)} %get-tuple-element.25, s32[8192]{0:T(1024)S(1)} %get-tuple-element.26, bf16[128,512]{1,0:T(8,128)(2,1)S(1)} %get-tuple-element.35), kind=kOutput, calls=%fused_computation.32 | convolution fusion | flops 1083170816 | bytes 229376 | tf_op jit(solution)/shard_map/dot_general | solution.py:52
  10.3 7.8 %fusion.1 = f32[512,256]{1,0:T(8,128)S(1)} fusion(bf16[8192,256]{1,0:T(8,128)(2,1)} %param.7, s32[8192]{0:T(1024)S(1)} %add_select_fusion.1), kind=kOutput, calls=%fused_computation.8 | convolution fusion | flops 2151677952 | bytes 4751360 | tf_op jit(solution)/shard_map/dot_general | solution.py:76
  18.5 1.2 %reshape.72 = f32[128,1,1152]{2,1,0:T(1,128)} reshape(f32[128,1152]{1,0:T(8,128)S(1)} %concatenate.3) | data formatting | bytes 1179648 | tf_op jit(solution)/shard_map/reshape | solution.py:94
  19.7 11.5 %all-to-all-start = ((f32[128,1,1152]{2,1,0:T(1,128)}), f32[128,1,1152]{2,1,0:T(1,128)S(1)}, u32[]{:S(2)}, u32[]{:S(2)}) async-start(f32[128,1,1152]{2,1,0:T(1,128)} %reshape.72), calls=%async_computation | async-start | bytes 1179648 | tf_op jit(solution)/shard_map/all_to_all | solution.py:93
  31.3 6.8 %fusion.10 = f32[512,256]{1,0:T(8,128)S(1)} fusion(bf16[8192,256]{1,0:T(8,128)(2,1)} %param.7, s32[8192]{0:T(1024)S(1)} %get-tuple-element.26, pred[8192]{0:T(1024)(128)(4,1)S(1)} %broadcast_compare_fusion.1), kind=kOutput, calls=%fused_computation.18 | convolution fusion | flops 2160066560 | bytes 4759552 | tf_op jit(solution)/shard_map/dot_general | solution.py:99
  39.0 6.4 %all-to-all-done = f32[128,1,1152]{2,1,0:T(1,128)S(1)} async-done(((f32[128,1,1152]{2,1,0:T(1,128)}), f32[128,1,1152]{2,1,0:T(1,128)S(1)}, u32[]{:S(2)}, u32[]{:S(2)}) %all-to-all-start) | async-done | bytes 589856 | tf_op jit(solution)/shard_map/all_to_all | solution.py:93
  47.9 3.0 %collective-permute-start.1 = (bf16[512,256]{1,0:T(8,128)(2,1)S(1)}, bf16[512,256]{1,0:T(8,128)(2,1)S(1)}, u32[]{:S(2)}, u32[]{:S(2)}) collective-permute-start(bf16[512,256]{1,0:T(8,128)(2,1)S(1)} %convolution_convert_fusion.2), channel_id=1, source_target_pairs={{1,0},{2,1},{3,2},{4,3},{5,4},{6,5},{7,6},{8,7},{9,8},{10,9},{11,1... | collective-permute-start | bytes 786440 | tf_op jit(solution)/shard_map/ppermute | solution.py:27
  50.9 2.6 %collective-permute-start = (bf16[512,256]{1,0:T(8,128)(2,1)S(1)}, bf16[512,256]{1,0:T(8,128)(2,1)S(1)}, u32[]{:S(2)}, u32[]{:S(2)}) collective-permute-start(bf16[512,256]{1,0:T(8,128)(2,1)S(1)} %convolution_convert_fusion.2), channel_id=1, source_target_pairs={{0,1},{1,2},{2,3},{3,4},{4,5},{5,6},{6,7},{7,8},{8,9},{9,10},{10,1... | collective-permute-start | bytes 786440 | tf_op jit(solution)/shard_map/ppermute | solution.py:26
  54.2 1.2 %convolution_bitcast_fusion.5 = f32[4,128,256]{2,1,0:T(8,128)} fusion(bf16[4,6,128,256]{3,2,1,0:T(8,128)(2,1)S(1)} %bitcast.90, bf16[4,6,128,128]{3,2,1,0:T(8,128)(2,1)S(1)} %copy-done.1, pred[4,6]{1,0:T(4,128)(4,1)S(1)} %get-tuple-element.29), kind=kOutput, calls=%fused_computation.38 | convolution fusion | flops 201719808 | bytes 2883608 | tf_op jit(solution)/shard_map/tkij,tkjf->tif/dot_general | solution.py:39
  55.4 1.4 %collective-permute-done = bf16[512,256]{1,0:T(8,128)(2,1)S(1)} collective-permute-done((bf16[512,256]{1,0:T(8,128)(2,1)S(1)}, bf16[512,256]{1,0:T(8,128)(2,1)S(1)}, u32[]{:S(2)}, u32[]{:S(2)}) %collective-permute-start) | collective-permute-done | bytes 262176 | tf_op jit(solution)/shard_map/ppermute | solution.py:26
  57.5 1.8 %gather_fusion.2 = bf16[24,128,256]{2,1,0:T(8,128)(2,1)} fusion(bf16[4,128,256]{2,1,0:T(8,128)(2,1)S(1)} %bitcast.80, s32[1024]{0:T(1024)S(1)} %pad_clamp_fusion), kind=kCustom, calls=%fused_computation.2 | custom fusion | bytes 3145824 | tf_op jit(solution)/shard_map/gather | solution.py:37
  59.3 1.9 %convolution_bitcast_fusion.3 = f32[4,128,256]{2,1,0:T(8,128)S(1)} fusion(bf16[4,6,128,256]{3,2,1,0:T(8,128)(2,1)} %bitcast.89, bf16[4,6,128,128]{3,2,1,0:T(8,128)(2,1)S(1)} %copy-done.1, pred[4,6]{1,0:T(4,128)(4,1)} %get-tuple-element.28), kind=kOutput, calls=%fused_computation.36 | convolution fusion | flops 201719808 | bytes 2883608 | tf_op jit(solution)/shard_map/tkij,tkjf->tif/dot_general | solution.py:39
  61.9 4.4 %collective-permute-start.2 = (bf16[512,256]{1,0:T(8,128)(2,1)S(1)}, bf16[512,256]{1,0:T(8,128)(2,1)S(1)}, u32[]{:S(2)}, u32[]{:S(2)}) collective-permute-start(bf16[512,256]{1,0:T(8,128)(2,1)S(1)} %convolution_convert_fusion.1), channel_id=1, source_target_pairs={{0,1},{1,2},{2,3},{3,4},{4,5},{5,6},{6,7},{7,8},{8,9},{9,10},{10,1... | collective-permute-start | bytes 786440 | tf_op jit(solution)/shard_map/ppermute | solution.py:26
  66.3 1.9 %collective-permute-start.3 = (bf16[512,256]{1,0:T(8,128)(2,1)S(1)}, bf16[512,256]{1,0:T(8,128)(2,1)S(1)}, u32[]{:S(2)}, u32[]{:S(2)}) collective-permute-start(bf16[512,256]{1,0:T(8,128)(2,1)S(1)} %convolution_convert_fusion.1), channel_id=1, source_target_pairs={{1,0},{2,1},{3,2},{4,3},{5,4},{6,5},{7,6},{8,7},{9,8},{10,9},{11,1... | collective-permute-start | bytes 786440 | tf_op jit(solution)/shard_map/ppermute | solution.py:27
  68.9 1.8 %convolution_bitcast_fusion.2 = f32[4,128,256]{2,1,0:T(8,128)} fusion(bf16[4,6,128,256]{3,2,1,0:T(8,128)(2,1)S(1)} %bitcast.88, bf16[4,6,128,128]{3,2,1,0:T(8,128)(2,1)S(1)} %copy-done.1, pred[4,6]{1,0:T(4,128)(4,1)} %copy-done.16), kind=kOutput, calls=%fused_computation.35 | convolution fusion | flops 201719808 | bytes 2883608 | tf_op jit(solution)/shard_map/tkij,tkjf->tif/dot_general | solution.py:39
  71.4 2.6 %collective-permute-done.3 = bf16[512,256]{1,0:T(8,128)(2,1)S(1)} collective-permute-done((bf16[512,256]{1,0:T(8,128)(2,1)S(1)}, bf16[512,256]{1,0:T(8,128)(2,1)S(1)}, u32[]{:S(2)}, u32[]{:S(2)}) %collective-permute-start.3) | collective-permute-done | bytes 262176 | tf_op jit(solution)/shard_map/ppermute | solution.py:27
  74.0 1.8 %gather_fusion.5 = bf16[24,128,256]{2,1,0:T(8,128)(2,1)} fusion(bf16[4,128,256]{2,1,0:T(8,128)(2,1)S(1)} %bitcast.81, s32[1024]{0:T(1024)S(1)} %pad_clamp_fusion), kind=kCustom, calls=%fused_computation.5 | custom fusion | bytes 3145824 | tf_op jit(solution)/shard_map/gather | solution.py:37
  75.8 1.8 %convolution_bitcast_fusion = f32[4,128,256]{2,1,0:T(8,128)S(1)} fusion(bf16[4,6,128,256]{3,2,1,0:T(8,128)(2,1)} %bitcast.87, bf16[4,6,128,128]{3,2,1,0:T(8,128)(2,1)S(1)} %copy-done.1, pred[4,6]{1,0:T(4,128)(4,1)S(1)} %copy-done.15), kind=kOutput, calls=%fused_computation.33 | convolution fusion | flops 201719808 | bytes 2883608 | tf_op jit(solution)/shard_map/tkij,tkjf->tif/dot_general | solution.py:39
  77.7 1.5 %fusion.33 = bf16[4,128,256]{2,1,0:T(8,128)(2,1)S(1)} fusion(f32[4,128,256]{2,1,0:T(8,128)S(1)} %convolution_bitcast_fusion, f32[4,128,256]{2,1,0:T(8,128)} %convolution_bitcast_fusion.2, bf16[4,6,128,256]{3,2,1,0:T(8,128)(2,1)S(1)} %bitcast.78, bf16[4,6,128,128]{3,2,1,0:T(8,128)(2,1)S(1)} %copy-done.1, pred[4,6]{1,0:T(4,128)(4,1)S(1)} %get-tuple-element.27), kind=kOutput, calls=%fused_computation.48 | convolution fusion | flops 202113024 | bytes 3670040 | tf_op jit(solution)/shard_map/tkij,tkjf->tif/dot_general | solution.py:39
  80.3 16.1 %all-to-all-start.1 = ((bf16[128,4,256]{2,1,0:T(4,128)(2,1)}), bf16[128,4,256]{2,1,0:T(4,128)(2,1)S(1)}, u32[]{:S(2)}, u32[]{:S(2)}) async-start(bf16[128,4,256]{2,1,0:T(4,128)(2,1)} %reshape.81), calls=%async_computation.1 | async-start | bytes 524288 | tf_op jit(solution)/shard_map/all_to_all | solution.py:119
  96.4 9.5 %convolution_add_fusion = f32[8192,256]{1,0:T(8,128)} fusion(bf16[512,256]{1,0:T(8,128)(2,1)S(1)} %bitcast.92, s32[8192]{0:T(1024)S(1)} %copy-done.6, bf16[8192,256]{1,0:T(8,128)(2,1)} %param.7, pred[8192]{0:T(1024)(128)(4,1)S(1)} %copy-done.13), kind=kOutput, calls=%fused_computation.16 | convolution fusion | flops 2164260864 | bytes 12886016 | tf_op jit(solution)/shard_map/dot_general | solution.py:124
  105.9 1.3 %all-to-all-done.1 = bf16[128,4,256]{2,1,0:T(4,128)(2,1)S(1)} async-done(((bf16[128,4,256]{2,1,0:T(4,128)(2,1)}), bf16[128,4,256]{2,1,0:T(4,128)(2,1)S(1)}, u32[]{:S(2)}, u32[]{:S(2)}) %all-to-all-start.1) | async-done | bytes 262176 | tf_op jit(solution)/shard_map/all_to_all | solution.py:119
  107.3 7.6 %fusion.7 = bf16[8192,256]{1,0:T(8,128)(2,1)} fusion(f32[8192,256]{1,0:T(8,128)} %convolution_add_fusion, bf16[512,256]{1,0:T(8,128)(2,1)S(1)} %reshape.82, s32[8192]{0:T(1024)S(1)} %copy-done.8), kind=kOutput, calls=%fused_computation.15 | convolution fusion | flops 2155872256 | bytes 12877824 | tf_op jit(solution)/shard_map/dot_general | solution.py:125
  (79 shorter events, 10.4 us)
Async XLA Ops:
  0.0 47.7 %copy-start = (bf16[256,256]{1,0:T(8,128)(2,1)S(1)}, bf16[256,256]{1,0:T(8,128)(2,1)}, u32[]{:S(2)}) copy-start(bf16[256,256]{1,0:T(8,128)(2,1)} %param.12) | copy-start | bytes 393220
  0.8 30.4 %copy-start.5 = (s32[8192]{0:T(1024)}, s32[8192]{0:T(1024)S(1)}, u32[]{:S(2)}) copy-start(s32[8192]{0:T(1024)S(1)} %get-tuple-element.26) | copy-start | bytes 98308
  4.6 4.9 %copy-start.3 = (s32[8192]{0:T(1024)S(1)}, s32[8192]{0:T(1024)}, u32[]{:S(2)}) copy-start(s32[8192]{0:T(1024)} %param.8) | copy-start | bytes 98308
  9.5 8.6 %copy-start.7 = (s32[8192]{0:T(1024)}, s32[8192]{0:T(1024)S(1)}, u32[]{:S(2)}) copy-start(s32[8192]{0:T(1024)S(1)} %add_select_fusion.1) | copy-start | bytes 98308
  19.7 25.7 %all-to-all-start = ((f32[128,1,1152]{2,1,0:T(1,128)}), f32[128,1,1152]{2,1,0:T(1,128)S(1)}, u32[]{:S(2)}, u32[]{:S(2)}) async-start(f32[128,1,1152]{2,1,0:T(1,128)} %reshape.72), calls=%async_computation | async-start | bytes 1179648 | tf_op jit(solution)/shard_map/all_to_all | solution.py:93
  31.3 6.9 %copy-start.12 = (pred[8192]{0:T(1024)(128)(4,1)}, pred[8192]{0:T(1024)(128)(4,1)S(1)}, u32[]{:S(2)}) copy-start(pred[8192]{0:T(1024)(128)(4,1)S(1)} %broadcast_compare_fusion.1) | copy-start | bytes 24580
  31.3 6.9 %copy-start.11 = (s32[4,6]{1,0:T(4,128)S(1)}, s32[4,6]{1,0:T(4,128)}, u32[]{:S(2)}) copy-start(s32[4,6]{1,0:T(4,128)} %param.9) | copy-start | bytes 292
  31.3 7.2 %copy-start.14 = (s32[4]{0:T(128)S(1)}, s32[4]{0:T(128)}, u32[]{:S(2)}) copy-start(s32[4]{0:T(128)} %param.10) | copy-start | bytes 52
  39.0 15.1 %copy-start.16 = (pred[4,6]{1,0:T(4,128)(4,1)}, pred[4,6]{1,0:T(4,128)(4,1)S(1)}, u32[]{:S(2)}) copy-start(pred[4,6]{1,0:T(4,128)(4,1)S(1)} %get-tuple-element.29) | copy-start | bytes 76
  45.6 8.6 %copy-start.1 = (bf16[4,6,128,128]{3,2,1,0:T(8,128)(2,1)S(1)}, bf16[4,6,128,128]{3,2,1,0:T(8,128)(2,1)}, u32[]{:S(2)}) copy-start(bf16[4,6,128,128]{3,2,1,0:T(8,128)(2,1)} %param.11) | copy-start | bytes 2359300
  46.0 0.6 copy-start.9
  47.9 9.5 %collective-permute-start.1 = (bf16[512,256]{1,0:T(8,128)(2,1)S(1)}, bf16[512,256]{1,0:T(8,128)(2,1)S(1)}, u32[]{:S(2)}, u32[]{:S(2)}) collective-permute-start(bf16[512,256]{1,0:T(8,128)(2,1)S(1)} %convolution_convert_fusion.2), channel_id=1, source_target_pairs={{1,0},{2,1},{3,2},{4,3},{5,4},{6,5},{7,6},{8,7},{9,8},{10,9},{11,1... | collective-permute-start | bytes 786440 | tf_op jit(solution)/shard_map/ppermute | solution.py:27
  50.9 5.9 %collective-permute-start = (bf16[512,256]{1,0:T(8,128)(2,1)S(1)}, bf16[512,256]{1,0:T(8,128)(2,1)S(1)}, u32[]{:S(2)}, u32[]{:S(2)}) collective-permute-start(bf16[512,256]{1,0:T(8,128)(2,1)S(1)} %convolution_convert_fusion.2), channel_id=1, source_target_pairs={{0,1},{1,2},{2,3},{3,4},{4,5},{5,6},{6,7},{7,8},{8,9},{9,10},{10,1... | collective-permute-start | bytes 786440 | tf_op jit(solution)/shard_map/ppermute | solution.py:26
  57.5 3.7 %copy-start.2 = (f32[4,128,256]{2,1,0:T(8,128)S(1)}, f32[4,128,256]{2,1,0:T(8,128)}, u32[]{:S(2)}) copy-start(f32[4,128,256]{2,1,0:T(8,128)} %convolution_bitcast_fusion.5) | copy-start | bytes 1572868
  59.3 2.3 %copy-start.4 = (bf16[256,256]{1,0:T(8,128)(2,1)S(1)}, bf16[256,256]{1,0:T(8,128)(2,1)}, u32[]{:S(2)}) copy-start(bf16[256,256]{1,0:T(8,128)(2,1)} %param.13) | copy-start | bytes 393220
  61.9 8.8 %collective-permute-start.2 = (bf16[512,256]{1,0:T(8,128)(2,1)S(1)}, bf16[512,256]{1,0:T(8,128)(2,1)S(1)}, u32[]{:S(2)}, u32[]{:S(2)}) collective-permute-start(bf16[512,256]{1,0:T(8,128)(2,1)S(1)} %convolution_convert_fusion.1), channel_id=1, source_target_pairs={{0,1},{1,2},{2,3},{3,4},{4,5},{5,6},{6,7},{7,8},{8,9},{9,10},{10,1... | collective-permute-start | bytes 786440 | tf_op jit(solution)/shard_map/ppermute | solution.py:26
  66.3 7.7 %collective-permute-start.3 = (bf16[512,256]{1,0:T(8,128)(2,1)S(1)}, bf16[512,256]{1,0:T(8,128)(2,1)S(1)}, u32[]{:S(2)}, u32[]{:S(2)}) collective-permute-start(bf16[512,256]{1,0:T(8,128)(2,1)S(1)} %convolution_convert_fusion.1), channel_id=1, source_target_pairs={{1,0},{2,1},{3,2},{4,3},{5,4},{6,5},{7,6},{8,7},{9,8},{10,9},{11,1... | collective-permute-start | bytes 786440 | tf_op jit(solution)/shard_map/ppermute | solution.py:27
  68.9 7.0 %copy-start.15 = (pred[4,6]{1,0:T(4,128)(4,1)S(1)}, pred[4,6]{1,0:T(4,128)(4,1)}, u32[]{:S(2)}) copy-start(pred[4,6]{1,0:T(4,128)(4,1)} %get-tuple-element.28) | copy-start | bytes 76
  75.8 3.3 %copy-start.10 = (s32[512]{0:T(512)S(1)}, s32[512]{0:T(512)}, u32[]{:S(2)}) copy-start(s32[512]{0:T(512)} %copy-done.9) | copy-start | bytes 6148
  77.6 18.7 %copy-start.6 = (s32[8192]{0:T(1024)S(1)}, s32[8192]{0:T(1024)}, u32[]{:S(2)}) copy-start(s32[8192]{0:T(1024)} %copy-done.5) | copy-start | bytes 98308
  77.7 18.7 %copy-start.13 = (pred[8192]{0:T(1024)(128)(4,1)S(1)}, pred[8192]{0:T(1024)(128)(4,1)}, u32[]{:S(2)}) copy-start(pred[8192]{0:T(1024)(128)(4,1)} %copy-done.12) | copy-start | bytes 24580
  80.3 26.9 %all-to-all-start.1 = ((bf16[128,4,256]{2,1,0:T(4,128)(2,1)}), bf16[128,4,256]{2,1,0:T(4,128)(2,1)S(1)}, u32[]{:S(2)}, u32[]{:S(2)}) async-start(bf16[128,4,256]{2,1,0:T(4,128)(2,1)} %reshape.81), calls=%async_computation.1 | async-start | bytes 524288 | tf_op jit(solution)/shard_map/all_to_all | solution.py:119
  96.4 10.9 %copy-start.8 = (s32[8192]{0:T(1024)S(1)}, s32[8192]{0:T(1024)}, u32[]{:S(2)}) copy-start(s32[8192]{0:T(1024)} %copy-done.7) | copy-start | bytes 98308

commit v11 on v3

--- a/solution.py
+++ b/solution.py
@@ -58,7 +58,7 @@
     lid_hot = (lids[:, None] == here[None, :]).astype(jnp.bfloat16)
     presence, rank, slot = distinct_slots(owner_hot, lid_hot, clusters_here)
     remote_slots = device_count * DCAP
-    slot_column = jnp.where(remote, owners * DCAP + slot, -1)
+    slot_column = jnp.where(remote, slot * device_count + owners, -1)
     slot_range = jnp.arange(remote_slots, dtype=jnp.int32)
     remote_hot = (slot_column[:, None] == slot_range[None, :]).astype(jnp.bfloat16)
     local_hot = jnp.where(remote[:, None], jnp.zeros((), jnp.bfloat16), lid_hot)
@@ -79,13 +79,15 @@
     meta = jnp.concatenate(
         [slot_counts, slot_ids, jnp.zeros((device_count, 128 - 2 * DCAP), jnp.float32)], axis=1
     )
-    payload = jnp.concatenate([remote_sums.reshape(device_count, DCAP * width), meta], axis=1)
+    payload = jnp.concatenate(
+        [remote_sums[k * device_count:(k + 1) * device_count] for k in range(DCAP)] + [meta], axis=1
+    )
     got = lax.all_to_all(
         payload.reshape(device_count, 1, -1), "nodes", split_axis=0, concat_axis=0, tiled=True
     ).reshape(device_count, -1)
-    got_sums = got[:, : DCAP * width].reshape(remote_slots, width)
-    got_counts = got[:, DCAP * width : DCAP * width + DCAP].reshape(remote_slots)
-    got_ids = got[:, DCAP * width + DCAP : DCAP * width + 2 * DCAP].reshape(remote_slots).astype(jnp.int32)
+    got_sums = jnp.concatenate([got[:, k * width:(k + 1) * width] for k in range(DCAP)], axis=0)
+    got_counts = got[:, DCAP * width : DCAP * width + DCAP].T.reshape(remote_slots)
+    got_ids = got[:, DCAP * width + DCAP : DCAP * width + 2 * DCAP].T.reshape(remote_slots).astype(jnp.int32)
     local_sums = lax.dot_general(
         local_hot, features, contract_rows, preferred_element_type=jnp.float32
     )
@@ -106,9 +108,13 @@
     answers = jnp.dot(
         got_hot.astype(jnp.bfloat16), coarse, preferred_element_type=jnp.float32
     ).astype(jnp.bfloat16)
+    back = jnp.concatenate(
+        [answers[k * device_count:(k + 1) * device_count] for k in range(DCAP)], axis=1
+    )
     returned = lax.all_to_all(
-        answers.reshape(device_count, DCAP, width), "nodes", split_axis=0, concat_axis=0, tiled=True
-    ).reshape(remote_slots, width)
+        back.reshape(device_count, 1, -1), "nodes", split_axis=0, concat_axis=0, tiled=True
+    ).reshape(device_count, -1)
+    returned = jnp.concatenate([returned[:, k * width:(k + 1) * width] for k in range(DCAP)], axis=0)
     value = (
         features.astype(jnp.float32)
         + jnp.dot(local_hot, coarse, preferred_element_type=jnp.float32)

time: 102 us -> 100 us (0.980)
  matrix products: 43.1 us -> 40 us
    dot_general x1, matrix products: 7.82 us -> 3.75 us  [local(): lax.dot_general(remote_hot, features, contract_rows, preferred_element_ty...]
    unnamed x13 -> x19, local copies, waits for them, and re-layouts: 0.07 us -> 1.41 us
  transfers between devices with their start and end apart: 6 -> 6, of which waited for: 6 -> 6; matrix products, arithmetic and copies ran while one was open for 16% -> 17% of each run, Pallas kernels for 0% -> 0%
where the time goes in v11:
time: 100 us; the launch traced here: 99.7 us
  matrix products  40 us (40%)
  starting transfers between devices  37 us (37%)
  waiting for transfers between devices  15 us (15%)
  local copies, waits for them, and re-layouts  4.87 us (5%)
  other arithmetic  2.47 us (2%)
    all_to_all x1, starting transfers between devices, local(): lax.all_to_all(back.reshape(device_count, 1, -1), 'nodes', split_axis=0,...  13.6 us
    all_to_all x1, starting transfers between devices, local(): lax.all_to_all(payload.reshape(device_count, 1, -1), 'nodes', split_axis=...  11.5 us
    dot_general x1, matrix products, local(): jnp.dot(local_hot, coarse, preferred_element_type=jnp.float32)  9.47 us
    dot_general x1, matrix products, local(): jnp.dot(remote_hot, returned, preferred_element_type=jnp.float32)  8.52 us
    all_to_all x1, waiting for transfers between devices, local(): lax.all_to_all(payload.reshape(device_count, 1, -1), 'nodes', split_axis=...  7.19 us
    ppermute x2, starting transfers between devices, with_halo(): lax.ppermute(lax.slice_in_dim(block, block.shape[dim] - width, None, axis...  6.95 us
    dot_general x1, matrix products, local(): lax.dot_general(local_hot, features, contract_rows, preferred_element_typ...  6.82 us
    ppermute x2, starting transfers between devices, with_halo(): lax.ppermute(lax.slice_in_dim(block, 0, width, axis=dim), axis, backward)  4.93 us
  transfers between devices with their start and end apart: 6, of which 6 were waited for; matrix products, arithmetic and copies ran while one was open for 17% of the time, Pallas kernels for 0%

profile of v11, /device:TPU:1, one launch (start us, length us, event | category | flops | bytes accessed | tf_op | source)
XLA Modules:
  0.0 99.7 jit_solution(13756941710709595971)
XLA Ops:
  0.0 0.8 add_select_fusion
  0.8 3.2 %broadcast_compare_fusion = (pred[128,512]{1,0:T(32,128)(4,1)S(1)}, f32[128,512]{1,0:T(8,128)S(1)}) fusion(s32[8192]{0:T(1024)S(1)} %get-tuple-element.42, s32[8192]{0:T(1024)S(1)} %get-tuple-element.41), kind=kOutput, calls=%fused_computation.82 | convolution fusion | flops 1079050240 | bytes 393216 | tf_op jit(solution)/shard_map/dot_general | solution.py:37
  4.6 4.8 %fusion.24 = f32[8192]{0:T(1024)S(1)} fusion(s32[8192]{0:T(1024)S(1)} %get-tuple-element.41, s32[8192]{0:T(1024)S(1)} %get-tuple-element.42, bf16[128,512]{1,0:T(8,128)(2,1)S(1)} %get-tuple-element.45), kind=kOutput, calls=%fused_computation.28 | convolution fusion | flops 1083170816 | bytes 229376 | tf_op jit(solution)/shard_map/dot_general | solution.py:42
  9.5 3.7 %fusion.1 = f32[512,256]{0,1:T(8,128)S(1)} fusion(bf16[8192,256]{1,0:T(8,128)(2,1)S(1)} %copy-done.4, s32[8192]{0:T(1024)S(1)} %add_select_fusion.1), kind=kOutput, calls=%fused_computation.4 | convolution fusion | flops 2151677952 | bytes 4751360 | tf_op jit(solution)/shard_map/dot_general | solution.py:66
  13.6 1.2 %copy.14 = f32[128,1,1152]{2,1,0:T(1,128)} copy(f32[128,1,1152]{0,2,1:T(8,128)S(1)} %bitcast.58) | data formatting | bytes 1179648 | tf_op jit(solution)/shard_map/reshape | solution.py:86
  14.8 11.5 %all-to-all-start = ((f32[128,1,1152]{2,1,0:T(1,128)}), f32[128,1,1152]{2,1,0:T(1,128)S(1)}, u32[]{:S(2)}, u32[]{:S(2)}) async-start(f32[128,1,1152]{2,1,0:T(1,128)} %copy.14), calls=%async_computation | async-start | bytes 1179648 | tf_op jit(solution)/shard_map/all_to_all | solution.py:85
  26.4 6.8 %fusion.10 = f32[512,256]{1,0:T(8,128)S(1)} fusion(bf16[8192,256]{1,0:T(8,128)(2,1)} %param.7, s32[8192]{0:T(1024)S(1)} %get-tuple-element.42, pred[8192]{0:T(1024)(128)(4,1)S(1)} %broadcast_compare_fusion.1), kind=kOutput, calls=%fused_computation.14 | convolution fusion | flops 2160066560 | bytes 4759552 | tf_op jit(solution)/shard_map/dot_general | solution.py:91
  33.4 7.2 %all-to-all-done = f32[128,1,1152]{2,1,0:T(1,128)S(1)} async-done(((f32[128,1,1152]{2,1,0:T(1,128)}), f32[128,1,1152]{2,1,0:T(1,128)S(1)}, u32[]{:S(2)}, u32[]{:S(2)}) %all-to-all-start) | async-done | bytes 589856 | tf_op jit(solution)/shard_map/all_to_all | solution.py:85
  41.1 1.1 %fusion.27 = bf16[512,256]{1,0:T(8,128)(2,1)S(1)} fusion(f32[512,256]{1,0:T(8,128)S(1)} %fusion.10, f32[128,256]{1,0:T(8,128)S(1)} %get-tuple-element.20, f32[128,256]{1,0:T(8,128)S(1)} %get-tuple-element.21, f32[128,256]{1,0:T(8,128)S(1)} %get-tuple-element.22, f32[128,256]{1,0:T(8,128)S(1)} %get-tuple-element.19, s32[512]{0:T(512)S(1)} %bitcast.64, ...), kind=kOutput, calls=%fused_computation.34 | convolution fusion | flops 806354944 | bytes 1314816 | tf_op jit(solution)/shard_map/dot_general | solution.py:96
  42.5 3.0 %collective-permute-start.1 = (bf16[512,256]{1,0:T(8,128)(2,1)S(1)}, bf16[512,256]{1,0:T(8,128)(2,1)S(1)}, u32[]{:S(2)}, u32[]{:S(2)}) collective-permute-start(bf16[512,256]{1,0:T(8,128)(2,1)S(1)} %convolution_convert_fusion.2), channel_id=1, source_target_pairs={{1,0},{2,1},{3,2},{4,3},{5,4},{6,5},{7,6},{8,7},{9,8},{10,9},{11,1... | collective-permute-start | bytes 786440 | tf_op jit(solution)/shard_map/ppermute | solution.py:17
  45.5 2.6 %collective-permute-start = (bf16[512,256]{1,0:T(8,128)(2,1)S(1)}, bf16[512,256]{1,0:T(8,128)(2,1)S(1)}, u32[]{:S(2)}, u32[]{:S(2)}) collective-permute-start(bf16[512,256]{1,0:T(8,128)(2,1)S(1)} %convolution_convert_fusion.2), channel_id=1, source_target_pairs={{0,1},{1,2},{2,3},{3,4},{4,5},{5,6},{6,7},{7,8},{8,9},{9,10},{10,1... | collective-permute-start | bytes 786440 | tf_op jit(solution)/shard_map/ppermute | solution.py:14
  48.2 2.0 %collective-permute-done.1 = bf16[512,256]{1,0:T(8,128)(2,1)S(1)} collective-permute-done((bf16[512,256]{1,0:T(8,128)(2,1)S(1)}, bf16[512,256]{1,0:T(8,128)(2,1)S(1)}, u32[]{:S(2)}, u32[]{:S(2)}) %collective-permute-start.1) | collective-permute-done | bytes 262176 | tf_op jit(solution)/shard_map/ppermute | solution.py:17
  50.2 1.2 %collective-permute-done = bf16[512,256]{1,0:T(8,128)(2,1)S(1)} collective-permute-done((bf16[512,256]{1,0:T(8,128)(2,1)S(1)}, bf16[512,256]{1,0:T(8,128)(2,1)S(1)}, u32[]{:S(2)}, u32[]{:S(2)}) %collective-permute-start) | collective-permute-done | bytes 262176 | tf_op jit(solution)/shard_map/ppermute | solution.py:14
  52.8 1.9 %collective-permute-start.3 = (bf16[512,256]{1,0:T(8,128)(2,1)S(1)}, bf16[512,256]{1,0:T(8,128)(2,1)S(1)}, u32[]{:S(2)}, u32[]{:S(2)}) collective-permute-start(bf16[512,256]{1,0:T(8,128)(2,1)S(1)} %convolution_convert_fusion.1), channel_id=1, source_target_pairs={{1,0},{2,1},{3,2},{4,3},{5,4},{6,5},{7,6},{8,7},{9,8},{10,9},{11,1... | collective-permute-start | bytes 786440 | tf_op jit(solution)/shard_map/ppermute | solution.py:17
  54.7 4.4 %collective-permute-start.2 = (bf16[512,256]{1,0:T(8,128)(2,1)S(1)}, bf16[512,256]{1,0:T(8,128)(2,1)S(1)}, u32[]{:S(2)}, u32[]{:S(2)}) collective-permute-start(bf16[512,256]{1,0:T(8,128)(2,1)S(1)} %convolution_convert_fusion.1), channel_id=1, source_target_pairs={{0,1},{1,2},{2,3},{3,4},{4,5},{5,6},{6,7},{7,8},{8,9},{9,10},{10,1... | collective-permute-start | bytes 786440 | tf_op jit(solution)/shard_map/ppermute | solution.py:14
  59.1 2.1 %collective-permute-done.3 = bf16[512,256]{1,0:T(8,128)(2,1)S(1)} collective-permute-done((bf16[512,256]{1,0:T(8,128)(2,1)S(1)}, bf16[512,256]{1,0:T(8,128)(2,1)S(1)}, u32[]{:S(2)}, u32[]{:S(2)}) %collective-permute-start.3) | collective-permute-done | bytes 262176 | tf_op jit(solution)/shard_map/ppermute | solution.py:17
  61.2 1.2 %collective-permute-done.2 = bf16[512,256]{1,0:T(8,128)(2,1)S(1)} collective-permute-done((bf16[512,256]{1,0:T(8,128)(2,1)S(1)}, bf16[512,256]{1,0:T(8,128)(2,1)S(1)}, u32[]{:S(2)}, u32[]{:S(2)}) %collective-permute-start.2) | collective-permute-done | bytes 262176 | tf_op jit(solution)/shard_map/ppermute | solution.py:14
  62.5 0.6 gather_fusion.1
  64.6 0.8 reduce
  65.6 0.9 reshape.98
  66.4 13.6 %all-to-all-start.1 = ((bf16[128,2,512]{2,1,0:T(2,128)(2,1)}), bf16[128,2,512]{2,1,0:T(2,128)(2,1)S(1)}, u32[]{:S(2)}, u32[]{:S(2)}) async-start(bf16[128,2,512]{2,1,0:T(2,128)(2,1)} %reshape.98), calls=%async_computation.1 | async-start | bytes 524288 | tf_op jit(solution)/shard_map/all_to_all | solution.py:114
  80.1 9.5 %convolution_add_fusion = f32[8192,256]{1,0:T(8,128)} fusion(bf16[512,256]{1,0:T(8,128)(2,1)S(1)} %bitcast.77, s32[8192]{0:T(1024)S(1)} %get-tuple-element.42, bf16[8192,256]{1,0:T(8,128)(2,1)} %param.7, pred[8192]{0:T(1024)(128)(4,1)S(1)} %broadcast_compare_fusion.1), kind=kOutput, calls=%fused_computation.12 | convolution fusion | flops 2164260864 | bytes 12886016 | tf_op jit(solution)/shard_map/dot_general | solution.py:120
  89.5 1.3 %all-to-all-done.1 = bf16[128,2,512]{2,1,0:T(2,128)(2,1)S(1)} async-done(((bf16[128,2,512]{2,1,0:T(2,128)(2,1)}), bf16[128,2,512]{2,1,0:T(2,128)(2,1)S(1)}, u32[]{:S(2)}, u32[]{:S(2)}) %all-to-all-start.1) | async-done | bytes 262176 | tf_op jit(solution)/shard_map/all_to_all | solution.py:114
  91.2 8.5 %fusion.7 = bf16[8192,256]{1,0:T(8,128)(2,1)} fusion(f32[8192,256]{1,0:T(8,128)} %convolution_add_fusion, s32[8192]{0:T(1024)S(1)} %add_select_fusion.1, bf16[128,256]{1,0:T(8,128)(2,1)S(1)} %get-tuple-element.34, bf16[128,256]{1,0:T(8,128)(2,1)S(1)} %get-tuple-element.35, bf16[128,256]{1,0:T(8,128)(2,1)S(1)} %get-tuple-element.36, ...), kind=kOutput, calls=%fused_computation.11 | convolution fusion | flops 2156920832 | bytes 12877824 | tf_op jit(solution)/shard_map/dot_general | solution.py:121
  (50 shorter events, 5.3 us)
Async XLA Ops:
  0.0 42.3 %copy-start = (bf16[256,256]{1,0:T(8,128)(2,1)S(1)}, bf16[256,256]{1,0:T(8,128)(2,1)}, u32[]{:S(2)}) copy-start(bf16[256,256]{1,0:T(8,128)(2,1)} %param.12) | copy-start | bytes 393220
  4.6 4.9 %copy-start.1 = (s32[8192]{0:T(1024)S(1)}, s32[8192]{0:T(1024)}, u32[]{:S(2)}) copy-start(s32[8192]{0:T(1024)} %param.8) | copy-start | bytes 98308
  4.6 4.9 %copy-start.4 = (bf16[8192,256]{1,0:T(8,128)(2,1)S(1)}, bf16[8192,256]{1,0:T(8,128)(2,1)}, u32[]{:S(2)}) copy-start(bf16[8192,256]{1,0:T(8,128)(2,1)} %param.7) | copy-start | bytes 12582916
  14.8 25.7 %all-to-all-start = ((f32[128,1,1152]{2,1,0:T(1,128)}), f32[128,1,1152]{2,1,0:T(1,128)S(1)}, u32[]{:S(2)}, u32[]{:S(2)}) async-start(f32[128,1,1152]{2,1,0:T(1,128)} %copy.14), calls=%async_computation | async-start | bytes 1179648 | tf_op jit(solution)/shard_map/all_to_all | solution.py:85
  26.4 6.9 %copy-start.3 = (s32[4,6]{1,0:T(4,128)S(1)}, s32[4,6]{1,0:T(4,128)}, u32[]{:S(2)}) copy-start(s32[4,6]{1,0:T(4,128)} %param.9) | copy-start | bytes 292
  33.2 14.9 %copy-start.6 = (s32[4]{0:T(128)S(1)}, s32[4]{0:T(128)}, u32[]{:S(2)}) copy-start(s32[4]{0:T(128)} %param.10) | copy-start | bytes 52
  41.1 11.0 %copy-start.5 = (bf16[4,6,128,128]{3,2,1,0:T(8,128)(2,1)S(1)}, bf16[4,6,128,128]{3,2,1,0:T(8,128)(2,1)}, u32[]{:S(2)}) copy-start(bf16[4,6,128,128]{3,2,1,0:T(8,128)(2,1)} %param.11) | copy-start | bytes 2359300
  42.3 10.3 %copy-start.2 = (bf16[256,256]{1,0:T(8,128)(2,1)S(1)}, bf16[256,256]{1,0:T(8,128)(2,1)}, u32[]{:S(2)}) copy-start(bf16[256,256]{1,0:T(8,128)(2,1)} %param.13) | copy-start | bytes 393220
  42.5 7.7 %collective-permute-start.1 = (bf16[512,256]{1,0:T(8,128)(2,1)S(1)}, bf16[512,256]{1,0:T(8,128)(2,1)S(1)}, u32[]{:S(2)}, u32[]{:S(2)}) collective-permute-start(bf16[512,256]{1,0:T(8,128)(2,1)S(1)} %convolution_convert_fusion.2), channel_id=1, source_target_pairs={{1,0},{2,1},{3,2},{4,3},{5,4},{6,5},{7,6},{8,7},{9,8},{10,9},{11,1... | collective-permute-start | bytes 786440 | tf_op jit(solution)/shard_map/ppermute | solution.py:17
  45.5 5.9 %collective-permute-start = (bf16[512,256]{1,0:T(8,128)(2,1)S(1)}, bf16[512,256]{1,0:T(8,128)(2,1)S(1)}, u32[]{:S(2)}, u32[]{:S(2)}) collective-permute-start(bf16[512,256]{1,0:T(8,128)(2,1)S(1)} %convolution_convert_fusion.2), channel_id=1, source_target_pairs={{0,1},{1,2},{2,3},{3,4},{4,5},{5,6},{6,7},{7,8},{8,9},{9,10},{10,1... | collective-permute-start | bytes 786440 | tf_op jit(solution)/shard_map/ppermute | solution.py:14
  52.8 8.4 %collective-permute-start.3 = (bf16[512,256]{1,0:T(8,128)(2,1)S(1)}, bf16[512,256]{1,0:T(8,128)(2,1)S(1)}, u32[]{:S(2)}, u32[]{:S(2)}) collective-permute-start(bf16[512,256]{1,0:T(8,128)(2,1)S(1)} %convolution_convert_fusion.1), channel_id=1, source_target_pairs={{1,0},{2,1},{3,2},{4,3},{5,4},{6,5},{7,6},{8,7},{9,8},{10,9},{11,1... | collective-permute-start | bytes 786440 | tf_op jit(solution)/shard_map/ppermute | solution.py:17
  54.7 7.7 %collective-permute-start.2 = (bf16[512,256]{1,0:T(8,128)(2,1)S(1)}, bf16[512,256]{1,0:T(8,128)(2,1)S(1)}, u32[]{:S(2)}, u32[]{:S(2)}) collective-permute-start(bf16[512,256]{1,0:T(8,128)(2,1)S(1)} %convolution_convert_fusion.1), channel_id=1, source_target_pairs={{0,1},{1,2},{2,3},{3,4},{4,5},{5,6},{6,7},{7,8},{8,9},{9,10},{10,1... | collective-permute-start | bytes 786440 | tf_op jit(solution)/shard_map/ppermute | solution.py:14
  66.4 24.4 %all-to-all-start.1 = ((bf16[128,2,512]{2,1,0:T(2,128)(2,1)}), bf16[128,2,512]{2,1,0:T(2,128)(2,1)S(1)}, u32[]{:S(2)}, u32[]{:S(2)}) async-start(bf16[128,2,512]{2,1,0:T(2,128)(2,1)} %reshape.98), calls=%async_computation.1 | async-start | bytes 524288 | tf_op jit(solution)/shard_map/all_to_all | solution.py:114

commit v12 on v7

--- a/solution.py
+++ b/solution.py
@@ -71,7 +71,7 @@
     lows = parts[:, :DCAP] * 32 + parts[:, DCAP:]
     slot = jnp.sum((lids[:, None] >= lows[:, 1:]).astype(jnp.int32), axis=1)
     remote_slots = device_count * DCAP
-    slot_column = jnp.where(remote, owners * DCAP + slot, -1)
+    slot_column = jnp.where(remote, slot * device_count + owners, -1)
     slot_range = jnp.arange(remote_slots, dtype=jnp.int32)
     remote_hot = (slot_column[:, None] == slot_range[None, :]).astype(jnp.bfloat16)
     local_hot = jnp.where(remote[:, None], jnp.zeros((), jnp.bfloat16), lid_hot)
@@ -85,13 +85,15 @@
          jnp.zeros((device_count, 128 - 2 * DCAP), jnp.float32)],
         axis=1,
     )
-    payload = jnp.concatenate([remote_sums.reshape(device_count, DCAP * width), meta], axis=1)
+    payload = jnp.concatenate(
+        [remote_sums[k * device_count:(k + 1) * device_count] for k in range(DCAP)] + [meta], axis=1
+    )
     got = lax.all_to_all(
         payload.reshape(device_count, 1, -1), "nodes", split_axis=0, concat_axis=0, tiled=True
     ).reshape(device_count, -1)
-    got_sums = got[:, : DCAP * width].reshape(remote_slots, width)
-    got_counts = got[:, DCAP * width : DCAP * width + DCAP].reshape(remote_slots)
-    got_ids = got[:, DCAP * width + DCAP : DCAP * width + 2 * DCAP].reshape(remote_slots).astype(jnp.int32)
+    got_sums = jnp.concatenate([got[:, k * width:(k + 1) * width] for k in range(DCAP)], axis=0)
+    got_counts = got[:, DCAP * width : DCAP * width + DCAP].T.reshape(remote_slots)
+    got_ids = got[:, DCAP * width + DCAP : DCAP * width + 2 * DCAP].T.reshape(remote_slots).astype(jnp.int32)
     local_sums = lax.dot_general(
         local_hot, features, contract_rows, preferred_element_type=jnp.float32
     )
@@ -112,9 +114,13 @@
     answers = jnp.dot(
         got_hot.astype(jnp.bfloat16), coarse, preferred_element_type=jnp.float32
     ).astype(jnp.bfloat16)
+    back = jnp.concatenate(
+        [answers[k * device_count:(k + 1) * device_count] for k in range(DCAP)], axis=1
+    )
     returned = lax.all_to_all(
-        answers.reshape(device_count, DCAP, width), "nodes", split_axis=0, concat_axis=0, tiled=True
-    ).reshape(remote_slots, width)
+        back.reshape(device_count, 1, -1), "nodes", split_axis=0, concat_axis=0, tiled=True
+    ).reshape(device_count, -1)
+    returned = jnp.concatenate([returned[:, k * width:(k + 1) * width] for k in range(DCAP)], axis=0)
     value = (
         features.astype(jnp.float32)
         + jnp.dot(local_hot, coarse, preferred_element_type=jnp.float32)

time: 103 us -> 101 us (0.981)
  matrix products: 43.1 us -> 39.8 us
    dot_general x2, matrix products: 3.15 us -> 0.86 us  [convolve(): jnp.einsum('tkij,tkjf->tif', weights, picked, preferred_element_type=jnp....]
    dot_general x1, matrix products: 8 us -> 5.94 us  [local(): lax.dot_general(remote_hot, features, contract_rows, preferred_element_ty...]
    unnamed x11 -> x17, local copies, waits for them, and re-layouts: 0.07 us -> 1.41 us
where the time goes in v12:
time: 101 us; the launch traced here: 100 us
  matrix products  39.8 us (39%)
  starting transfers between devices  37 us (37%)
  waiting for transfers between devices  15 us (15%)
  local copies, waits for them, and re-layouts  4.91 us (5%)
  other arithmetic  3.18 us (3%)
    all_to_all x1, starting transfers between devices, local(): lax.all_to_all(back.reshape(device_count, 1, -1), 'nodes', split_axis=0,...  13.6 us
    all_to_all x1, starting transfers between devices, local(): lax.all_to_all(payload.reshape(device_count, 1, -1), 'nodes', split_axis=...  11.5 us
    dot_general x1, matrix products, local(): jnp.dot(local_hot, coarse, preferred_element_type=jnp.float32)  9.47 us
    dot_general x1, matrix products, local(): jnp.dot(remote_hot, returned, preferred_element_type=jnp.float32)  8.53 us
    all_to_all x1, waiting for transfers between devices, local(): lax.all_to_all(payload.reshape(device_count, 1, -1), 'nodes', split_axis=...  7.19 us
    ppermute x2, starting transfers between devices, with_halo(): lax.ppermute(lax.slice_in_dim(block, block.shape[dim] - width, None, axis...  6.94 us
    dot_general x1, matrix products, local(): lax.dot_general(local_hot, features, contract_rows, preferred_element_typ...  6.81 us
    dot_general x1, matrix products, local(): lax.dot_general(remote_hot, features, contract_rows, preferred_element_ty...  5.94 us
  transfers between devices with their start and end apart: 6, of which 6 were waited for; matrix products, arithmetic and copies ran while one was open for 16% of the time, Pallas kernels for 0%

profile of v12, /device:TPU:1, one launch (start us, length us, event | category | flops | bytes accessed | tf_op | source)
XLA Modules:
  0.0 100.3 jit_solution(1441374847406850199)
XLA Ops:
  0.0 0.8 add_select_fusion
  0.8 4.3 %broadcast_compare_fusion = (pred[128,512]{1,0:T(32,128)(4,1)S(1)}, f32[128,512]{1,0:T(8,128)S(1)}) fusion(s32[8192]{0:T(1024)S(1)} %get-tuple-element.34, s32[8192]{0:T(1024)S(1)} %get-tuple-element.33), kind=kOutput, calls=%fused_computation.82 | convolution fusion | flops 1079050240 | bytes 393216 | tf_op jit(solution)/shard_map/dot_general | solution.py:37
  6.6 1.3 %convolution_convert_fusion = s32[8192,8]{0,1:T(8,128)S(1)} fusion(s32[8192]{0:T(1024)S(1)} %get-tuple-element.33, bf16[128,4]{0,1:T(4,128)(2,1)S(1)} %get-tuple-element.36, bf16[128,4]{0,1:T(4,128)(2,1)S(1)} %get-tuple-element.37), kind=kOutput, calls=%fused_computation.11 | convolution fusion | flops 17895424 | bytes 296960 | tf_op jit(solution)/shard_map/dot_general | solution.py:70
  8.1 5.9 %fusion.1 = f32[512,256]{0,1:T(8,128)S(1)} fusion(bf16[8192,256]{1,0:T(8,128)(2,1)} %param.7, s32[8192]{0:T(1024)S(1)} %add_select_fusion.1), kind=kOutput, calls=%fused_computation.4 | convolution fusion | flops 2151677952 | bytes 4751360 | tf_op jit(solution)/shard_map/dot_general | solution.py:79
  14.2 1.2 %copy.14 = f32[128,1,1152]{2,1,0:T(1,128)} copy(f32[128,1,1152]{0,2,1:T(8,128)S(1)} %bitcast.61) | data formatting | bytes 1179648 | tf_op jit(solution)/shard_map/reshape | solution.py:92
  15.4 11.5 %all-to-all-start = ((f32[128,1,1152]{2,1,0:T(1,128)}), f32[128,1,1152]{2,1,0:T(1,128)S(1)}, u32[]{:S(2)}, u32[]{:S(2)}) async-start(f32[128,1,1152]{2,1,0:T(1,128)} %copy.14), calls=%async_computation | async-start | bytes 1179648 | tf_op jit(solution)/shard_map/all_to_all | solution.py:91
  27.0 6.8 %fusion.8 = f32[512,256]{1,0:T(8,128)S(1)} fusion(bf16[8192,256]{1,0:T(8,128)(2,1)} %param.7, s32[8192]{0:T(1024)S(1)} %get-tuple-element.34, pred[8192]{0:T(1024)(128)(4,1)S(1)} %broadcast_compare_fusion.1), kind=kOutput, calls=%fused_computation.13 | convolution fusion | flops 2160066560 | bytes 4759552 | tf_op jit(solution)/shard_map/dot_general | solution.py:97
  33.9 7.2 %all-to-all-done = f32[128,1,1152]{2,1,0:T(1,128)S(1)} async-done(((f32[128,1,1152]{2,1,0:T(1,128)}), f32[128,1,1152]{2,1,0:T(1,128)S(1)}, u32[]{:S(2)}, u32[]{:S(2)}) %all-to-all-start) | async-done | bytes 589856 | tf_op jit(solution)/shard_map/all_to_all | solution.py:91
  41.7 1.1 %fusion.23 = bf16[512,256]{1,0:T(8,128)(2,1)S(1)} fusion(f32[512,256]{1,0:T(8,128)S(1)} %fusion.8, f32[128,256]{1,0:T(8,128)S(1)} %get-tuple-element.16, f32[128,256]{1,0:T(8,128)S(1)} %get-tuple-element.17, f32[128,256]{1,0:T(8,128)S(1)} %get-tuple-element.18, f32[128,256]{1,0:T(8,128)S(1)} %get-tuple-element.15, s32[512]{0:T(512)S(1)} %bitcast.67, ...), kind=kOutput, calls=%fused_computation.31 | convolution fusion | flops 806354944 | bytes 1314816 | tf_op jit(solution)/shard_map/dot_general | solution.py:102
  43.1 3.0 %collective-permute-start.1 = (bf16[512,256]{1,0:T(8,128)(2,1)S(1)}, bf16[512,256]{1,0:T(8,128)(2,1)S(1)}, u32[]{:S(2)}, u32[]{:S(2)}) collective-permute-start(bf16[512,256]{1,0:T(8,128)(2,1)S(1)} %convolution_convert_fusion.3), channel_id=1, source_target_pairs={{1,0},{2,1},{3,2},{4,3},{5,4},{6,5},{7,6},{8,7},{9,8},{10,9},{11,1... | collective-permute-start | bytes 786440 | tf_op jit(solution)/shard_map/ppermute | solution.py:17
  46.1 2.6 %collective-permute-start = (bf16[512,256]{1,0:T(8,128)(2,1)S(1)}, bf16[512,256]{1,0:T(8,128)(2,1)S(1)}, u32[]{:S(2)}, u32[]{:S(2)}) collective-permute-start(bf16[512,256]{1,0:T(8,128)(2,1)S(1)} %convolution_convert_fusion.3), channel_id=1, source_target_pairs={{0,1},{1,2},{2,3},{3,4},{4,5},{5,6},{6,7},{7,8},{8,9},{9,10},{10,1... | collective-permute-start | bytes 786440 | tf_op jit(solution)/shard_map/ppermute | solution.py:14
  48.7 2.0 %collective-permute-done.1 = bf16[512,256]{1,0:T(8,128)(2,1)S(1)} collective-permute-done((bf16[512,256]{1,0:T(8,128)(2,1)S(1)}, bf16[512,256]{1,0:T(8,128)(2,1)S(1)}, u32[]{:S(2)}, u32[]{:S(2)}) %collective-permute-start.1) | collective-permute-done | bytes 262176 | tf_op jit(solution)/shard_map/ppermute | solution.py:17
  50.8 1.2 %collective-permute-done = bf16[512,256]{1,0:T(8,128)(2,1)S(1)} collective-permute-done((bf16[512,256]{1,0:T(8,128)(2,1)S(1)}, bf16[512,256]{1,0:T(8,128)(2,1)S(1)}, u32[]{:S(2)}, u32[]{:S(2)}) %collective-permute-start) | collective-permute-done | bytes 262176 | tf_op jit(solution)/shard_map/ppermute | solution.py:14
  52.0 0.6 gather_fusion
  53.3 1.9 %collective-permute-start.3 = (bf16[512,256]{1,0:T(8,128)(2,1)S(1)}, bf16[512,256]{1,0:T(8,128)(2,1)S(1)}, u32[]{:S(2)}, u32[]{:S(2)}) collective-permute-start(bf16[512,256]{1,0:T(8,128)(2,1)S(1)} %convolution_convert_fusion.2), channel_id=1, source_target_pairs={{1,0},{2,1},{3,2},{4,3},{5,4},{6,5},{7,6},{8,7},{9,8},{10,9},{11,1... | collective-permute-start | bytes 786440 | tf_op jit(solution)/shard_map/ppermute | solution.py:17
  55.3 4.4 %collective-permute-start.2 = (bf16[512,256]{1,0:T(8,128)(2,1)S(1)}, bf16[512,256]{1,0:T(8,128)(2,1)S(1)}, u32[]{:S(2)}, u32[]{:S(2)}) collective-permute-start(bf16[512,256]{1,0:T(8,128)(2,1)S(1)} %convolution_convert_fusion.2), channel_id=1, source_target_pairs={{0,1},{1,2},{2,3},{3,4},{4,5},{5,6},{6,7},{7,8},{8,9},{9,10},{10,1... | collective-permute-start | bytes 786440 | tf_op jit(solution)/shard_map/ppermute | solution.py:14
  59.7 2.1 %collective-permute-done.3 = bf16[512,256]{1,0:T(8,128)(2,1)S(1)} collective-permute-done((bf16[512,256]{1,0:T(8,128)(2,1)S(1)}, bf16[512,256]{1,0:T(8,128)(2,1)S(1)}, u32[]{:S(2)}, u32[]{:S(2)}) %collective-permute-start.3) | collective-permute-done | bytes 262176 | tf_op jit(solution)/shard_map/ppermute | solution.py:17
  61.8 1.2 %collective-permute-done.2 = bf16[512,256]{1,0:T(8,128)(2,1)S(1)} collective-permute-done((bf16[512,256]{1,0:T(8,128)(2,1)S(1)}, bf16[512,256]{1,0:T(8,128)(2,1)S(1)}, u32[]{:S(2)}, u32[]{:S(2)}) %collective-permute-start.2) | collective-permute-done | bytes 262176 | tf_op jit(solution)/shard_map/ppermute | solution.py:14
  65.2 0.8 reduce
  66.1 0.9 reshape.150
  67.0 13.6 %all-to-all-start.1 = ((bf16[128,2,512]{2,1,0:T(2,128)(2,1)}), bf16[128,2,512]{2,1,0:T(2,128)(2,1)S(1)}, u32[]{:S(2)}, u32[]{:S(2)}) async-start(bf16[128,2,512]{2,1,0:T(2,128)(2,1)} %reshape.150), calls=%async_computation.1 | async-start | bytes 524288 | tf_op jit(solution)/shard_map/all_to_all | solution.py:120
  80.6 9.5 %convolution_add_fusion = f32[8192,256]{1,0:T(8,128)} fusion(bf16[512,256]{1,0:T(8,128)(2,1)S(1)} %bitcast.76, s32[8192]{0:T(1024)S(1)} %get-tuple-element.34, bf16[8192,256]{1,0:T(8,128)(2,1)} %param.7, pred[8192]{0:T(1024)(128)(4,1)S(1)} %broadcast_compare_fusion.1), kind=kOutput, calls=%fused_computation.10 | convolution fusion | flops 2164260864 | bytes 12886016 | tf_op jit(solution)/shard_map/dot_general | solution.py:126
  90.1 1.3 %all-to-all-done.1 = bf16[128,2,512]{2,1,0:T(2,128)(2,1)S(1)} async-done(((bf16[128,2,512]{2,1,0:T(2,128)(2,1)}), bf16[128,2,512]{2,1,0:T(2,128)(2,1)S(1)}, u32[]{:S(2)}, u32[]{:S(2)}) %all-to-all-start.1) | async-done | bytes 262176 | tf_op jit(solution)/shard_map/all_to_all | solution.py:120
  91.8 8.5 %fusion.5 = bf16[8192,256]{1,0:T(8,128)(2,1)} fusion(f32[8192,256]{1,0:T(8,128)} %convolution_add_fusion, s32[8192]{0:T(1024)S(1)} %add_select_fusion.1, bf16[128,256]{1,0:T(8,128)(2,1)S(1)} %get-tuple-element.24, bf16[128,256]{1,0:T(8,128)(2,1)S(1)} %get-tuple-element.25, bf16[128,256]{1,0:T(8,128)(2,1)S(1)} %get-tuple-element.26, ...), kind=kOutput, calls=%fused_computation.9 | convolution fusion | flops 2156920832 | bytes 12877824 | tf_op jit(solution)/shard_map/dot_general | solution.py:127
  (59 shorter events, 6.0 us)
Async XLA Ops:
  0.0 42.8 %copy-start = (bf16[256,256]{1,0:T(8,128)(2,1)S(1)}, bf16[256,256]{1,0:T(8,128)(2,1)}, u32[]{:S(2)}) copy-start(bf16[256,256]{1,0:T(8,128)(2,1)} %param.12) | copy-start | bytes 393220
  5.2 2.9 %copy-start.1 = (s32[8192]{0:T(1024)S(1)}, s32[8192]{0:T(1024)}, u32[]{:S(2)}) copy-start(s32[8192]{0:T(1024)} %param.8) | copy-start | bytes 98308
  15.4 25.7 %all-to-all-start = ((f32[128,1,1152]{2,1,0:T(1,128)}), f32[128,1,1152]{2,1,0:T(1,128)S(1)}, u32[]{:S(2)}, u32[]{:S(2)}) async-start(f32[128,1,1152]{2,1,0:T(1,128)} %copy.14), calls=%async_computation | async-start | bytes 1179648 | tf_op jit(solution)/shard_map/all_to_all | solution.py:91
  27.0 6.9 %copy-start.3 = (s32[4,6]{1,0:T(4,128)S(1)}, s32[4,6]{1,0:T(4,128)}, u32[]{:S(2)}) copy-start(s32[4,6]{1,0:T(4,128)} %param.9) | copy-start | bytes 292
  33.8 14.9 %copy-start.5 = (s32[4]{0:T(128)S(1)}, s32[4]{0:T(128)}, u32[]{:S(2)}) copy-start(s32[4]{0:T(128)} %param.10) | copy-start | bytes 52
  41.7 11.0 %copy-start.4 = (bf16[4,6,128,128]{3,2,1,0:T(8,128)(2,1)S(1)}, bf16[4,6,128,128]{3,2,1,0:T(8,128)(2,1)}, u32[]{:S(2)}) copy-start(bf16[4,6,128,128]{3,2,1,0:T(8,128)(2,1)} %param.11) | copy-start | bytes 2359300
  42.8 10.3 %copy-start.2 = (bf16[256,256]{1,0:T(8,128)(2,1)S(1)}, bf16[256,256]{1,0:T(8,128)(2,1)}, u32[]{:S(2)}) copy-start(bf16[256,256]{1,0:T(8,128)(2,1)} %param.13) | copy-start | bytes 393220
  43.1 7.7 %collective-permute-start.1 = (bf16[512,256]{1,0:T(8,128)(2,1)S(1)}, bf16[512,256]{1,0:T(8,128)(2,1)S(1)}, u32[]{:S(2)}, u32[]{:S(2)}) collective-permute-start(bf16[512,256]{1,0:T(8,128)(2,1)S(1)} %convolution_convert_fusion.3), channel_id=1, source_target_pairs={{1,0},{2,1},{3,2},{4,3},{5,4},{6,5},{7,6},{8,7},{9,8},{10,9},{11,1... | collective-permute-start | bytes 786440 | tf_op jit(solution)/shard_map/ppermute | solution.py:17
  46.1 5.9 %collective-permute-start = (bf16[512,256]{1,0:T(8,128)(2,1)S(1)}, bf16[512,256]{1,0:T(8,128)(2,1)S(1)}, u32[]{:S(2)}, u32[]{:S(2)}) collective-permute-start(bf16[512,256]{1,0:T(8,128)(2,1)S(1)} %convolution_convert_fusion.3), channel_id=1, source_target_pairs={{0,1},{1,2},{2,3},{3,4},{4,5},{5,6},{6,7},{7,8},{8,9},{9,10},{10,1... | collective-permute-start | bytes 786440 | tf_op jit(solution)/shard_map/ppermute | solution.py:14
  53.3 8.4 %collective-permute-start.3 = (bf16[512,256]{1,0:T(8,128)(2,1)S(1)}, bf16[512,256]{1,0:T(8,128)(2,1)S(1)}, u32[]{:S(2)}, u32[]{:S(2)}) collective-permute-start(bf16[512,256]{1,0:T(8,128)(2,1)S(1)} %convolution_convert_fusion.2), channel_id=1, source_target_pairs={{1,0},{2,1},{3,2},{4,3},{5,4},{6,5},{7,6},{8,7},{9,8},{10,9},{11,1... | collective-permute-start | bytes 786440 | tf_op jit(solution)/shard_map/ppermute | solution.py:17
  55.3 7.7 %collective-permute-start.2 = (bf16[512,256]{1,0:T(8,128)(2,1)S(1)}, bf16[512,256]{1,0:T(8,128)(2,1)S(1)}, u32[]{:S(2)}, u32[]{:S(2)}) collective-permute-start(bf16[512,256]{1,0:T(8,128)(2,1)S(1)} %convolution_convert_fusion.2), channel_id=1, source_target_pairs={{0,1},{1,2},{2,3},{3,4},{4,5},{5,6},{6,7},{7,8},{8,9},{9,10},{10,1... | collective-permute-start | bytes 786440 | tf_op jit(solution)/shard_map/ppermute | solution.py:14
  67.0 24.4 %all-to-all-start.1 = ((bf16[128,2,512]{2,1,0:T(2,128)(2,1)}), bf16[128,2,512]{2,1,0:T(2,128)(2,1)S(1)}, u32[]{:S(2)}, u32[]{:S(2)}) async-start(bf16[128,2,512]{2,1,0:T(2,128)(2,1)} %reshape.150), calls=%async_computation.1 | async-start | bytes 524288 | tf_op jit(solution)/shard_map/all_to_all | solution.py:120

commit v13 on v11

--- a/solution.py
+++ b/solution.py
@@ -92,12 +92,15 @@
         local_hot, features, contract_rows, preferred_element_type=jnp.float32
     )
     local_counts = lax.dynamic_index_in_dim(presence, myself, axis=0, keepdims=False)
-    got_hot = (got_ids[:, None] == here[None, :]).astype(jnp.float32)
-    sums_all = local_sums + lax.dot_general(
-        got_hot, got_sums, contract_rows,
-        precision=lax.Precision.HIGHEST, preferred_element_type=jnp.float32,
+    got_hot = (got_ids[:, None] == here[None, :]).astype(jnp.bfloat16)
+    got_high = got_sums.astype(jnp.bfloat16)
+    got_low = (got_sums - got_high.astype(jnp.float32)).astype(jnp.bfloat16)
+    sums_all = (
+        local_sums
+        + lax.dot_general(got_hot, got_high, contract_rows, preferred_element_type=jnp.float32)
+        + lax.dot_general(got_hot, got_low, contract_rows, preferred_element_type=jnp.float32)
     )
-    counts_all = local_counts + jnp.sum(got_hot * got_counts[:, None], axis=0)
+    counts_all = local_counts + jnp.sum(got_hot.astype(jnp.float32) * got_counts[:, None], axis=0)
     pooled = (sums_all / jnp.sqrt(counts_all + 1.0)[:, None]).astype(jnp.bfloat16)
     first_proj = jnp.dot(pooled, w_first, preferred_element_type=jnp.float32).astype(jnp.bfloat16)
     hidden = jnp.maximum(
@@ -106,7 +109,7 @@
     second_proj = jnp.dot(hidden, w_second, preferred_element_type=jnp.float32).astype(jnp.bfloat16)
     coarse = convolve(second_proj, tile_cols, tile_counts, adjacency, myself).astype(jnp.bfloat16)
     answers = jnp.dot(
-        got_hot.astype(jnp.bfloat16), coarse, preferred_element_type=jnp.float32
+        got_hot, coarse, preferred_element_type=jnp.float32
     ).astype(jnp.bfloat16)
     back = jnp.concatenate(
         [answers[k * device_count:(k + 1) * device_count] for k in range(DCAP)], axis=1

time: 100 us -> 100 us (level)
  no operation moved by 1% of the time
where the time goes in v13:
time: 100 us; the launch traced here: 99.8 us
  matrix products  40 us (40%)
  starting transfers between devices  37.1 us (37%)
  waiting for transfers between devices  15 us (15%)
  local copies, waits for them, and re-layouts  4.87 us (5%)
  other arithmetic  2.47 us (2%)
    all_to_all x1, starting transfers between devices, local(): lax.all_to_all(back.reshape(device_count, 1, -1), 'nodes', split_axis=0,...  13.6 us
    all_to_all x1, starting transfers between devices, local(): lax.all_to_all(payload.reshape(device_count, 1, -1), 'nodes', split_axis=...  11.5 us
    dot_general x1, matrix products, local(): jnp.dot(local_hot, coarse, preferred_element_type=jnp.float32)  9.47 us
    dot_general x1, matrix products, local(): jnp.dot(remote_hot, returned, preferred_element_type=jnp.float32)  8.53 us
    all_to_all x1, waiting for transfers between devices, local(): lax.all_to_all(payload.reshape(device_count, 1, -1), 'nodes', split_axis=...  7.19 us
    ppermute x2, starting transfers between devices, with_halo(): lax.ppermute(lax.slice_in_dim(block, block.shape[dim] - width, None, axis...  6.94 us
    dot_general x1, matrix products, local(): lax.dot_general(local_hot, features, contract_rows, preferred_element_typ...  6.82 us
    ppermute x2, starting transfers between devices, with_halo(): lax.ppermute(lax.slice_in_dim(block, 0, width, axis=dim), axis, backward)  5.06 us
  transfers between devices with their start and end apart: 6, of which 6 were waited for; matrix products, arithmetic and copies ran while one was open for 17% of the time, Pallas kernels for 0%

profile of v13, /device:TPU:1, one launch (start us, length us, event | category | flops | bytes accessed | tf_op | source)
XLA Modules:
  0.0 99.8 jit_solution(2552069334706391302)
XLA Ops:
  0.0 0.8 add_select_fusion
  0.8 3.2 %broadcast_compare_fusion = (pred[128,512]{1,0:T(32,128)(4,1)S(1)}, f32[128,512]{1,0:T(8,128)S(1)}) fusion(s32[8192]{0:T(1024)S(1)} %get-tuple-element.42, s32[8192]{0:T(1024)S(1)} %get-tuple-element.41), kind=kOutput, calls=%fused_computation.81 | convolution fusion | flops 1079050240 | bytes 393216 | tf_op jit(solution)/shard_map/dot_general | solution.py:37
  4.6 4.8 %fusion.24 = f32[8192]{0:T(1024)S(1)} fusion(s32[8192]{0:T(1024)S(1)} %get-tuple-element.41, s32[8192]{0:T(1024)S(1)} %get-tuple-element.42, bf16[128,512]{1,0:T(8,128)(2,1)S(1)} %get-tuple-element.45), kind=kOutput, calls=%fused_computation.28 | convolution fusion | flops 1083170816 | bytes 229376 | tf_op jit(solution)/shard_map/dot_general | solution.py:42
  9.5 3.7 %fusion.1 = f32[512,256]{0,1:T(8,128)S(1)} fusion(bf16[8192,256]{1,0:T(8,128)(2,1)S(1)} %copy-done.4, s32[8192]{0:T(1024)S(1)} %add_select_fusion.1), kind=kOutput, calls=%fused_computation.4 | convolution fusion | flops 2151677952 | bytes 4751360 | tf_op jit(solution)/shard_map/dot_general | solution.py:66
  13.6 1.2 %copy.14 = f32[128,1,1152]{2,1,0:T(1,128)} copy(f32[128,1,1152]{0,2,1:T(8,128)S(1)} %bitcast.57) | data formatting | bytes 1179648 | tf_op jit(solution)/shard_map/reshape | solution.py:86
  14.8 11.5 %all-to-all-start = ((f32[128,1,1152]{2,1,0:T(1,128)}), f32[128,1,1152]{2,1,0:T(1,128)S(1)}, u32[]{:S(2)}, u32[]{:S(2)}) async-start(f32[128,1,1152]{2,1,0:T(1,128)} %copy.14), calls=%async_computation | async-start | bytes 1179648 | tf_op jit(solution)/shard_map/all_to_all | solution.py:85
  26.4 6.8 %fusion.10 = f32[512,256]{1,0:T(8,128)S(1)} fusion(bf16[8192,256]{1,0:T(8,128)(2,1)} %param.7, s32[8192]{0:T(1024)S(1)} %get-tuple-element.42, pred[8192]{0:T(1024)(128)(4,1)S(1)} %broadcast_compare_fusion.1), kind=kOutput, calls=%fused_computation.14 | convolution fusion | flops 2160066560 | bytes 4759552 | tf_op jit(solution)/shard_map/dot_general | solution.py:91
  33.4 7.2 %all-to-all-done = f32[128,1,1152]{2,1,0:T(1,128)S(1)} async-done(((f32[128,1,1152]{2,1,0:T(1,128)}), f32[128,1,1152]{2,1,0:T(1,128)S(1)}, u32[]{:S(2)}, u32[]{:S(2)}) %all-to-all-start) | async-done | bytes 589856 | tf_op jit(solution)/shard_map/all_to_all | solution.py:85
  41.7 0.7 convolution_convert_fusion.2
  42.4 3.1 %collective-permute-start.1 = (bf16[512,256]{1,0:T(8,128)(2,1)S(1)}, bf16[512,256]{1,0:T(8,128)(2,1)S(1)}, u32[]{:S(2)}, u32[]{:S(2)}) collective-permute-start(bf16[512,256]{1,0:T(8,128)(2,1)S(1)} %convolution_convert_fusion.2), channel_id=1, source_target_pairs={{1,0},{2,1},{3,2},{4,3},{5,4},{6,5},{7,6},{8,7},{9,8},{10,9},{11,1... | collective-permute-start | bytes 786440 | tf_op jit(solution)/shard_map/ppermute | solution.py:17
  45.6 2.6 %collective-permute-start = (bf16[512,256]{1,0:T(8,128)(2,1)S(1)}, bf16[512,256]{1,0:T(8,128)(2,1)S(1)}, u32[]{:S(2)}, u32[]{:S(2)}) collective-permute-start(bf16[512,256]{1,0:T(8,128)(2,1)S(1)} %convolution_convert_fusion.2), channel_id=1, source_target_pairs={{0,1},{1,2},{2,3},{3,4},{4,5},{5,6},{6,7},{7,8},{8,9},{9,10},{10,1... | collective-permute-start | bytes 786440 | tf_op jit(solution)/shard_map/ppermute | solution.py:14
  48.2 2.0 %collective-permute-done.1 = bf16[512,256]{1,0:T(8,128)(2,1)S(1)} collective-permute-done((bf16[512,256]{1,0:T(8,128)(2,1)S(1)}, bf16[512,256]{1,0:T(8,128)(2,1)S(1)}, u32[]{:S(2)}, u32[]{:S(2)}) %collective-permute-start.1) | collective-permute-done | bytes 262176 | tf_op jit(solution)/shard_map/ppermute | solution.py:17
  50.3 1.2 %collective-permute-done = bf16[512,256]{1,0:T(8,128)(2,1)S(1)} collective-permute-done((bf16[512,256]{1,0:T(8,128)(2,1)S(1)}, bf16[512,256]{1,0:T(8,128)(2,1)S(1)}, u32[]{:S(2)}, u32[]{:S(2)}) %collective-permute-start) | collective-permute-done | bytes 262176 | tf_op jit(solution)/shard_map/ppermute | solution.py:14
  51.5 0.6 gather_fusion
  52.8 1.9 %collective-permute-start.3 = (bf16[512,256]{1,0:T(8,128)(2,1)S(1)}, bf16[512,256]{1,0:T(8,128)(2,1)S(1)}, u32[]{:S(2)}, u32[]{:S(2)}) collective-permute-start(bf16[512,256]{1,0:T(8,128)(2,1)S(1)} %convolution_convert_fusion.1), channel_id=1, source_target_pairs={{1,0},{2,1},{3,2},{4,3},{5,4},{6,5},{7,6},{8,7},{9,8},{10,9},{11,1... | collective-permute-start | bytes 786440 | tf_op jit(solution)/shard_map/ppermute | solution.py:17
  54.8 4.4 %collective-permute-start.2 = (bf16[512,256]{1,0:T(8,128)(2,1)S(1)}, bf16[512,256]{1,0:T(8,128)(2,1)S(1)}, u32[]{:S(2)}, u32[]{:S(2)}) collective-permute-start(bf16[512,256]{1,0:T(8,128)(2,1)S(1)} %convolution_convert_fusion.1), channel_id=1, source_target_pairs={{0,1},{1,2},{2,3},{3,4},{4,5},{5,6},{6,7},{7,8},{8,9},{9,10},{10,1... | collective-permute-start | bytes 786440 | tf_op jit(solution)/shard_map/ppermute | solution.py:14
  59.2 2.1 %collective-permute-done.3 = bf16[512,256]{1,0:T(8,128)(2,1)S(1)} collective-permute-done((bf16[512,256]{1,0:T(8,128)(2,1)S(1)}, bf16[512,256]{1,0:T(8,128)(2,1)S(1)}, u32[]{:S(2)}, u32[]{:S(2)}) %collective-permute-start.3) | collective-permute-done | bytes 262176 | tf_op jit(solution)/shard_map/ppermute | solution.py:17
  61.3 1.2 %collective-permute-done.2 = bf16[512,256]{1,0:T(8,128)(2,1)S(1)} collective-permute-done((bf16[512,256]{1,0:T(8,128)(2,1)S(1)}, bf16[512,256]{1,0:T(8,128)(2,1)S(1)}, u32[]{:S(2)}, u32[]{:S(2)}) %collective-permute-start.2) | collective-permute-done | bytes 262176 | tf_op jit(solution)/shard_map/ppermute | solution.py:14
  64.7 0.8 reduce
  65.7 0.9 reshape.98
  66.6 13.6 %all-to-all-start.1 = ((bf16[128,2,512]{2,1,0:T(2,128)(2,1)}), bf16[128,2,512]{2,1,0:T(2,128)(2,1)S(1)}, u32[]{:S(2)}, u32[]{:S(2)}) async-start(bf16[128,2,512]{2,1,0:T(2,128)(2,1)} %reshape.98), calls=%async_computation.1 | async-start | bytes 524288 | tf_op jit(solution)/shard_map/all_to_all | solution.py:117
  80.2 9.5 %convolution_add_fusion = f32[8192,256]{1,0:T(8,128)} fusion(bf16[512,256]{1,0:T(8,128)(2,1)S(1)} %bitcast.77, s32[8192]{0:T(1024)S(1)} %get-tuple-element.42, bf16[8192,256]{1,0:T(8,128)(2,1)} %param.7, pred[8192]{0:T(1024)(128)(4,1)S(1)} %broadcast_compare_fusion.1), kind=kOutput, calls=%fused_computation.12 | convolution fusion | flops 2164260864 | bytes 12886016 | tf_op jit(solution)/shard_map/dot_general | solution.py:123
  89.6 1.3 %all-to-all-done.1 = bf16[128,2,512]{2,1,0:T(2,128)(2,1)S(1)} async-done(((bf16[128,2,512]{2,1,0:T(2,128)(2,1)}), bf16[128,2,512]{2,1,0:T(2,128)(2,1)S(1)}, u32[]{:S(2)}, u32[]{:S(2)}) %all-to-all-start.1) | async-done | bytes 262176 | tf_op jit(solution)/shard_map/all_to_all | solution.py:117
  91.3 8.5 %fusion.7 = bf16[8192,256]{1,0:T(8,128)(2,1)} fusion(f32[8192,256]{1,0:T(8,128)} %convolution_add_fusion, s32[8192]{0:T(1024)S(1)} %add_select_fusion.1, bf16[128,256]{1,0:T(8,128)(2,1)S(1)} %get-tuple-element.34, bf16[128,256]{1,0:T(8,128)(2,1)S(1)} %get-tuple-element.35, bf16[128,256]{1,0:T(8,128)(2,1)S(1)} %get-tuple-element.36, ...), kind=kOutput, calls=%fused_computation.11 | convolution fusion | flops 2156920832 | bytes 12877824 | tf_op jit(solution)/shard_map/dot_general | solution.py:124
  (50 shorter events, 5.7 us)
Async XLA Ops:
  0.0 41.7 %copy-start = (bf16[256,256]{1,0:T(8,128)(2,1)S(1)}, bf16[256,256]{1,0:T(8,128)(2,1)}, u32[]{:S(2)}) copy-start(bf16[256,256]{1,0:T(8,128)(2,1)} %param.12) | copy-start | bytes 393220
  4.6 4.9 %copy-start.1 = (s32[8192]{0:T(1024)S(1)}, s32[8192]{0:T(1024)}, u32[]{:S(2)}) copy-start(s32[8192]{0:T(1024)} %param.8) | copy-start | bytes 98308
  4.6 4.9 %copy-start.4 = (bf16[8192,256]{1,0:T(8,128)(2,1)S(1)}, bf16[8192,256]{1,0:T(8,128)(2,1)}, u32[]{:S(2)}) copy-start(bf16[8192,256]{1,0:T(8,128)(2,1)} %param.7) | copy-start | bytes 12582916
  14.8 25.7 %all-to-all-start = ((f32[128,1,1152]{2,1,0:T(1,128)}), f32[128,1,1152]{2,1,0:T(1,128)S(1)}, u32[]{:S(2)}, u32[]{:S(2)}) async-start(f32[128,1,1152]{2,1,0:T(1,128)} %copy.14), calls=%async_computation | async-start | bytes 1179648 | tf_op jit(solution)/shard_map/all_to_all | solution.py:85
  26.4 6.9 %copy-start.3 = (s32[4,6]{1,0:T(4,128)S(1)}, s32[4,6]{1,0:T(4,128)}, u32[]{:S(2)}) copy-start(s32[4,6]{1,0:T(4,128)} %param.9) | copy-start | bytes 292
  33.2 14.9 %copy-start.6 = (s32[4]{0:T(128)S(1)}, s32[4]{0:T(128)}, u32[]{:S(2)}) copy-start(s32[4]{0:T(128)} %param.10) | copy-start | bytes 52
  41.7 10.5 %copy-start.5 = (bf16[4,6,128,128]{3,2,1,0:T(8,128)(2,1)S(1)}, bf16[4,6,128,128]{3,2,1,0:T(8,128)(2,1)}, u32[]{:S(2)}) copy-start(bf16[4,6,128,128]{3,2,1,0:T(8,128)(2,1)} %param.11) | copy-start | bytes 2359300
  42.4 10.2 %copy-start.2 = (bf16[256,256]{1,0:T(8,128)(2,1)S(1)}, bf16[256,256]{1,0:T(8,128)(2,1)}, u32[]{:S(2)}) copy-start(bf16[256,256]{1,0:T(8,128)(2,1)} %param.13) | copy-start | bytes 393220
  42.4 7.8 %collective-permute-start.1 = (bf16[512,256]{1,0:T(8,128)(2,1)S(1)}, bf16[512,256]{1,0:T(8,128)(2,1)S(1)}, u32[]{:S(2)}, u32[]{:S(2)}) collective-permute-start(bf16[512,256]{1,0:T(8,128)(2,1)S(1)} %convolution_convert_fusion.2), channel_id=1, source_target_pairs={{1,0},{2,1},{3,2},{4,3},{5,4},{6,5},{7,6},{8,7},{9,8},{10,9},{11,1... | collective-permute-start | bytes 786440 | tf_op jit(solution)/shard_map/ppermute | solution.py:17
  45.6 5.9 %collective-permute-start = (bf16[512,256]{1,0:T(8,128)(2,1)S(1)}, bf16[512,256]{1,0:T(8,128)(2,1)S(1)}, u32[]{:S(2)}, u32[]{:S(2)}) collective-permute-start(bf16[512,256]{1,0:T(8,128)(2,1)S(1)} %convolution_convert_fusion.2), channel_id=1, source_target_pairs={{0,1},{1,2},{2,3},{3,4},{4,5},{5,6},{6,7},{7,8},{8,9},{9,10},{10,1... | collective-permute-start | bytes 786440 | tf_op jit(solution)/shard_map/ppermute | solution.py:14
  52.8 8.4 %collective-permute-start.3 = (bf16[512,256]{1,0:T(8,128)(2,1)S(1)}, bf16[512,256]{1,0:T(8,128)(2,1)S(1)}, u32[]{:S(2)}, u32[]{:S(2)}) collective-permute-start(bf16[512,256]{1,0:T(8,128)(2,1)S(1)} %convolution_convert_fusion.1), channel_id=1, source_target_pairs={{1,0},{2,1},{3,2},{4,3},{5,4},{6,5},{7,6},{8,7},{9,8},{10,9},{11,1... | collective-permute-start | bytes 786440 | tf_op jit(solution)/shard_map/ppermute | solution.py:17
  54.8 7.7 %collective-permute-start.2 = (bf16[512,256]{1,0:T(8,128)(2,1)S(1)}, bf16[512,256]{1,0:T(8,128)(2,1)S(1)}, u32[]{:S(2)}, u32[]{:S(2)}) collective-permute-start(bf16[512,256]{1,0:T(8,128)(2,1)S(1)} %convolution_convert_fusion.1), channel_id=1, source_target_pairs={{0,1},{1,2},{2,3},{3,4},{4,5},{5,6},{6,7},{7,8},{8,9},{9,10},{10,1... | collective-permute-start | bytes 786440 | tf_op jit(solution)/shard_map/ppermute | solution.py:14
  66.6 24.4 %all-to-all-start.1 = ((bf16[128,2,512]{2,1,0:T(2,128)(2,1)}), bf16[128,2,512]{2,1,0:T(2,128)(2,1)S(1)}, u32[]{:S(2)}, u32[]{:S(2)}) async-start(bf16[128,2,512]{2,1,0:T(2,128)(2,1)} %reshape.98), calls=%async_computation.1 | async-start | bytes 524288 | tf_op jit(solution)/shard_map/all_to_all | solution.py:117
